TPU v7x, 32 devices: a whole 2x2x4 slice. The times are simulated.
32 devices in a mesh: energy: 8 (over y, x, core), space: 4 (over z).
Axes of the slice: x: 2, y: 2, z: 4, core: 2. Of those that a mesh axis runs over, the one named last changes fastest.
Arguments:
- g_lesser: bfloat16 [4, 2, 32, 16384], P('space', None, 'energy'), may hold values from -6 to 6
- g_greater: bfloat16 [4, 2, 32, 16384], P('space', None, 'energy'), may hold values from -6 to 6
- v_diag: float32 [4, 128, 128], P('space'), may hold values from -0.5 to 0.5
- v_couple: float32 [4, 128, 128], P('space'), may hold values from -0.5 to 0.5
Outputs:
- screened: float32 [4, 2, 32, 16384], P('space', None, 'energy')
All inputs are finite; a program needn't handle non-finite values.
Results may differ from a plain program's by a relative error of at most 0.0003.
Values may be sent and summed in bfloat16 or wider, within the bound.
No kernel may reach another device: no remote copies, remote signals or barrier semaphores. Data moves between devices by JAX's collectives and lax.ppermute only.
A program may use at most 64 MiB of HBM per device.

v0:
```python
import math

import jax
import jax.numpy as jnp
from jax import lax
from jax.sharding import PartitionSpec as P

BS = 128
QUANT = 128


def shifted(x, axis, by):
    devices = lax.axis_size(axis)
    pairs = [(i, i + by) for i in range(devices) if 0 <= i + by < devices]
    return lax.ppermute(x, axis, pairs)


def product(left, right):
    return jnp.dot(left, right, precision=lax.Precision.HIGHEST, preferred_element_type=jnp.float32)


def complex_apply(real_table, sum_table, diff_table, re_part, im_part):
    first = product(real_table, re_part + im_part)
    second = product(sum_table, im_part)
    third = product(diff_table, re_part)
    return (first - second, first + third)


def correlate(lesser, greater):
    count = lesser.shape[2]
    width = lesser.shape[3]
    length = 2 * count
    rows = lax.iota(jnp.int32, length)[:, None]
    cols = lax.iota(jnp.int32, count)[None, :]
    phase = (rows * cols % length).astype(jnp.float32) * (2.0 * math.pi / length)
    cosine = jnp.cos(phase)
    sine = jnp.sin(phase)
    fwd_sum = cosine - sine
    fwd_diff = -sine - cosine
    both_re = jnp.concatenate([lesser[0, 0], greater[0, 0]], axis=1).astype(jnp.float32)
    both_im = jnp.concatenate([lesser[0, 1], greater[0, 1]], axis=1).astype(jnp.float32)
    s_re, s_im = complex_apply(cosine, fwd_sum, fwd_diff, both_re, both_im)
    l_re = s_re[:, :width]
    l_im = s_im[:, :width]
    g_re = s_re[:, width:]
    g_im = s_im[:, width:]
    z_re = l_re * g_re + l_im * g_im
    z_im = l_im * g_re - l_re * g_im
    inv_cos = cosine.T / length
    inv_sin = sine.T / length
    c_re, c_im = complex_apply(inv_cos, inv_cos + inv_sin, inv_sin - inv_cos, z_re, z_im)
    scale = count ** (-0.5)
    return jnp.stack([-scale * c_im, scale * c_re])[None]


def sandwich(left, field, right):
    inner = jnp.matmul(left, field, precision=lax.Precision.HIGHEST)
    return jnp.matmul(inner, right, precision=lax.Precision.HIGHEST)


def per_device(g_lesser, g_greater, v_diag, v_couple):
    groups = lax.axis_size("energy")
    e_local = g_lesser.shape[2]
    elements = g_lesser.shape[3]
    tile_width = (elements + groups * QUANT - 1) // (groups * QUANT) * QUANT
    padding = tile_width * groups - elements
    widths = ((0, 0), (0, 0), (0, 0), (0, padding))
    lesser_pad = jnp.pad(g_lesser, widths)
    greater_pad = jnp.pad(g_greater, widths)
    lesser_tile, greater_tile = (
        lax.all_to_all(lesser_pad, "energy", split_axis=3, concat_axis=2, tiled=True),
        lax.all_to_all(greater_pad, "energy", split_axis=3, concat_axis=2, tiled=True),
    )
    polar_tile = correlate(lesser_tile, greater_tile)
    polar_back = lax.all_to_all(polar_tile, "energy", split_axis=2, concat_axis=3, tiled=True)
    polar = polar_back[:, :, :, :elements].reshape(2, e_local, BS, BS)
    diag_block = v_diag[0]
    couple_own = v_couple[0]
    couple_prev = shifted(couple_own, "space", 1)
    to_next = sandwich(couple_own.T, polar, couple_own)
    to_prev = sandwich(couple_prev, polar, couple_prev.T)
    from_below = shifted(to_next, "space", 1)
    from_above = shifted(to_prev, "space", -1)
    local = sandwich(diag_block, polar, diag_block)
    total = local + from_below + from_above
    return total.reshape(1, 2, e_local, elements)


def solution(mesh):
    placed = (
        P("space", None, "energy", None),
        P("space", None, "energy", None),
        P("space", None, None),
        P("space", None, None),
    )
    return jax.shard_map(
        per_device,
        mesh=mesh,
        in_specs=placed,
        out_specs=P("space", None, "energy", None),
        check_vma=False,
    )
```

profile of v0, /device:TPU:0, one launch (start us, length us, event | category | flops | bytes accessed | tf_op | source)
XLA Modules:
  0.0 189.8 jit_solution(7003850882801027311)
XLA Ops:
  0.0 0.0 copy-start
  0.0 0.0 copy-start.1
  0.0 15.6 %copy.33 = bf16[1,2,4,16384]{2,1,0,3:T(2,128)(2,1)} copy(bf16[1,2,4,16384]{3,2,1,0:T(4,128)(2,1)} %param.4) | data formatting | bytes 524288 | tf_op args[0]
  15.6 16.8 %reshape.14 = bf16[8,2,8192]{2,1,0:T(2,128)(2,1)} reshape(bf16[16384,1,2,4]{3,2,1,0:T(2,128)(2,1)} %bitcast.75) | data formatting | bytes 524288
  32.4 5.2 %all-to-all-start = ((bf16[8,2,8192]{2,1,0:T(2,128)(2,1)}), bf16[8,2,8192]{2,1,0:T(2,128)(2,1)S(1)}, u32[]{:S(2)}, u32[]{:S(2)}) async-start(bf16[8,2,8192]{2,1,0:T(2,128)(2,1)} %reshape.14), calls=%async_computation | async-start | bytes 524288 | tf_op jit(solution)/shard_map/all_to_all | solution.py:71
  37.6 0.0 copy-done.1
  37.6 13.1 %copy.35 = bf16[1,2,4,16384]{2,1,0,3:T(2,128)(2,1)} copy(bf16[1,2,4,16384]{3,2,1,0:T(4,128)(2,1)S(1)} %copy-done.1) | data formatting | bytes 524288 | tf_op args[1]
  50.7 16.8 %reshape.12 = bf16[8,2,8192]{2,1,0:T(2,128)(2,1)} reshape(bf16[16384,1,2,4]{3,2,1,0:T(2,128)(2,1)} %bitcast.76) | data formatting | bytes 524288
  67.6 0.0 all-to-all-done
  67.6 4.2 %all-to-all-start.1 = ((bf16[8,2,8192]{2,1,0:T(2,128)(2,1)}), bf16[8,2,8192]{2,1,0:T(2,128)(2,1)S(1)}, u32[]{:S(2)}, u32[]{:S(2)}) async-start(bf16[8,2,8192]{2,1,0:T(2,128)(2,1)} %reshape.12), calls=%async_computation.1 | async-start | bytes 524288 | tf_op jit(solution)/shard_map/all_to_all | solution.py:72
  71.7 19.1 %reshape.15 = bf16[16384,1,2,4]{3,2,1,0:T(2,128)(2,1)} reshape(bf16[8,2,8192]{2,1,0:T(2,128)(2,1)S(1)} %all-to-all-done) | data formatting | bytes 524288
  90.8 19.2 %copy.34 = bf16[1,2,4,8,2048]{4,1,2,3,0:T(2,128)(2,1)S(1)} copy(bf16[1,2,4,8,2048]{2,1,4,3,0:T(2,128)(2,1)} %bitcast.73) | data formatting | bytes 524288 | tf_op jit(solution)/shard_map/all_to_all | solution.py:71
  110.0 0.4 fusion.79
  110.4 0.0 all-to-all-done.1
  110.4 19.1 %reshape.13 = bf16[16384,1,2,4]{3,2,1,0:T(2,128)(2,1)} reshape(bf16[8,2,8192]{2,1,0:T(2,128)(2,1)S(1)} %all-to-all-done.1) | data formatting | bytes 524288
  129.6 19.2 %copy.36 = bf16[1,2,4,8,2048]{4,1,2,3,0:T(2,128)(2,1)S(1)} copy(bf16[1,2,4,8,2048]{2,1,4,3,0:T(2,128)(2,1)} %bitcast.74) | data formatting | bytes 524288 | tf_op jit(solution)/shard_map/all_to_all | solution.py:72
  148.8 0.4 fusion.80
  149.2 0.2 copy_bitcast_fusion.3
  149.3 0.0 copy-start.2
  149.3 0.2 copy_bitcast_fusion.1
  149.5 1.1 fusion.7
  150.6 0.7 convolution_subtract_fusion
  151.3 0.7 convolution_add_fusion
  152.0 0.1 multiply_subtract_fusion
  152.2 0.5 fusion.5
  152.7 0.5 fusion.3
  153.1 0.5 fusion.1
  153.7 1.2 copy.39
  154.9 4.2 %all-to-all-start.2 = ((f32[1,2,32,2048]{3,1,0,2:T(2,128)}), f32[1,2,32,2048]{3,1,0,2:T(2,128)S(1)}, u32[]{:S(2)}, u32[]{:S(2)}) async-start(f32[1,2,32,2048]{3,1,0,2:T(2,128)} %copy.39), calls=%async_computation.2 | async-start | bytes 1048576 | tf_op jit(solution)/shard_map/all_to_all | solution.py:75
  159.0 0.0 copy-done.2
  159.0 3.5 %collective-permute-start.1 = (f32[128,128]{1,0:T(8,128)S(1)}, f32[128,128]{1,0:T(8,128)S(1)}, u32[]{:S(2)}, u32[]{:S(2)}) collective-permute-start(f32[128,128]{1,0:T(8,128)S(1)} %bitcast.81), channel_id=1, source_target_pairs={{0,1},{1,2},{2,3},{4,5},{5,6},{6,7},{8,9},{9,10},{10,11},{12,13},{... | collective-permute-start | bytes 196616 | tf_op jit(solution)/shard_map/ppermute | solution.py:15
  162.5 6.2 %all-to-all-done.2 = f32[1,2,32,2048]{3,1,0,2:T(2,128)S(1)} async-done(((f32[1,2,32,2048]{3,1,0,2:T(2,128)}), f32[1,2,32,2048]{3,1,0,2:T(2,128)S(1)}, u32[]{:S(2)}, u32[]{:S(2)}) %all-to-all-start.2) | async-done | bytes 524320 | tf_op jit(solution)/shard_map/all_to_all | solution.py:75
  168.8 0.3 copy.65
  169.1 0.1 reshape.7
  169.2 1.0 convolution_bitcast_fusion.1
  170.2 0.0 collective-permute-done.1
  170.2 1.0 convolution_bitcast_fusion
  171.2 1.0 fusion.11
  172.2 1.5 collective-permute-start.2
  173.7 1.0 fusion.14
  174.7 4.6 %collective-permute-start = (f32[2,4,128,128]{3,2,1,0:T(8,128)S(1)}, f32[2,4,128,128]{3,2,1,0:T(8,128)S(1)}, u32[]{:S(2)}, u32[]{:S(2)}) collective-permute-start(f32[2,4,128,128]{3,2,1,0:T(8,128)S(1)} %fusion.14), channel_id=1, source_target_pairs={{0,1},{1,2},{2,3},{4,5},{5,6},{6,7},{8,9},{9,10},{10,11},{12,13},{... | collective-permute-start | bytes 1572872 | tf_op jit(solution)/shard_map/ppermute | solution.py:15
  179.3 0.0 copy-done
  179.3 1.0 convolution_bitcast_fusion.2
  180.3 5.1 %collective-permute-done.2 = f32[2,4,128,128]{3,2,1,0:T(8,128)S(1)} collective-permute-done((f32[2,4,128,128]{3,2,1,0:T(8,128)S(1)}, f32[2,4,128,128]{3,2,1,0:T(8,128)S(1)}, u32[]{:S(2)}, u32[]{:S(2)}) %collective-permute-start.2) | collective-permute-done | bytes 524320 | tf_op jit(solution)/shard_map/ppermute | solution.py:15
  185.4 2.4 %collective-permute-done = f32[2,4,128,128]{3,2,1,0:T(8,128)S(1)} collective-permute-done((f32[2,4,128,128]{3,2,1,0:T(8,128)S(1)}, f32[2,4,128,128]{3,2,1,0:T(8,128)S(1)}, u32[]{:S(2)}, u32[]{:S(2)}) %collective-permute-start) | collective-permute-done | bytes 524320 | tf_op jit(solution)/shard_map/ppermute | solution.py:15
  187.8 1.0 fusion.4
  188.8 1.0 reshape.8
  (1 shorter events, 0.0 us)
Async XLA Ops:
  0.0 179.3 %copy-start = (f32[1,128,128]{2,1,0:T(8,128)S(1)}, f32[1,128,128]{2,1,0:T(8,128)}, u32[]{:S(2)}) copy-start(f32[1,128,128]{2,1,0:T(8,128)} %param.6) | copy-start | bytes 196612
  0.0 37.6 %copy-start.1 = (bf16[1,2,4,16384]{3,2,1,0:T(4,128)(2,1)S(1)}, bf16[1,2,4,16384]{3,2,1,0:T(4,128)(2,1)}, u32[]{:S(2)}) copy-start(bf16[1,2,4,16384]{3,2,1,0:T(4,128)(2,1)} %param.5) | copy-start | bytes 786436
  32.4 35.1 %all-to-all-start = ((bf16[8,2,8192]{2,1,0:T(2,128)(2,1)}), bf16[8,2,8192]{2,1,0:T(2,128)(2,1)S(1)}, u32[]{:S(2)}, u32[]{:S(2)}) async-start(bf16[8,2,8192]{2,1,0:T(2,128)(2,1)} %reshape.14), calls=%async_computation | async-start | bytes 524288 | tf_op jit(solution)/shard_map/all_to_all | solution.py:71
  67.6 42.9 %all-to-all-start.1 = ((bf16[8,2,8192]{2,1,0:T(2,128)(2,1)}), bf16[8,2,8192]{2,1,0:T(2,128)(2,1)S(1)}, u32[]{:S(2)}, u32[]{:S(2)}) async-start(bf16[8,2,8192]{2,1,0:T(2,128)(2,1)} %reshape.12), calls=%async_computation.1 | async-start | bytes 524288 | tf_op jit(solution)/shard_map/all_to_all | solution.py:72
  149.3 9.7 %copy-start.2 = (f32[1,128,128]{2,1,0:T(8,128)S(1)}, f32[1,128,128]{2,1,0:T(8,128)}, u32[]{:S(2)}) copy-start(f32[1,128,128]{2,1,0:T(8,128)} %param.7) | copy-start | bytes 196612
  154.9 13.9 %all-to-all-start.2 = ((f32[1,2,32,2048]{3,1,0,2:T(2,128)}), f32[1,2,32,2048]{3,1,0,2:T(2,128)S(1)}, u32[]{:S(2)}, u32[]{:S(2)}) async-start(f32[1,2,32,2048]{3,1,0,2:T(2,128)} %copy.39), calls=%async_computation.2 | async-start | bytes 1048576 | tf_op jit(solution)/shard_map/all_to_all | solution.py:75
  159.0 11.1 %collective-permute-start.1 = (f32[128,128]{1,0:T(8,128)S(1)}, f32[128,128]{1,0:T(8,128)S(1)}, u32[]{:S(2)}, u32[]{:S(2)}) collective-permute-start(f32[128,128]{1,0:T(8,128)S(1)} %bitcast.81), channel_id=1, source_target_pairs={{0,1},{1,2},{2,3},{4,5},{5,6},{6,7},{8,9},{9,10},{10,11},{12,13},{... | collective-permute-start | bytes 196616 | tf_op jit(solution)/shard_map/ppermute | solution.py:15
  172.2 13.2 %collective-permute-start.2 = (f32[2,4,128,128]{3,2,1,0:T(8,128)S(1)}, f32[2,4,128,128]{3,2,1,0:T(8,128)S(1)}, u32[]{:S(2)}, u32[]{:S(2)}) collective-permute-start(f32[2,4,128,128]{3,2,1,0:T(8,128)S(1)} %fusion.11), channel_id=1, source_target_pairs={{1,0},{2,1},{3,2},{5,4},{6,5},{7,6},{9,8},{10,9},{11,10},{13,12},{... | collective-permute-start | bytes 1572872 | tf_op jit(solution)/shard_map/ppermute | solution.py:15
  174.7 13.1 %collective-permute-start = (f32[2,4,128,128]{3,2,1,0:T(8,128)S(1)}, f32[2,4,128,128]{3,2,1,0:T(8,128)S(1)}, u32[]{:S(2)}, u32[]{:S(2)}) collective-permute-start(f32[2,4,128,128]{3,2,1,0:T(8,128)S(1)} %fusion.14), channel_id=1, source_target_pairs={{0,1},{1,2},{2,3},{4,5},{5,6},{6,7},{8,9},{9,10},{10,11},{12,13},{... | collective-permute-start | bytes 1572872 | tf_op jit(solution)/shard_map/ppermute | solution.py:15
where the time goes:
time: 193 us; the launch traced here: 190 us
  local copies, waits for them, and re-layouts  143 us (74%)
  starting transfers between devices  23.1 us (12%)
  waiting for transfers between devices  13.7 us (7%)
  matrix products  9.89 us (5%)
    unnamed x13, local copies, waits for them, and re-layouts  101 us
    all_to_all x1, local copies, waits for them, and re-layouts, per_device(): lax.all_to_all(lesser_pad, 'energy', split_axis=3, concat_axis=2, tiled=T...  19.2 us
    all_to_all x1, local copies, waits for them, and re-layouts, per_device(): lax.all_to_all(greater_pad, 'energy', split_axis=3, concat_axis=2, tiled=...  19.2 us
    ppermute x3, starting transfers between devices, shifted(): return lax.ppermute(x, axis, pairs)  9.58 us
    ppermute x3, waiting for transfers between devices, shifted(): return lax.ppermute(x, axis, pairs)  7.5 us
    all_to_all x1, waiting for transfers between devices, per_device(): lax.all_to_all(polar_tile, 'energy', split_axis=2, concat_axis=3, tiled=T...  6.24 us
    all_to_all x1, starting transfers between devices, per_device(): lax.all_to_all(lesser_pad, 'energy', split_axis=3, concat_axis=2, tiled=T...  5.17 us
    all_to_all x1, starting transfers between devices, per_device(): lax.all_to_all(polar_tile, 'energy', split_axis=2, concat_axis=3, tiled=T...  4.18 us
  transfers between devices with their start and end apart: 6, of which 3 were waited for; matrix products, arithmetic and copies ran while one was open for 38% of the time, Pallas kernels for 0%

commit v1 on v0

--- a/solution.py
+++ b/solution.py
@@ -26,9 +26,7 @@
     return (first - second, first + third)
 
 
-def correlate(lesser, greater):
-    count = lesser.shape[2]
-    width = lesser.shape[3]
+def correlate(both_re, both_im, count, width):
     length = 2 * count
     rows = lax.iota(jnp.int32, length)[:, None]
     cols = lax.iota(jnp.int32, count)[None, :]
@@ -37,8 +35,6 @@
     sine = jnp.sin(phase)
     fwd_sum = cosine - sine
     fwd_diff = -sine - cosine
-    both_re = jnp.concatenate([lesser[0, 0], greater[0, 0]], axis=1).astype(jnp.float32)
-    both_im = jnp.concatenate([lesser[0, 1], greater[0, 1]], axis=1).astype(jnp.float32)
     s_re, s_im = complex_apply(cosine, fwd_sum, fwd_diff, both_re, both_im)
     l_re = s_re[:, :width]
     l_im = s_im[:, :width]
@@ -50,7 +46,7 @@
     inv_sin = sine.T / length
     c_re, c_im = complex_apply(inv_cos, inv_cos + inv_sin, inv_sin - inv_cos, z_re, z_im)
     scale = count ** (-0.5)
-    return jnp.stack([-scale * c_im, scale * c_re])[None]
+    return jnp.stack([-scale * c_im, scale * c_re])
 
 
 def sandwich(left, field, right):
@@ -62,21 +58,30 @@
     groups = lax.axis_size("energy")
     e_local = g_lesser.shape[2]
     elements = g_lesser.shape[3]
+    count = e_local * groups
     tile_width = (elements + groups * QUANT - 1) // (groups * QUANT) * QUANT
     padding = tile_width * groups - elements
-    widths = ((0, 0), (0, 0), (0, 0), (0, padding))
-    lesser_pad = jnp.pad(g_lesser, widths)
-    greater_pad = jnp.pad(g_greater, widths)
-    lesser_tile, greater_tile = (
-        lax.all_to_all(lesser_pad, "energy", split_axis=3, concat_axis=2, tiled=True),
-        lax.all_to_all(greater_pad, "energy", split_axis=3, concat_axis=2, tiled=True),
-    )
-    polar_tile = correlate(lesser_tile, greater_tile)
-    polar_back = lax.all_to_all(polar_tile, "energy", split_axis=2, concat_axis=3, tiled=True)
-    polar = polar_back[:, :, :, :elements].reshape(2, e_local, BS, BS)
-    diag_block = v_diag[0]
+
     couple_own = v_couple[0]
     couple_prev = shifted(couple_own, "space", 1)
+
+    both = jnp.stack([g_lesser[0], g_greater[0]])
+    both = jnp.pad(both, ((0, 0), (0, 0), (0, 0), (0, padding)))
+    both = both.reshape(2, 2, e_local, groups, tile_width)
+    both = both.transpose(3, 0, 1, 2, 4).reshape(groups, 4 * e_local, tile_width)
+    got = lax.all_to_all(both, "energy", 0, 0, tiled=True)
+    got = got.reshape(groups, 2, 2, e_local, tile_width).astype(jnp.float32)
+    got = got.transpose(2, 0, 3, 1, 4).reshape(2, count, 2 * tile_width)
+    polar_tile = correlate(got[0], got[1], count, tile_width)
+
+    send = polar_tile.reshape(2, groups, e_local, tile_width).transpose(1, 0, 2, 3)
+    send = send.reshape(groups, 2 * e_local, tile_width)
+    back = lax.all_to_all(send, "energy", 0, 0, tiled=True)
+    back = back.reshape(groups, 2, e_local, tile_width).transpose(1, 2, 0, 3)
+    back = back.reshape(2, e_local, groups * tile_width)[:, :, :elements]
+    polar = back.reshape(2, e_local, BS, BS)
+
+    diag_block = v_diag[0]
     to_next = sandwich(couple_own.T, polar, couple_own)
     to_prev = sandwich(couple_prev, polar, couple_prev.T)
     from_below = shifted(to_next, "space", 1)

time: 193 us -> 60.1 us (0.31)
  the two profiles are of different devices: /device:TPU:0 before, /device:TPU:26 now
where the time goes in v1:
time: 60.1 us; the launch traced here: 59.7 us
  waiting for transfers between devices  20.2 us (34%)
  blocking collectives  12.3 us (20%)
  starting transfers between devices  10.1 us (17%)
  matrix products  9.88 us (16%)
  local copies, waits for them, and re-layouts  5.11 us (9%)
  other arithmetic  1.79 us (3%)
    ppermute x3, waiting for transfers between devices, shifted(): return lax.ppermute(x, axis, pairs)  13.2 us
    all_to_all x1, blocking collectives, per_device(): got = lax.all_to_all(both, 'energy', 0, 0, tiled=True)  12.3 us
    all_to_all x1, waiting for transfers between devices, per_device(): back = lax.all_to_all(send, 'energy', 0, 0, tiled=True)  7.01 us
    ppermute x3, starting transfers between devices, shifted(): return lax.ppermute(x, axis, pairs)  5.13 us
    all_to_all x1, starting transfers between devices, per_device(): back = lax.all_to_all(send, 'energy', 0, 0, tiled=True)  5 us
    dot_general x6, matrix products, product(): jnp.dot(left, right, precision=lax.Precision.HIGHEST, preferred_element_t...  3.92 us
    dot_general x3, matrix products, sandwich(): return jnp.matmul(inner, right, precision=lax.Precision.HIGHEST)  2.99 us
    dot_general x3, matrix products, sandwich(): inner = jnp.matmul(left, field, precision=lax.Precision.HIGHEST)  2.98 us
  transfers between devices with their start and end apart: 4, of which 3 were waited for; matrix products, arithmetic and copies ran while one was open for 6% of the time, Pallas kernels for 0%

profile of v1, /device:TPU:26, one launch (start us, length us, event | category | flops | bytes accessed | tf_op | source)
XLA Modules:
  0.0 59.7 jit_solution(3500478383097570853)
XLA Ops:
  0.0 0.0 copy-start
  0.0 1.5 %pad_maximum_fusion = bf16[2,2,4,16384]{3,2,1,0:T(4,128)(2,1)S(1)} fusion(bf16[1,2,4,16384]{3,2,1,0:T(4,128)(2,1)} %param.5, bf16[1,2,4,16384]{3,2,1,0:T(4,128)(2,1)} %param.4), kind=kLoop, calls=%fused_computation.13 | loop fusion | flops 262144 | bytes 1048576 | tf_op jit(solution)/shard_map/stack | solution.py:68
  1.5 0.2 copy.48
  1.7 0.1 reshape.34
  1.8 12.3 %all_to_all.10 = bf16[8,16,2048]{2,1,0:T(8,128)(2,1)S(1)} all-to-all(bf16[8,16,2048]{2,1,0:T(8,128)(2,1)S(1)} %reshape.34), channel_id=1, replica_groups=mesh['energy'=8,'space'=4] {'energy'}, dimensions={0} | all-to-all | bytes 1048576 | tf_op jit(solution)/shard_map/all_to_all | solution.py:72
  14.2 0.3 copy.19
  14.5 0.1 transpose.38
  14.6 0.1 slice_add_fusion
  14.7 0.4 copy.20
  15.1 0.3 copy.44
  15.4 1.1 %fusion.31 = f32[64,4096]{1,0:T(8,128)S(1)} fusion(f32[32,4096]{1,0:T(8,128)S(1)} %bitcast.73), kind=kOutput, calls=%fused_computation.50 | convolution fusion | flops 100691968 | bytes 1572864 | tf_op jit(solution)/shard_map/dot_general | solution.py:19
  16.5 0.3 copy.21
  16.8 0.1 copy.45
  16.9 0.3 copy.22
  17.2 0.1 copy.46
  17.3 0.7 %convolution_subtract_fusion = f32[64,4096]{1,0:T(8,128)S(1)} fusion(f32[64,4096]{1,0:T(8,128)S(1)} %fusion.31, bf16[32,4096]{1,0:T(8,128)(2,1)S(1)} %bitcast.79), kind=kOutput, calls=%fused_computation.1 | convolution fusion | flops 100956160 | bytes 2359296 | tf_op jit(solution)/shard_map/dot_general | solution.py:19
  18.0 0.7 %convolution_add_fusion = f32[64,4096]{1,0:T(8,128)S(1)} fusion(f32[64,4096]{1,0:T(8,128)S(1)} %fusion.31, bf16[32,4096]{1,0:T(8,128)(2,1)S(1)} %bitcast.80), kind=kOutput, calls=%fused_computation | convolution fusion | flops 100958208 | bytes 2359296 | tf_op jit(solution)/shard_map/dot_general | solution.py:19
  18.7 0.1 multiply_subtract_fusion
  18.8 0.5 fusion.3
  19.3 0.5 fusion.1
  19.8 0.5 fusion
  20.3 0.1 stack.13
  20.4 0.2 copy.23
  20.5 0.1 stack.14
  20.6 0.2 copy.24
  20.8 1.1 %copy.25 = f32[8,8,2048]{2,1,0:T(8,128)} copy(f32[8,8,2048]{2,0,1:T(8,128)S(1)} %bitcast.74) | data formatting | bytes 1048576 | tf_op jit(solution)/shard_map/reshape | solution.py:78
  21.9 0.0 copy-start.1
  21.9 5.0 %all-to-all-start.1 = ((f32[8,8,2048]{2,1,0:T(8,128)}), f32[8,8,2048]{2,1,0:T(8,128)S(1)}, u32[]{:S(2)}, u32[]{:S(2)}) async-start(f32[8,8,2048]{2,1,0:T(8,128)} %copy.25), calls=%async_computation.1 | async-start | bytes 1048576 | tf_op jit(solution)/shard_map/all_to_all | solution.py:79
  26.9 0.0 copy-done.1
  26.9 1.3 %collective-permute-start.1 = (f32[128,128]{1,0:T(8,128)S(1)}, f32[128,128]{1,0:T(8,128)S(1)}, u32[]{:S(2)}, u32[]{:S(2)}) collective-permute-start(f32[128,128]{1,0:T(8,128)S(1)} %bitcast.83), channel_id=1, source_target_pairs={{0,1},{1,2},{2,3},{4,5},{5,6},{6,7},{8,9},{9,10},{10,11},{12,13},{... | collective-permute-start | bytes 196616 | tf_op jit(solution)/shard_map/ppermute | solution.py:15
  28.2 7.0 %all-to-all-done.1 = f32[8,8,2048]{2,1,0:T(8,128)S(1)} async-done(((f32[8,8,2048]{2,1,0:T(8,128)}), f32[8,8,2048]{2,1,0:T(8,128)S(1)}, u32[]{:S(2)}, u32[]{:S(2)}) %all-to-all-start.1) | async-done | bytes 524320 | tf_op jit(solution)/shard_map/all_to_all | solution.py:79
  35.2 0.3 copy.42
  35.5 0.1 reshape_reshape.3
  35.6 1.0 %convolution_bitcast_fusion.1 = f32[2,4,128,128]{2,3,1,0:T(8,128)S(1)} fusion(f32[2,4,128,128]{3,2,1,0:T(8,128)S(1)} %reshape_reshape.3, f32[1,128,128]{2,1,0:T(8,128)S(1)} %copy-done.1), kind=kOutput, calls=%fused_computation.7 | convolution fusion | flops 201326592 | bytes 1114112 | tf_op jit(solution)/shard_map/dot_general | solution.py:53
  36.6 0.0 collective-permute-done.1
  36.6 1.0 %convolution_bitcast_fusion = f32[2,4,128,128]{2,3,1,0:T(8,128)S(1)} fusion(f32[2,4,128,128]{3,2,1,0:T(8,128)S(1)} %reshape_reshape.3, f32[128,128]{1,0:T(8,128)S(1)} %collective-permute-done.1), kind=kOutput, calls=%fused_computation.6 | convolution fusion | flops 201326592 | bytes 1114112 | tf_op jit(solution)/shard_map/dot_general | solution.py:53
  37.6 1.0 %fusion.5 = f32[2,4,128,128]{3,2,1,0:T(8,128)S(1)} fusion(f32[2,4,128,128]{2,3,1,0:T(8,128)S(1)} %convolution_bitcast_fusion, f32[128,128]{1,0:T(8,128)S(1)} %collective-permute-done.1), kind=kOutput, calls=%fused_computation.19 | convolution fusion | flops 201326592 | bytes 1114112 | tf_op jit(solution)/shard_map/dot_general | solution.py:54
  38.6 2.6 %collective-permute-start.2 = (f32[2,4,128,128]{3,2,1,0:T(8,128)S(1)}, f32[2,4,128,128]{3,2,1,0:T(8,128)S(1)}, u32[]{:S(2)}, u32[]{:S(2)}) collective-permute-start(f32[2,4,128,128]{3,2,1,0:T(8,128)S(1)} %fusion.5), channel_id=1, source_target_pairs={{1,0},{2,1},{3,2},{5,4},{6,5},{7,6},{9,8},{10,9},{11,10},{13,12},{... | collective-permute-start | bytes 1572872 | tf_op jit(solution)/shard_map/ppermute | solution.py:15
  41.2 1.0 %fusion.8 = f32[2,4,128,128]{3,2,1,0:T(8,128)S(1)} fusion(f32[2,4,128,128]{2,3,1,0:T(8,128)S(1)} %convolution_bitcast_fusion.1, f32[1,128,128]{2,1,0:T(8,128)S(1)} %copy-done.1), kind=kOutput, calls=%fused_computation.22 | convolution fusion | flops 201326592 | bytes 1114112 | tf_op jit(solution)/shard_map/dot_general | solution.py:54
  42.2 1.3 %collective-permute-start = (f32[2,4,128,128]{3,2,1,0:T(8,128)S(1)}, f32[2,4,128,128]{3,2,1,0:T(8,128)S(1)}, u32[]{:S(2)}, u32[]{:S(2)}) collective-permute-start(f32[2,4,128,128]{3,2,1,0:T(8,128)S(1)} %fusion.8), channel_id=1, source_target_pairs={{0,1},{1,2},{2,3},{4,5},{5,6},{6,7},{8,9},{9,10},{10,11},{12,13},{... | collective-permute-start | bytes 1572872 | tf_op jit(solution)/shard_map/ppermute | solution.py:15
  43.5 0.0 copy-done
  43.5 1.0 %convolution_bitcast_fusion.2 = f32[2,4,128,128]{2,3,1,0:T(8,128)S(1)} fusion(f32[2,4,128,128]{3,2,1,0:T(8,128)S(1)} %reshape_reshape.3, f32[1,128,128]{2,1,0:T(8,128)S(1)} %copy-done), kind=kOutput, calls=%fused_computation.8 | convolution fusion | flops 201326592 | bytes 1114112 | tf_op jit(solution)/shard_map/dot_general | solution.py:53
  44.5 7.9 %collective-permute-done.2 = f32[2,4,128,128]{3,2,1,0:T(8,128)S(1)} collective-permute-done((f32[2,4,128,128]{3,2,1,0:T(8,128)S(1)}, f32[2,4,128,128]{3,2,1,0:T(8,128)S(1)}, u32[]{:S(2)}, u32[]{:S(2)}) %collective-permute-start.2) | collective-permute-done | bytes 524320 | tf_op jit(solution)/shard_map/ppermute | solution.py:15
  52.4 5.3 %collective-permute-done = f32[2,4,128,128]{3,2,1,0:T(8,128)S(1)} collective-permute-done((f32[2,4,128,128]{3,2,1,0:T(8,128)S(1)}, f32[2,4,128,128]{3,2,1,0:T(8,128)S(1)}, u32[]{:S(2)}, u32[]{:S(2)}) %collective-permute-start) | collective-permute-done | bytes 524320 | tf_op jit(solution)/shard_map/ppermute | solution.py:15
  57.7 1.0 %fusion.2 = f32[2,4,128,128]{3,2,1,0:T(8,128)S(1)} fusion(f32[2,4,128,128]{3,2,1,0:T(8,128)S(1)} %collective-permute-done.2, f32[2,4,128,128]{3,2,1,0:T(8,128)S(1)} %collective-permute-done, f32[2,4,128,128]{2,3,1,0:T(8,128)S(1)} %convolution_bitcast_fusion.2, f32[1,128,128]{2,1,0:T(8,128)S(1)} %copy-done), kind=kOutput, calls=%fused_computation.10 | convolution fusion | flops 201588736 | bytes 2162688 | tf_op jit(solution)/shard_map/dot_general | solution.py:54
  58.7 1.0 %reshape.38 = f32[1,2,4,16384]{3,2,1,0:T(4,128)} reshape(f32[2,4,128,128]{3,2,1,0:T(8,128)S(1)} %fusion.2) | data formatting | bytes 1048576 | tf_op jit(solution)/shard_map/reshape | solution.py:91
  (2 shorter events, 0.1 us)
Async XLA Ops:
  0.0 43.5 %copy-start = (f32[1,128,128]{2,1,0:T(8,128)S(1)}, f32[1,128,128]{2,1,0:T(8,128)}, u32[]{:S(2)}) copy-start(f32[1,128,128]{2,1,0:T(8,128)} %param.6) | copy-start | bytes 196612
  21.9 5.0 %copy-start.1 = (f32[1,128,128]{2,1,0:T(8,128)S(1)}, f32[1,128,128]{2,1,0:T(8,128)}, u32[]{:S(2)}) copy-start(f32[1,128,128]{2,1,0:T(8,128)} %param.7) | copy-start | bytes 196612
  21.9 13.3 %all-to-all-start.1 = ((f32[8,8,2048]{2,1,0:T(8,128)}), f32[8,8,2048]{2,1,0:T(8,128)S(1)}, u32[]{:S(2)}, u32[]{:S(2)}) async-start(f32[8,8,2048]{2,1,0:T(8,128)} %copy.25), calls=%async_computation.1 | async-start | bytes 1048576 | tf_op jit(solution)/shard_map/all_to_all | solution.py:79
  26.9 9.7 %collective-permute-start.1 = (f32[128,128]{1,0:T(8,128)S(1)}, f32[128,128]{1,0:T(8,128)S(1)}, u32[]{:S(2)}, u32[]{:S(2)}) collective-permute-start(f32[128,128]{1,0:T(8,128)S(1)} %bitcast.83), channel_id=1, source_target_pairs={{0,1},{1,2},{2,3},{4,5},{5,6},{6,7},{8,9},{9,10},{10,11},{12,13},{... | collective-permute-start | bytes 196616 | tf_op jit(solution)/shard_map/ppermute | solution.py:15
  38.6 13.7 %collective-permute-start.2 = (f32[2,4,128,128]{3,2,1,0:T(8,128)S(1)}, f32[2,4,128,128]{3,2,1,0:T(8,128)S(1)}, u32[]{:S(2)}, u32[]{:S(2)}) collective-permute-start(f32[2,4,128,128]{3,2,1,0:T(8,128)S(1)} %fusion.5), channel_id=1, source_target_pairs={{1,0},{2,1},{3,2},{5,4},{6,5},{7,6},{9,8},{10,9},{11,10},{13,12},{... | collective-permute-start | bytes 1572872 | tf_op jit(solution)/shard_map/ppermute | solution.py:15
  42.2 15.5 %collective-permute-start = (f32[2,4,128,128]{3,2,1,0:T(8,128)S(1)}, f32[2,4,128,128]{3,2,1,0:T(8,128)S(1)}, u32[]{:S(2)}, u32[]{:S(2)}) collective-permute-start(f32[2,4,128,128]{3,2,1,0:T(8,128)S(1)} %fusion.8), channel_id=1, source_target_pairs={{0,1},{1,2},{2,3},{4,5},{5,6},{6,7},{8,9},{9,10},{10,11},{12,13},{... | collective-permute-start | bytes 1572872 | tf_op jit(solution)/shard_map/ppermute | solution.py:15

commit v2 on v1

v2 whole, which is shorter than its diff:
```python
import math

import jax
import jax.numpy as jnp
from jax import lax
from jax.sharding import PartitionSpec as P

BS = 128
QUANT = 128


def shifted(x, axis, by):
    devices = lax.axis_size(axis)
    pairs = [(i, i + by) for i in range(devices) if 0 <= i + by < devices]
    return lax.ppermute(x, axis, pairs)


def tables(count, e_local, groups):
    length = 2 * count
    k = lax.iota(jnp.int32, length)
    n = lax.iota(jnp.int32, count)
    phase = ((k[:, None] * n[None, :]) % length).astype(jnp.float32) * (2.0 * math.pi / length)
    cosine = jnp.cos(phase)
    sine = jnp.sin(phase)
    re_rows = jnp.stack([cosine, sine], axis=1)
    im_rows = jnp.stack([-sine, cosine], axis=1)
    per_part = jnp.stack([re_rows, im_rows])
    per_part = per_part.reshape(2, length, 2, groups, e_local).transpose(0, 1, 3, 2, 4)
    zero = jnp.zeros_like(per_part)
    lesser_rows = jnp.stack([per_part, zero], axis=3)
    greater_rows = jnp.stack([zero, per_part], axis=3)
    forward = jnp.stack([lesser_rows, greater_rows]).reshape(4 * length, 4 * count)
    scale = count ** (-0.5) / length
    inv_cos = cosine.T * scale
    inv_sin = sine.T * scale
    ri0 = jnp.concatenate([-inv_sin, -inv_cos], axis=1)
    ri1 = jnp.concatenate([inv_cos, -inv_sin], axis=1)
    inverse = jnp.stack([ri0, ri1]).reshape(2, groups, e_local, 2 * length)
    inverse = inverse.transpose(1, 0, 2, 3).reshape(2 * count, 2 * length)
    return forward, inverse


def correlate(got, forward, inverse):
    high = lax.reduce_precision(forward, exponent_bits=8, mantissa_bits=7)
    low = forward - high
    split = jnp.concatenate([high, low]).astype(jnp.bfloat16)
    both = jnp.dot(split, got, preferred_element_type=jnp.float32)
    rows = forward.shape[0]
    spectrum = both[:rows] + both[rows:]
    length = rows // 4
    l_re, l_im, g_re, g_im = (spectrum[i * length:(i + 1) * length] for i in range(4))
    z_re = l_re * g_re + l_im * g_im
    z_im = l_im * g_re - l_re * g_im
    z = jnp.concatenate([z_re, z_im])
    return jnp.dot(inverse, z, precision=lax.Precision.HIGHEST, preferred_element_type=jnp.float32)


def sandwich(left, field, right):
    inner = jnp.matmul(left, field, precision=lax.Precision.HIGHEST)
    return jnp.matmul(inner, right, precision=lax.Precision.HIGHEST)


def per_device(g_lesser, g_greater, v_diag, v_couple):
    groups = lax.axis_size("energy")
    e_local = g_lesser.shape[2]
    elements = g_lesser.shape[3]
    count = e_local * groups
    tile_width = (elements + groups * QUANT - 1) // (groups * QUANT) * QUANT
    padding = tile_width * groups - elements

    couple_own = v_couple[0]
    couple_prev = shifted(couple_own, "space", 1)
    forward, inverse = tables(count, e_local, groups)

    both = jnp.stack([g_lesser[0], g_greater[0]])
    both = jnp.pad(both, ((0, 0), (0, 0), (0, 0), (0, padding)))
    both = both.reshape(2, 2, e_local, groups, tile_width)
    both = both.transpose(3, 0, 1, 2, 4).reshape(groups, 4 * e_local, tile_width)
    got = lax.all_to_all(both, "energy", 0, 0, tiled=True)
    polar_tile = correlate(got.reshape(groups * 4 * e_local, tile_width), forward, inverse)

    send = polar_tile.reshape(groups, 2 * e_local, tile_width)
    back = lax.all_to_all(send, "energy", 0, 0, tiled=True)
    back = back.reshape(groups, 2, e_local, tile_width).transpose(1, 2, 0, 3)
    back = back.reshape(2, e_local, groups * tile_width)[:, :, :elements]
    polar = back.reshape(2, e_local, BS, BS)

    polar_below = shifted(polar, "space", 1)
    polar_above = shifted(polar, "space", -1)
    diag_block = v_diag[0]
    local = sandwich(diag_block, polar, diag_block)
    from_below = sandwich(couple_prev.T, polar_below, couple_prev)
    from_above = sandwich(couple_own, polar_above, couple_own.T)
    total = local + from_below + from_above
    return total.reshape(1, 2, e_local, elements)


def solution(mesh):
    placed = (
        P("space", None, "energy", None),
        P("space", None, "energy", None),
        P("space", None, None),
        P("space", None, None),
    )
    return jax.shard_map(
        per_device,
        mesh=mesh,
        in_specs=placed,
        out_specs=P("space", None, "energy", None),
        check_vma=False,
    )
```

time: 60.1 us -> 55.6 us (0.925)
  the two profiles are of different devices: /device:TPU:26 before, /device:TPU:0 now
where the time goes in v2:
time: 55.6 us; the launch traced here: 55.3 us
  waiting for transfers between devices  15.9 us (29%)
  starting transfers between devices  14.5 us (26%)
  blocking collectives  12.3 us (22%)
  matrix products  6.52 us (12%)
  local copies, waits for them, and re-layouts  3.34 us (6%)
  other arithmetic  2.44 us (4%)
    all_to_all x1, blocking collectives, per_device(): back = lax.all_to_all(send, 'energy', 0, 0, tiled=True)  12.3 us
    ppermute x3, starting transfers between devices, shifted(): return lax.ppermute(x, axis, pairs)  9.36 us
    all_to_all x1, waiting for transfers between devices, per_device(): got = lax.all_to_all(both, 'energy', 0, 0, tiled=True)  8.63 us
    ppermute x3, waiting for transfers between devices, shifted(): return lax.ppermute(x, axis, pairs)  7.31 us
    all_to_all x1, starting transfers between devices, per_device(): got = lax.all_to_all(both, 'energy', 0, 0, tiled=True)  5.17 us
    dot_general x3, matrix products, sandwich(): return jnp.matmul(inner, right, precision=lax.Precision.HIGHEST)  2.99 us
    dot_general x3, matrix products, sandwich(): inner = jnp.matmul(left, field, precision=lax.Precision.HIGHEST)  2.13 us
    another operation x1, other arithmetic, per_device(): both = jnp.stack([g_lesser[0], g_greater[0]])  1.45 us
  transfers between devices with their start and end apart: 4, of which 3 were waited for; matrix products, arithmetic and copies ran while one was open for 7% of the time, Pallas kernels for 0%

profile of v2, /device:TPU:0, one launch (start us, length us, event | category | flops | bytes accessed | tf_op | source)
XLA Modules:
  0.0 55.3 jit_solution(10966078606390816935)
XLA Ops:
  0.0 0.0 copy-start
  0.0 1.5 %pad_maximum_fusion = bf16[2,2,4,16384]{3,2,1,0:T(4,128)(2,1)S(1)} fusion(bf16[1,2,4,16384]{3,2,1,0:T(4,128)(2,1)} %param.5, bf16[1,2,4,16384]{3,2,1,0:T(4,128)(2,1)} %param.4), kind=kLoop, calls=%fused_computation.11 | loop fusion | flops 262144 | bytes 1048576 | tf_op jit(solution)/shard_map/stack | solution.py:75
  1.5 0.2 copy.28
  1.7 0.9 %reshape.195 = bf16[8,16,2048]{2,1,0:T(8,128)(2,1)} reshape(bf16[8,2,2,4,2048]{4,3,2,1,0:T(4,128)(2,1)S(1)} %bitcast.71) | data formatting | bytes 1048576 | tf_op jit(solution)/shard_map/reshape | solution.py:78
  2.6 5.2 %all-to-all-start = ((bf16[8,16,2048]{2,1,0:T(8,128)(2,1)}), bf16[8,16,2048]{2,1,0:T(8,128)(2,1)S(1)}, u32[]{:S(2)}, u32[]{:S(2)}) async-start(bf16[8,16,2048]{2,1,0:T(8,128)(2,1)} %reshape.195), calls=%async_computation | async-start | bytes 1048576 | tf_op jit(solution)/shard_map/all_to_all | solution.py:79
  7.8 0.2 fusion.24
  8.0 0.1 copy.8
  8.1 0.2 copy.9
  8.3 0.3 reshape.193
  8.6 0.2 fusion.27
  8.8 0.1 maximum_maximum_fusion
  8.9 8.6 %all-to-all-done = bf16[8,16,2048]{2,1,0:T(8,128)(2,1)S(1)} async-done(((bf16[8,16,2048]{2,1,0:T(8,128)(2,1)}), bf16[8,16,2048]{2,1,0:T(8,128)(2,1)S(1)}, u32[]{:S(2)}, u32[]{:S(2)}) %all-to-all-start) | async-done | bytes 524320 | tf_op jit(solution)/shard_map/all_to_all | solution.py:79
  17.5 0.7 %fusion.4 = f32[512,2048]{1,0:T(8,128)S(1)} fusion(bf16[128,2048]{1,0:T(8,128)(2,1)S(1)} %bitcast.70, bf16[256,128]{0,1:T(8,128)(2,1)S(1)} %get-tuple-element.8, bf16[256,128]{0,1:T(8,128)(2,1)S(1)} %get-tuple-element.7), kind=kOutput, calls=%fused_computation.18 | convolution fusion | flops 268697600 | bytes 4849664 | tf_op jit(solution)/shard_map/dot_general | solution.py:47
  18.3 0.3 slice_add_fusion
  18.6 0.1 multiply_add_fusion
  18.8 0.7 %fusion = f32[8,8,2048]{2,1,0:T(8,128)S(1)} fusion(f32[8,8,128]{2,1,0:T(8,128)S(1)} %bitcast.75, f32[64,2048]{1,0:T(8,128)S(1)} %get-tuple-element.6, f32[64,2048]{1,0:T(8,128)S(1)} %get-tuple-element.5), kind=kOutput, calls=%fused_computation.7 | convolution fusion | flops 201588736 | bytes 1605632 | tf_op jit(solution)/shard_map/dot_general | solution.py:55
  19.4 0.0 copy-start.1
  19.5 12.3 %all_to_all.10 = f32[8,8,2048]{2,1,0:T(8,128)S(1)} all-to-all(f32[8,8,2048]{2,1,0:T(8,128)S(1)} %fusion), channel_id=1, replica_groups=mesh['energy'=8,'space'=4] {'energy'}, dimensions={0} | all-to-all | bytes 1048576 | tf_op jit(solution)/shard_map/all_to_all | solution.py:83
  31.7 0.3 copy.25
  32.1 0.1 reshape_reshape.3
  32.1 0.2 copy.14
  32.4 1.3 %collective-permute-start.2 = (f32[2,4,128,128]{2,3,1,0:T(8,128)S(1)}, f32[2,4,128,128]{2,3,1,0:T(8,128)S(1)}, u32[]{:S(2)}, u32[]{:S(2)}) collective-permute-start(f32[2,4,128,128]{2,3,1,0:T(8,128)S(1)} %copy.14), channel_id=1, source_target_pairs={{1,0},{2,1},{3,2},{5,4},{6,5},{7,6},{9,8},{10,9},{11,10},{13,12},{... | collective-permute-start | bytes 1572872 | tf_op jit(solution)/shard_map/ppermute | solution.py:15
  33.7 0.0 copy-done.1
  33.7 4.5 %collective-permute-start.1 = (f32[128,128]{1,0:T(8,128)S(1)}, f32[128,128]{1,0:T(8,128)S(1)}, u32[]{:S(2)}, u32[]{:S(2)}) collective-permute-start(f32[128,128]{1,0:T(8,128)S(1)} %bitcast.74), channel_id=1, source_target_pairs={{0,1},{1,2},{2,3},{4,5},{5,6},{6,7},{8,9},{9,10},{10,11},{12,13},{... | collective-permute-start | bytes 196616 | tf_op jit(solution)/shard_map/ppermute | solution.py:15
  38.2 3.5 %collective-permute-start = (f32[2,4,128,128]{2,3,1,0:T(8,128)S(1)}, f32[2,4,128,128]{2,3,1,0:T(8,128)S(1)}, u32[]{:S(2)}, u32[]{:S(2)}) collective-permute-start(f32[2,4,128,128]{2,3,1,0:T(8,128)S(1)} %copy.14), channel_id=1, source_target_pairs={{0,1},{1,2},{2,3},{4,5},{5,6},{6,7},{8,9},{9,10},{10,11},{12,13},{... | collective-permute-start | bytes 1572872 | tf_op jit(solution)/shard_map/ppermute | solution.py:15
  41.7 0.0 copy-done
  41.8 1.0 %convolution_bitcast_fusion.2 = f32[2,4,128,128]{2,3,1,0:T(8,128)S(1)} fusion(f32[2,4,128,128]{3,2,1,0:T(8,128)S(1)} %reshape_reshape.3, f32[1,128,128]{2,1,0:T(8,128)S(1)} %copy-done), kind=kOutput, calls=%fused_computation.3 | convolution fusion | flops 201326592 | bytes 1114112 | tf_op jit(solution)/shard_map/dot_general | solution.py:59
  42.8 1.0 %fusion.12 = f32[2,4,128,128]{3,2,1,0:T(8,128)S(1)} fusion(f32[2,4,128,128]{2,3,1,0:T(8,128)S(1)} %convolution_bitcast_fusion.2, f32[1,128,128]{2,1,0:T(8,128)S(1)} %copy-done), kind=kOutput, calls=%fused_computation.29 | convolution fusion | flops 201326592 | bytes 1114112 | tf_op jit(solution)/shard_map/dot_general | solution.py:60
  43.8 3.5 %collective-permute-done.2 = f32[2,4,128,128]{2,3,1,0:T(8,128)S(1)} collective-permute-done((f32[2,4,128,128]{2,3,1,0:T(8,128)S(1)}, f32[2,4,128,128]{2,3,1,0:T(8,128)S(1)}, u32[]{:S(2)}, u32[]{:S(2)}) %collective-permute-start.2) | collective-permute-done | bytes 524320 | tf_op jit(solution)/shard_map/ppermute | solution.py:15
  47.3 0.6 %convolution_bitcast_fusion = f32[2,4,128,128]{2,3,1,0:T(8,128)S(1)} fusion(f32[2,4,128,128]{2,3,1,0:T(8,128)S(1)} %collective-permute-done.2, f32[1,128,128]{2,1,0:T(8,128)S(1)} %copy-done.1), kind=kOutput, calls=%fused_computation.1 | convolution fusion | flops 201326592 | bytes 1114112 | tf_op jit(solution)/shard_map/dot_general | solution.py:59
  47.8 0.0 collective-permute-done.1
  47.9 3.8 %collective-permute-done = f32[2,4,128,128]{2,3,1,0:T(8,128)S(1)} collective-permute-done((f32[2,4,128,128]{2,3,1,0:T(8,128)S(1)}, f32[2,4,128,128]{2,3,1,0:T(8,128)S(1)}, u32[]{:S(2)}, u32[]{:S(2)}) %collective-permute-start) | collective-permute-done | bytes 524320 | tf_op jit(solution)/shard_map/ppermute | solution.py:15
  51.7 0.6 %convolution_bitcast_fusion.1 = f32[2,4,128,128]{2,3,1,0:T(8,128)S(1)} fusion(f32[2,4,128,128]{2,3,1,0:T(8,128)S(1)} %collective-permute-done, f32[128,128]{1,0:T(8,128)S(1)} %collective-permute-done.1), kind=kOutput, calls=%fused_computation.2 | convolution fusion | flops 201326592 | bytes 1114112 | tf_op jit(solution)/shard_map/dot_general | solution.py:59
  52.2 1.0 %convolution_add_fusion.1 = f32[2,4,128,128]{3,2,1,0:T(8,128)S(1)} fusion(f32[2,4,128,128]{3,2,1,0:T(8,128)S(1)} %fusion.12, f32[2,4,128,128]{2,3,1,0:T(8,128)S(1)} %convolution_bitcast_fusion.1, f32[128,128]{1,0:T(8,128)S(1)} %collective-permute-done.1), kind=kOutput, calls=%fused_computation.5 | convolution fusion | flops 201457664 | bytes 1638400 | tf_op jit(solution)/shard_map/dot_general | solution.py:60
  53.2 1.0 %convolution_add_fusion = f32[2,4,128,128]{3,2,1,0:T(8,128)S(1)} fusion(f32[2,4,128,128]{3,2,1,0:T(8,128)S(1)} %convolution_add_fusion.1, f32[2,4,128,128]{2,3,1,0:T(8,128)S(1)} %convolution_bitcast_fusion, f32[1,128,128]{2,1,0:T(8,128)S(1)} %copy-done.1), kind=kOutput, calls=%fused_computation.4 | convolution fusion | flops 201457664 | bytes 1638400 | tf_op jit(solution)/shard_map/dot_general | solution.py:60
  54.2 1.0 %reshape.198 = f32[1,2,4,16384]{3,2,1,0:T(4,128)} reshape(f32[2,4,128,128]{3,2,1,0:T(8,128)S(1)} %convolution_add_fusion) | data formatting | bytes 1048576 | tf_op jit(solution)/shard_map/reshape | solution.py:95
  (5 shorter events, 0.1 us)
Async XLA Ops:
  0.0 41.7 %copy-start = (f32[1,128,128]{2,1,0:T(8,128)S(1)}, f32[1,128,128]{2,1,0:T(8,128)}, u32[]{:S(2)}) copy-start(f32[1,128,128]{2,1,0:T(8,128)} %param.6) | copy-start | bytes 196612
  2.6 14.9 %all-to-all-start = ((bf16[8,16,2048]{2,1,0:T(8,128)(2,1)}), bf16[8,16,2048]{2,1,0:T(8,128)(2,1)S(1)}, u32[]{:S(2)}, u32[]{:S(2)}) async-start(bf16[8,16,2048]{2,1,0:T(8,128)(2,1)} %reshape.195), calls=%async_computation | async-start | bytes 1048576 | tf_op jit(solution)/shard_map/all_to_all | solution.py:79
  19.4 14.2 %copy-start.1 = (f32[1,128,128]{2,1,0:T(8,128)S(1)}, f32[1,128,128]{2,1,0:T(8,128)}, u32[]{:S(2)}) copy-start(f32[1,128,128]{2,1,0:T(8,128)} %param.7) | copy-start | bytes 196612
  32.4 14.9 %collective-permute-start.2 = (f32[2,4,128,128]{2,3,1,0:T(8,128)S(1)}, f32[2,4,128,128]{2,3,1,0:T(8,128)S(1)}, u32[]{:S(2)}, u32[]{:S(2)}) collective-permute-start(f32[2,4,128,128]{2,3,1,0:T(8,128)S(1)} %copy.14), channel_id=1, source_target_pairs={{1,0},{2,1},{3,2},{5,4},{6,5},{7,6},{9,8},{10,9},{11,10},{13,12},{... | collective-permute-start | bytes 1572872 | tf_op jit(solution)/shard_map/ppermute | solution.py:15
  33.7 14.2 %collective-permute-start.1 = (f32[128,128]{1,0:T(8,128)S(1)}, f32[128,128]{1,0:T(8,128)S(1)}, u32[]{:S(2)}, u32[]{:S(2)}) collective-permute-start(f32[128,128]{1,0:T(8,128)S(1)} %bitcast.74), channel_id=1, source_target_pairs={{0,1},{1,2},{2,3},{4,5},{5,6},{6,7},{8,9},{9,10},{10,11},{12,13},{... | collective-permute-start | bytes 196616 | tf_op jit(solution)/shard_map/ppermute | solution.py:15
  38.2 13.4 %collective-permute-start = (f32[2,4,128,128]{2,3,1,0:T(8,128)S(1)}, f32[2,4,128,128]{2,3,1,0:T(8,128)S(1)}, u32[]{:S(2)}, u32[]{:S(2)}) collective-permute-start(f32[2,4,128,128]{2,3,1,0:T(8,128)S(1)} %copy.14), channel_id=1, source_target_pairs={{0,1},{1,2},{2,3},{4,5},{5,6},{6,7},{8,9},{9,10},{10,11},{12,13},{... | collective-permute-start | bytes 1572872 | tf_op jit(solution)/shard_map/ppermute | solution.py:15

commit v3 on v2

--- a/solution.py
+++ b/solution.py
@@ -69,7 +69,6 @@
     padding = tile_width * groups - elements
 
     couple_own = v_couple[0]
-    couple_prev = shifted(couple_own, "space", 1)
     forward, inverse = tables(count, e_local, groups)
 
     both = jnp.stack([g_lesser[0], g_greater[0]])
@@ -85,11 +84,11 @@
     back = back.reshape(2, e_local, groups * tile_width)[:, :, :elements]
     polar = back.reshape(2, e_local, BS, BS)
 
-    polar_below = shifted(polar, "space", 1)
+    diag_block = v_diag[0]
     polar_above = shifted(polar, "space", -1)
-    diag_block = v_diag[0]
+    to_next = sandwich(couple_own.T, polar, couple_own)
+    from_below = shifted(to_next, "space", 1)
     local = sandwich(diag_block, polar, diag_block)
-    from_below = sandwich(couple_prev.T, polar_below, couple_prev)
     from_above = sandwich(couple_own, polar_above, couple_own.T)
     total = local + from_below + from_above
     return total.reshape(1, 2, e_local, elements)

time: 55.6 us -> 52.7 us (0.948)
  starting transfers between devices: 14.5 us -> 11 us
    ppermute x3 -> x2, starting transfers between devices: 9.36 us -> 5.87 us  [shifted(): return lax.ppermute(x, axis, pairs)]
    ppermute x3 -> x2, waiting for transfers between devices: 7.31 us -> 7.6 us  [shifted(): return lax.ppermute(x, axis, pairs)]
  transfers between devices with their start and end apart: 4 -> 3, of which waited for: 3 -> 3; matrix products, arithmetic and copies ran while one was open for 7% -> 11% of each run, Pallas kernels for 0% -> 0%
where the time goes in v3:
time: 52.7 us; the launch traced here: 52.3 us
  waiting for transfers between devices  16.2 us (31%)
  blocking collectives  12.2 us (23%)
  starting transfers between devices  11 us (21%)
  matrix products  6.96 us (13%)
  local copies, waits for them, and re-layouts  3.34 us (6%)
  other arithmetic  2.44 us (5%)
    all_to_all x1, blocking collectives, per_device(): back = lax.all_to_all(send, 'energy', 0, 0, tiled=True)  12.2 us
    all_to_all x1, waiting for transfers between devices, per_device(): got = lax.all_to_all(both, 'energy', 0, 0, tiled=True)  8.63 us
    ppermute x2, waiting for transfers between devices, shifted(): return lax.ppermute(x, axis, pairs)  7.6 us
    ppermute x2, starting transfers between devices, shifted(): return lax.ppermute(x, axis, pairs)  5.87 us
    all_to_all x1, starting transfers between devices, per_device(): got = lax.all_to_all(both, 'energy', 0, 0, tiled=True)  5.17 us
    dot_general x3, matrix products, sandwich(): return jnp.matmul(inner, right, precision=lax.Precision.HIGHEST)  2.99 us
    dot_general x3, matrix products, sandwich(): inner = jnp.matmul(left, field, precision=lax.Precision.HIGHEST)  2.56 us
    another operation x1, other arithmetic, per_device(): both = jnp.stack([g_lesser[0], g_greater[0]])  1.45 us
  transfers between devices with their start and end apart: 3, of which 3 were waited for; matrix products, arithmetic and copies ran while one was open for 11% of the time, Pallas kernels for 0%

profile of v3, /device:TPU:0, one launch (start us, length us, event | category | flops | bytes accessed | tf_op | source)
XLA Modules:
  0.0 52.3 jit_solution(1556001151868927371)
XLA Ops:
  0.0 0.0 copy-start
  0.0 1.5 %pad_maximum_fusion = bf16[2,2,4,16384]{3,2,1,0:T(4,128)(2,1)S(1)} fusion(bf16[1,2,4,16384]{3,2,1,0:T(4,128)(2,1)} %param.5, bf16[1,2,4,16384]{3,2,1,0:T(4,128)(2,1)} %param.4), kind=kLoop, calls=%fused_computation.11 | loop fusion | flops 262144 | bytes 1048576 | tf_op jit(solution)/shard_map/stack | solution.py:74
  1.5 0.2 copy.28
  1.7 0.9 %reshape.195 = bf16[8,16,2048]{2,1,0:T(8,128)(2,1)} reshape(bf16[8,2,2,4,2048]{4,3,2,1,0:T(4,128)(2,1)S(1)} %bitcast.68) | data formatting | bytes 1048576 | tf_op jit(solution)/shard_map/reshape | solution.py:77
  2.6 5.2 %all-to-all-start = ((bf16[8,16,2048]{2,1,0:T(8,128)(2,1)}), bf16[8,16,2048]{2,1,0:T(8,128)(2,1)S(1)}, u32[]{:S(2)}, u32[]{:S(2)}) async-start(bf16[8,16,2048]{2,1,0:T(8,128)(2,1)} %reshape.195), calls=%async_computation | async-start | bytes 1048576 | tf_op jit(solution)/shard_map/all_to_all | solution.py:78
  7.8 0.2 fusion.26
  8.0 0.1 copy.8
  8.1 0.2 copy.9
  8.3 0.3 reshape.193
  8.6 0.2 fusion.29
  8.8 0.1 maximum_maximum_fusion
  8.9 8.6 %all-to-all-done = bf16[8,16,2048]{2,1,0:T(8,128)(2,1)S(1)} async-done(((bf16[8,16,2048]{2,1,0:T(8,128)(2,1)}), bf16[8,16,2048]{2,1,0:T(8,128)(2,1)S(1)}, u32[]{:S(2)}, u32[]{:S(2)}) %all-to-all-start) | async-done | bytes 524320 | tf_op jit(solution)/shard_map/all_to_all | solution.py:78
  17.5 0.7 %fusion.5 = f32[512,2048]{1,0:T(8,128)S(1)} fusion(bf16[128,2048]{1,0:T(8,128)(2,1)S(1)} %bitcast.67, bf16[256,128]{0,1:T(8,128)(2,1)S(1)} %get-tuple-element.8, bf16[256,128]{0,1:T(8,128)(2,1)S(1)} %get-tuple-element.7), kind=kOutput, calls=%fused_computation.18 | convolution fusion | flops 268697600 | bytes 4849664 | tf_op jit(solution)/shard_map/dot_general | solution.py:47
  18.3 0.3 slice_add_fusion
  18.6 0.1 multiply_add_fusion
  18.8 0.7 %fusion.1 = f32[8,8,2048]{2,1,0:T(8,128)S(1)} fusion(f32[8,8,128]{2,1,0:T(8,128)S(1)} %bitcast.71, f32[64,2048]{1,0:T(8,128)S(1)} %get-tuple-element.6, f32[64,2048]{1,0:T(8,128)S(1)} %get-tuple-element.5), kind=kOutput, calls=%fused_computation.7 | convolution fusion | flops 201588736 | bytes 1605632 | tf_op jit(solution)/shard_map/dot_general | solution.py:55
  19.4 12.2 %all_to_all.10 = f32[8,8,2048]{2,1,0:T(8,128)S(1)} all-to-all(f32[8,8,2048]{2,1,0:T(8,128)S(1)} %fusion.1), channel_id=1, replica_groups=mesh['energy'=8,'space'=4] {'energy'}, dimensions={0} | all-to-all | bytes 1048576 | tf_op jit(solution)/shard_map/all_to_all | solution.py:82
  31.6 0.3 copy.25
  31.9 0.0 copy-start.1
  31.9 0.1 reshape_reshape.3
  32.0 0.2 copy.16
  32.2 1.3 %collective-permute-start.1 = (f32[2,4,128,128]{2,3,1,0:T(8,128)S(1)}, f32[2,4,128,128]{2,3,1,0:T(8,128)S(1)}, u32[]{:S(2)}, u32[]{:S(2)}) collective-permute-start(f32[2,4,128,128]{2,3,1,0:T(8,128)S(1)} %copy.16), channel_id=1, source_target_pairs={{1,0},{2,1},{3,2},{5,4},{6,5},{7,6},{9,8},{10,9},{11,10},{13,12},{... | collective-permute-start | bytes 1572872 | tf_op jit(solution)/shard_map/ppermute | solution.py:15
  33.5 0.0 copy-done
  33.5 1.0 %convolution_bitcast_fusion.1 = f32[2,4,128,128]{2,3,1,0:T(8,128)S(1)} fusion(f32[2,4,128,128]{3,2,1,0:T(8,128)S(1)} %reshape_reshape.3, f32[1,128,128]{2,1,0:T(8,128)S(1)} %copy-done), kind=kOutput, calls=%fused_computation.2 | convolution fusion | flops 201326592 | bytes 1114112 | tf_op jit(solution)/shard_map/dot_general | solution.py:59
  34.5 1.0 %fusion.14 = f32[2,4,128,128]{3,2,1,0:T(8,128)S(1)} fusion(f32[2,4,128,128]{2,3,1,0:T(8,128)S(1)} %convolution_bitcast_fusion.1, f32[1,128,128]{2,1,0:T(8,128)S(1)} %copy-done), kind=kOutput, calls=%fused_computation.30 | convolution fusion | flops 201326592 | bytes 1114112 | tf_op jit(solution)/shard_map/dot_general | solution.py:60
  35.5 4.6 %collective-permute-start = (f32[2,4,128,128]{3,2,1,0:T(8,128)S(1)}, f32[2,4,128,128]{3,2,1,0:T(8,128)S(1)}, u32[]{:S(2)}, u32[]{:S(2)}) collective-permute-start(f32[2,4,128,128]{3,2,1,0:T(8,128)S(1)} %fusion.14), channel_id=1, source_target_pairs={{0,1},{1,2},{2,3},{4,5},{5,6},{6,7},{8,9},{9,10},{10,11},{12,13},{... | collective-permute-start | bytes 1572872 | tf_op jit(solution)/shard_map/ppermute | solution.py:15
  40.1 0.0 copy-done.1
  40.1 1.0 %convolution_bitcast_fusion.2 = f32[2,4,128,128]{2,3,1,0:T(8,128)S(1)} fusion(f32[2,4,128,128]{3,2,1,0:T(8,128)S(1)} %reshape_reshape.3, f32[1,128,128]{2,1,0:T(8,128)S(1)} %copy-done.1), kind=kOutput, calls=%fused_computation.3 | convolution fusion | flops 201326592 | bytes 1114112 | tf_op jit(solution)/shard_map/dot_general | solution.py:59
  41.1 6.0 %collective-permute-done.1 = f32[2,4,128,128]{2,3,1,0:T(8,128)S(1)} collective-permute-done((f32[2,4,128,128]{2,3,1,0:T(8,128)S(1)}, f32[2,4,128,128]{2,3,1,0:T(8,128)S(1)}, u32[]{:S(2)}, u32[]{:S(2)}) %collective-permute-start.1) | collective-permute-done | bytes 524320 | tf_op jit(solution)/shard_map/ppermute | solution.py:15
  47.1 0.6 %convolution_bitcast_fusion = f32[2,4,128,128]{2,3,1,0:T(8,128)S(1)} fusion(f32[2,4,128,128]{2,3,1,0:T(8,128)S(1)} %collective-permute-done.1, f32[1,128,128]{2,1,0:T(8,128)S(1)} %copy-done), kind=kOutput, calls=%fused_computation.1 | convolution fusion | flops 201326592 | bytes 1114112 | tf_op jit(solution)/shard_map/dot_general | solution.py:59
  47.7 1.0 %fusion.11 = f32[2,4,128,128]{3,2,1,0:T(8,128)S(1)} fusion(f32[2,4,128,128]{2,3,1,0:T(8,128)S(1)} %convolution_bitcast_fusion, f32[1,128,128]{2,1,0:T(8,128)S(1)} %copy-done), kind=kOutput, calls=%fused_computation.27 | convolution fusion | flops 201326592 | bytes 1114112 | tf_op jit(solution)/shard_map/dot_general | solution.py:60
  48.7 1.6 %collective-permute-done = f32[2,4,128,128]{3,2,1,0:T(8,128)S(1)} collective-permute-done((f32[2,4,128,128]{3,2,1,0:T(8,128)S(1)}, f32[2,4,128,128]{3,2,1,0:T(8,128)S(1)}, u32[]{:S(2)}, u32[]{:S(2)}) %collective-permute-start) | collective-permute-done | bytes 524320 | tf_op jit(solution)/shard_map/ppermute | solution.py:15
  50.3 1.0 %fusion = f32[2,4,128,128]{3,2,1,0:T(8,128)S(1)} fusion(f32[2,4,128,128]{3,2,1,0:T(8,128)S(1)} %fusion.11, f32[2,4,128,128]{3,2,1,0:T(8,128)S(1)} %collective-permute-done, f32[2,4,128,128]{2,3,1,0:T(8,128)S(1)} %convolution_bitcast_fusion.2, f32[1,128,128]{2,1,0:T(8,128)S(1)} %copy-done.1), kind=kOutput, calls=%fused_computation.5 | convolution fusion | flops 201588736 | bytes 2162688 | tf_op jit(solution)/shard_map/dot_general | solution.py:60
  51.3 1.0 %reshape.198 = f32[1,2,4,16384]{3,2,1,0:T(4,128)} reshape(f32[2,4,128,128]{3,2,1,0:T(8,128)S(1)} %fusion) | data formatting | bytes 1048576 | tf_op jit(solution)/shard_map/reshape | solution.py:94
  (5 shorter events, 0.1 us)
Async XLA Ops:
  0.0 33.5 %copy-start = (f32[1,128,128]{2,1,0:T(8,128)S(1)}, f32[1,128,128]{2,1,0:T(8,128)}, u32[]{:S(2)}) copy-start(f32[1,128,128]{2,1,0:T(8,128)} %param.7) | copy-start | bytes 196612
  2.6 14.9 %all-to-all-start = ((bf16[8,16,2048]{2,1,0:T(8,128)(2,1)}), bf16[8,16,2048]{2,1,0:T(8,128)(2,1)S(1)}, u32[]{:S(2)}, u32[]{:S(2)}) async-start(bf16[8,16,2048]{2,1,0:T(8,128)(2,1)} %reshape.195), calls=%async_computation | async-start | bytes 1048576 | tf_op jit(solution)/shard_map/all_to_all | solution.py:78
  31.9 8.2 %copy-start.1 = (f32[1,128,128]{2,1,0:T(8,128)S(1)}, f32[1,128,128]{2,1,0:T(8,128)}, u32[]{:S(2)}) copy-start(f32[1,128,128]{2,1,0:T(8,128)} %param.6) | copy-start | bytes 196612
  32.2 14.9 %collective-permute-start.1 = (f32[2,4,128,128]{2,3,1,0:T(8,128)S(1)}, f32[2,4,128,128]{2,3,1,0:T(8,128)S(1)}, u32[]{:S(2)}, u32[]{:S(2)}) collective-permute-start(f32[2,4,128,128]{2,3,1,0:T(8,128)S(1)} %copy.16), channel_id=1, source_target_pairs={{1,0},{2,1},{3,2},{5,4},{6,5},{7,6},{9,8},{10,9},{11,10},{13,12},{... | collective-permute-start | bytes 1572872 | tf_op jit(solution)/shard_map/ppermute | solution.py:15
  35.5 14.8 %collective-permute-start = (f32[2,4,128,128]{3,2,1,0:T(8,128)S(1)}, f32[2,4,128,128]{3,2,1,0:T(8,128)S(1)}, u32[]{:S(2)}, u32[]{:S(2)}) collective-permute-start(f32[2,4,128,128]{3,2,1,0:T(8,128)S(1)} %fusion.14), channel_id=1, source_target_pairs={{0,1},{1,2},{2,3},{4,5},{5,6},{6,7},{8,9},{9,10},{10,11},{12,13},{... | collective-permute-start | bytes 1572872 | tf_op jit(solution)/shard_map/ppermute | solution.py:15

commit v4 on v2

--- a/solution.py
+++ b/solution.py
@@ -72,10 +72,12 @@
     couple_prev = shifted(couple_own, "space", 1)
     forward, inverse = tables(count, e_local, groups)
 
-    both = jnp.stack([g_lesser[0], g_greater[0]])
-    both = jnp.pad(both, ((0, 0), (0, 0), (0, 0), (0, padding)))
-    both = both.reshape(2, 2, e_local, groups, tile_width)
-    both = both.transpose(3, 0, 1, 2, 4).reshape(groups, 4 * e_local, tile_width)
+    def by_destination(part):
+        part = jnp.pad(part[0], ((0, 0), (0, 0), (0, padding)))
+        return part.reshape(2, e_local, groups, tile_width).transpose(2, 0, 1, 3)
+
+    both = jnp.concatenate([by_destination(g_lesser), by_destination(g_greater)], axis=1)
+    both, couple_prev = lax.optimization_barrier((both, couple_prev))
     got = lax.all_to_all(both, "energy", 0, 0, tiled=True)
     polar_tile = correlate(got.reshape(groups * 4 * e_local, tile_width), forward, inverse)
 
@@ -85,9 +87,9 @@
     back = back.reshape(2, e_local, groups * tile_width)[:, :, :elements]
     polar = back.reshape(2, e_local, BS, BS)
 
+    diag_block = v_diag[0]
+    polar_above = shifted(polar, "space", -1)
     polar_below = shifted(polar, "space", 1)
-    polar_above = shifted(polar, "space", -1)
-    diag_block = v_diag[0]
     local = sandwich(diag_block, polar, diag_block)
     from_below = sandwich(couple_prev.T, polar_below, couple_prev)
     from_above = sandwich(couple_own, polar_above, couple_own.T)

time: 55.6 us -> 59.1 us (1.063)
  waiting for transfers between devices: 15.9 us -> 19.5 us
  local copies, waits for them, and re-layouts: 3.34 us -> 4.97 us
  starting transfers between devices: 14.5 us -> 13.6 us
    ppermute x3, waiting for transfers between devices: 7.31 us -> 10.1 us  [shifted(): return lax.ppermute(x, axis, pairs)]
    another operation x2 -> x1, other arithmetic: 1.47 us -> 0.02 us  [the longest x1 1.45 us: per_device(): both = jnp.stack([g_lesser[0], g_greater[0]])]
    all_to_all x1, starting transfers between devices: 5.17 us -> 3.73 us  [per_device(): got = lax.all_to_all(both, 'energy', 0, 0, tiled=True)]
    reshape x2 -> x3, local copies, waits for them, and re-layouts: 1.16 us -> 2.38 us  [the longest x2 2.26 us: by_destination(): return part.reshape(2, e_local, groups, tile_width).transpose(2, 0, 1, 3)]
    concatenate x0 -> x1, other arithmetic: none -> 1.14 us  [per_device(): jnp.concatenate([by_destination(g_lesser), by_destination(g_greater)], ax...]
    all_to_all x1, waiting for transfers between devices: 8.63 us -> 9.41 us  [per_device(): got = lax.all_to_all(both, 'energy', 0, 0, tiled=True)]
  transfers between devices with their start and end apart: 4 -> 4, of which waited for: 3 -> 3; matrix products, arithmetic and copies ran while one was open for 7% -> 14% of each run, Pallas kernels for 0% -> 0%
where the time goes in v4:
time: 59.1 us; the launch traced here: 58.7 us
  waiting for transfers between devices  19.5 us (33%)
  starting transfers between devices  13.6 us (23%)
  blocking collectives  12.2 us (21%)
  matrix products  6.16 us (10%)
  local copies, waits for them, and re-layouts  4.97 us (8%)
  other arithmetic  2.12 us (4%)
    all_to_all x1, blocking collectives, per_device(): back = lax.all_to_all(send, 'energy', 0, 0, tiled=True)  12.2 us
    ppermute x3, waiting for transfers between devices, shifted(): return lax.ppermute(x, axis, pairs)  10.1 us
    ppermute x3, starting transfers between devices, shifted(): return lax.ppermute(x, axis, pairs)  9.86 us
    all_to_all x1, waiting for transfers between devices, per_device(): got = lax.all_to_all(both, 'energy', 0, 0, tiled=True)  9.41 us
    all_to_all x1, starting transfers between devices, per_device(): got = lax.all_to_all(both, 'energy', 0, 0, tiled=True)  3.73 us
    dot_general x3, matrix products, sandwich(): return jnp.matmul(inner, right, precision=lax.Precision.HIGHEST)  2.56 us
    reshape x2, local copies, waits for them, and re-layouts, by_destination(): return part.reshape(2, e_local, groups, tile_width).transpose(2, 0, 1, 3)  2.26 us
    dot_general x3, matrix products, sandwich(): inner = jnp.matmul(left, field, precision=lax.Precision.HIGHEST)  2.2 us
  transfers between devices with their start and end apart: 4, of which 3 were waited for; matrix products, arithmetic and copies ran while one was open for 14% of the time, Pallas kernels for 0%

profile of v4, /device:TPU:0, one launch (start us, length us, event | category | flops | bytes accessed | tf_op | source)
XLA Modules:
  0.0 58.7 jit_solution(12275922973672896356)
XLA Ops:
  0.0 0.0 copy-start
  0.0 5.1 %collective-permute-start = (f32[128,128]{1,0:T(8,128)}, f32[128,128]{1,0:T(8,128)S(1)}, u32[]{:S(2)}, u32[]{:S(2)}) collective-permute-start(f32[128,128]{1,0:T(8,128)} %bitcast.68), channel_id=1, source_target_pairs={{0,1},{1,2},{2,3},{4,5},{5,6},{6,7},{8,9},{9,10},{10,11},{12,13},{... | collective-permute-start | bytes 196616 | tf_op jit(solution)/shard_map/ppermute | solution.py:15
  5.1 0.2 fusion.24
  5.2 0.1 copy.9
  5.3 1.1 %reshape.196 = bf16[2,4,8,2048]{3,2,1,0:T(8,128)(2,1)S(1)} reshape(bf16[1,2,4,16384]{3,2,1,0:T(4,128)(2,1)} %param.4) | data formatting | bytes 524288 | tf_op jit(solution)/shard_map/reshape | solution.py:77
  6.5 1.1 %reshape.197 = bf16[2,4,8,2048]{3,2,1,0:T(8,128)(2,1)S(1)} reshape(bf16[1,2,4,16384]{3,2,1,0:T(4,128)(2,1)} %param.5) | data formatting | bytes 524288 | tf_op jit(solution)/shard_map/reshape | solution.py:77
  7.6 0.4 copy_bitcast_fusion
  8.0 1.1 %pad_maximum_fusion = bf16[8,4,4,2048]{3,2,1,0:T(4,128)(2,1)} fusion(bf16[8,2,4,2048]{3,2,1,0:T(4,128)(2,1)S(1)} %get-tuple-element.21, bf16[8,2,4,2048]{3,2,1,0:T(4,128)(2,1)S(1)} %get-tuple-element.22), kind=kLoop, calls=%fused_computation.10 | loop fusion | flops 262144 | bytes 1048576 | tf_op jit(solution)/shard_map/concatenate | solution.py:79
  9.2 0.2 copy.10
  9.4 0.3 reshape.195
  9.7 0.0 collective-permute-done
  9.7 3.7 %all-to-all-start = ((bf16[8,4,4,2048]{3,2,1,0:T(4,128)(2,1)}), bf16[8,4,4,2048]{3,2,1,0:T(4,128)(2,1)S(1)}, u32[]{:S(2)}, u32[]{:S(2)}) async-start(bf16[8,4,4,2048]{3,2,1,0:T(4,128)(2,1)} %pad_maximum_fusion), calls=%async_computation | async-start | bytes 1048576 | tf_op jit(solution)/shard_map/all_to_all | solution.py:81
  13.4 0.2 fusion.27
  13.6 0.1 maximum_maximum_fusion
  13.7 9.4 %all-to-all-done = bf16[8,4,4,2048]{3,2,1,0:T(4,128)(2,1)S(1)} async-done(((bf16[8,4,4,2048]{3,2,1,0:T(4,128)(2,1)}), bf16[8,4,4,2048]{3,2,1,0:T(4,128)(2,1)S(1)}, u32[]{:S(2)}, u32[]{:S(2)}) %all-to-all-start) | async-done | bytes 524320 | tf_op jit(solution)/shard_map/all_to_all | solution.py:81
  23.1 0.1 reshape.198
  23.3 0.7 %fusion.4 = f32[512,2048]{1,0:T(8,128)S(1)} fusion(bf16[128,2048]{1,0:T(8,128)(2,1)S(1)} %reshape.198, bf16[256,128]{0,1:T(8,128)(2,1)S(1)} %get-tuple-element.12, bf16[256,128]{0,1:T(8,128)(2,1)S(1)} %get-tuple-element.11), kind=kOutput, calls=%fused_computation.19 | convolution fusion | flops 268697600 | bytes 4849664 | tf_op jit(solution)/shard_map/dot_general | solution.py:47
  24.0 0.3 slice_add_fusion
  24.3 0.1 multiply_add_fusion
  24.5 0.7 %fusion = f32[8,8,2048]{2,1,0:T(8,128)S(1)} fusion(f32[8,8,128]{2,1,0:T(8,128)S(1)} %bitcast.69, f32[64,2048]{1,0:T(8,128)S(1)} %get-tuple-element.10, f32[64,2048]{1,0:T(8,128)S(1)} %get-tuple-element.9), kind=kOutput, calls=%fused_computation.7 | convolution fusion | flops 201588736 | bytes 1605632 | tf_op jit(solution)/shard_map/dot_general | solution.py:55
  25.2 12.2 %all_to_all.10 = f32[8,8,2048]{2,1,0:T(8,128)S(1)} all-to-all(f32[8,8,2048]{2,1,0:T(8,128)S(1)} %fusion), channel_id=1, replica_groups=mesh['energy'=8,'space'=4] {'energy'}, dimensions={0} | all-to-all | bytes 1048576 | tf_op jit(solution)/shard_map/all_to_all | solution.py:85
  37.3 0.3 copy.26
  37.6 0.1 reshape_reshape.3
  37.7 3.5 %collective-permute-start.1 = (f32[2,4,128,128]{3,2,1,0:T(8,128)S(1)}, f32[2,4,128,128]{3,2,1,0:T(8,128)S(1)}, u32[]{:S(2)}, u32[]{:S(2)}) collective-permute-start(f32[2,4,128,128]{3,2,1,0:T(8,128)S(1)} %reshape_reshape.3), channel_id=1, source_target_pairs={{0,1},{1,2},{2,3},{4,5},{5,6},{6,7},{8,9},{9,10},{10,11},{12,13},{... | collective-permute-start | bytes 1572872 | tf_op jit(solution)/shard_map/ppermute | solution.py:15
  41.2 0.2 copy.17
  41.5 1.3 %collective-permute-start.2 = (f32[2,4,128,128]{2,3,1,0:T(8,128)S(1)}, f32[2,4,128,128]{2,3,1,0:T(8,128)S(1)}, u32[]{:S(2)}, u32[]{:S(2)}) collective-permute-start(f32[2,4,128,128]{2,3,1,0:T(8,128)S(1)} %copy.17), channel_id=1, source_target_pairs={{1,0},{2,1},{3,2},{5,4},{6,5},{7,6},{9,8},{10,9},{11,10},{13,12},{... | collective-permute-start | bytes 1572872 | tf_op jit(solution)/shard_map/ppermute | solution.py:15
  42.8 0.0 copy-done
  42.8 1.0 %convolution_bitcast_fusion.2 = f32[2,4,128,128]{2,3,1,0:T(8,128)S(1)} fusion(f32[2,4,128,128]{3,2,1,0:T(8,128)S(1)} %reshape_reshape.3, f32[1,128,128]{2,1,0:T(8,128)S(1)} %copy-done), kind=kOutput, calls=%fused_computation.3 | convolution fusion | flops 201326592 | bytes 1114112 | tf_op jit(solution)/shard_map/dot_general | solution.py:59
  43.8 0.0 copy-start.1
  43.8 1.0 %fusion.10 = f32[2,4,128,128]{3,2,1,0:T(8,128)S(1)} fusion(f32[2,4,128,128]{2,3,1,0:T(8,128)S(1)} %convolution_bitcast_fusion.2, f32[1,128,128]{2,1,0:T(8,128)S(1)} %copy-done), kind=kOutput, calls=%fused_computation.28 | convolution fusion | flops 201326592 | bytes 1114112 | tf_op jit(solution)/shard_map/dot_general | solution.py:60
  44.8 7.0 %collective-permute-done.1 = f32[2,4,128,128]{3,2,1,0:T(8,128)S(1)} collective-permute-done((f32[2,4,128,128]{3,2,1,0:T(8,128)S(1)}, f32[2,4,128,128]{3,2,1,0:T(8,128)S(1)}, u32[]{:S(2)}, u32[]{:S(2)}) %collective-permute-start.1) | collective-permute-done | bytes 524320 | tf_op jit(solution)/shard_map/ppermute | solution.py:15
  51.7 0.6 %convolution_bitcast_fusion.1 = f32[2,4,128,128]{3,2,1,0:T(8,128)S(1)} fusion(f32[2,4,128,128]{3,2,1,0:T(8,128)S(1)} %collective-permute-done.1, f32[128,128]{1,0:T(8,128)S(1)} %collective-permute-done), kind=kOutput, calls=%fused_computation.2 | convolution fusion | flops 201326592 | bytes 1114112 | tf_op jit(solution)/shard_map/dot_general | solution.py:59
  52.4 0.6 convolution_add_fusion.1
  52.9 3.1 %collective-permute-done.2 = f32[2,4,128,128]{2,3,1,0:T(8,128)S(1)} collective-permute-done((f32[2,4,128,128]{2,3,1,0:T(8,128)S(1)}, f32[2,4,128,128]{2,3,1,0:T(8,128)S(1)}, u32[]{:S(2)}, u32[]{:S(2)}) %collective-permute-start.2) | collective-permute-done | bytes 524320 | tf_op jit(solution)/shard_map/ppermute | solution.py:15
  56.1 0.0 copy-done.1
  56.1 0.6 convolution_bitcast_fusion
  56.7 1.0 %convolution_add_fusion = f32[2,4,128,128]{3,2,1,0:T(8,128)S(1)} fusion(f32[2,4,128,128]{3,2,1,0:T(8,128)S(1)} %convolution_add_fusion.1, f32[2,4,128,128]{2,3,1,0:T(8,128)S(1)} %convolution_bitcast_fusion, f32[1,128,128]{2,1,0:T(8,128)S(1)} %copy-done.1), kind=kOutput, calls=%fused_computation.4 | convolution fusion | flops 201457664 | bytes 1638400 | tf_op jit(solution)/shard_map/dot_general | solution.py:60
  57.7 1.0 %reshape.200 = f32[1,2,4,16384]{3,2,1,0:T(4,128)} reshape(f32[2,4,128,128]{3,2,1,0:T(8,128)S(1)} %convolution_add_fusion) | data formatting | bytes 1048576 | tf_op jit(solution)/shard_map/reshape | solution.py:97
  (5 shorter events, 0.1 us)
Async XLA Ops:
  0.0 42.8 %copy-start = (f32[1,128,128]{2,1,0:T(8,128)S(1)}, f32[1,128,128]{2,1,0:T(8,128)}, u32[]{:S(2)}) copy-start(f32[1,128,128]{2,1,0:T(8,128)} %param.6) | copy-start | bytes 196612
  0.0 9.7 %collective-permute-start = (f32[128,128]{1,0:T(8,128)}, f32[128,128]{1,0:T(8,128)S(1)}, u32[]{:S(2)}, u32[]{:S(2)}) collective-permute-start(f32[128,128]{1,0:T(8,128)} %bitcast.68), channel_id=1, source_target_pairs={{0,1},{1,2},{2,3},{4,5},{5,6},{6,7},{8,9},{9,10},{10,11},{12,13},{... | collective-permute-start | bytes 196616 | tf_op jit(solution)/shard_map/ppermute | solution.py:15
  9.7 13.5 %all-to-all-start = ((bf16[8,4,4,2048]{3,2,1,0:T(4,128)(2,1)}), bf16[8,4,4,2048]{3,2,1,0:T(4,128)(2,1)S(1)}, u32[]{:S(2)}, u32[]{:S(2)}) async-start(bf16[8,4,4,2048]{3,2,1,0:T(4,128)(2,1)} %pad_maximum_fusion), calls=%async_computation | async-start | bytes 1048576 | tf_op jit(solution)/shard_map/all_to_all | solution.py:81
  37.7 14.0 %collective-permute-start.1 = (f32[2,4,128,128]{3,2,1,0:T(8,128)S(1)}, f32[2,4,128,128]{3,2,1,0:T(8,128)S(1)}, u32[]{:S(2)}, u32[]{:S(2)}) collective-permute-start(f32[2,4,128,128]{3,2,1,0:T(8,128)S(1)} %reshape_reshape.3), channel_id=1, source_target_pairs={{0,1},{1,2},{2,3},{4,5},{5,6},{6,7},{8,9},{9,10},{10,11},{12,13},{... | collective-permute-start | bytes 1572872 | tf_op jit(solution)/shard_map/ppermute | solution.py:15
  41.5 14.6 %collective-permute-start.2 = (f32[2,4,128,128]{2,3,1,0:T(8,128)S(1)}, f32[2,4,128,128]{2,3,1,0:T(8,128)S(1)}, u32[]{:S(2)}, u32[]{:S(2)}) collective-permute-start(f32[2,4,128,128]{2,3,1,0:T(8,128)S(1)} %copy.17), channel_id=1, source_target_pairs={{1,0},{2,1},{3,2},{5,4},{6,5},{7,6},{9,8},{10,9},{11,10},{13,12},{... | collective-permute-start | bytes 1572872 | tf_op jit(solution)/shard_map/ppermute | solution.py:15
  43.8 12.3 %copy-start.1 = (f32[1,128,128]{2,1,0:T(8,128)S(1)}, f32[1,128,128]{2,1,0:T(8,128)}, u32[]{:S(2)}) copy-start(f32[1,128,128]{2,1,0:T(8,128)} %param.7) | copy-start | bytes 196612

commit v5 on v3

--- a/solution.py
+++ b/solution.py
@@ -56,8 +56,8 @@
 
 
 def sandwich(left, field, right):
-    inner = jnp.matmul(left, field, precision=lax.Precision.HIGHEST)
-    return jnp.matmul(inner, right, precision=lax.Precision.HIGHEST)
+    inner = jnp.matmul(left, field, precision=lax.Precision.HIGH)
+    return jnp.matmul(inner, right, precision=lax.Precision.HIGH)
 
 
 def per_device(g_lesser, g_greater, v_diag, v_couple):
@@ -90,8 +90,9 @@
     from_below = shifted(to_next, "space", 1)
     local = sandwich(diag_block, polar, diag_block)
     from_above = sandwich(couple_own, polar_above, couple_own.T)
-    total = local + from_below + from_above
-    return total.reshape(1, 2, e_local, elements)
+    local, from_below, from_above = lax.optimization_barrier((local, from_below, from_above))
+    shape = (1, 2, e_local, elements)
+    return local.reshape(shape) + from_below.reshape(shape) + from_above.reshape(shape)
 
 
 def solution(mesh):

time: 52.7 us -> 50.9 us (0.966)
  matrix products: 6.96 us -> 4.73 us
    dot_general x6, matrix products: 5.55 us -> 3.32 us  [the longest x3 1.77 us: sandwich(): return jnp.matmul(inner, right, precision=lax.Precision.HIGH)]
    reshape x1 -> x0, local copies, waits for them, and re-layouts: 1.02 us -> none  [per_device(): return total.reshape(1, 2, e_local, elements)]
    add x0 -> x1, local copies, waits for them, and re-layouts: none -> 1.02 us  [per_device(): local.reshape(shape) + from_below.reshape(shape) + from_above.reshape(shape)]
  transfers between devices with their start and end apart: 3 -> 3, of which waited for: 3 -> 3; matrix products, arithmetic and copies ran while one was open for 11% -> 9% of each run, Pallas kernels for 0% -> 0%
where the time goes in v5:
time: 50.9 us; the launch traced here: 50.6 us
  waiting for transfers between devices  16.6 us (33%)
  blocking collectives  12.2 us (24%)
  starting transfers between devices  11 us (22%)
  matrix products  4.73 us (9%)
  local copies, waits for them, and re-layouts  3.34 us (7%)
  other arithmetic  2.52 us (5%)
    all_to_all x1, blocking collectives, per_device(): back = lax.all_to_all(send, 'energy', 0, 0, tiled=True)  12.2 us
    all_to_all x1, waiting for transfers between devices, per_device(): got = lax.all_to_all(both, 'energy', 0, 0, tiled=True)  8.63 us
    ppermute x2, waiting for transfers between devices, shifted(): return lax.ppermute(x, axis, pairs)  8.01 us
    ppermute x2, starting transfers between devices, shifted(): return lax.ppermute(x, axis, pairs)  5.87 us
    all_to_all x1, starting transfers between devices, per_device(): got = lax.all_to_all(both, 'energy', 0, 0, tiled=True)  5.17 us
    dot_general x3, matrix products, sandwich(): return jnp.matmul(inner, right, precision=lax.Precision.HIGH)  1.77 us
    dot_general x3, matrix products, sandwich(): inner = jnp.matmul(left, field, precision=lax.Precision.HIGH)  1.55 us
    another operation x1, other arithmetic, per_device(): both = jnp.stack([g_lesser[0], g_greater[0]])  1.45 us
  transfers between devices with their start and end apart: 3, of which 3 were waited for; matrix products, arithmetic and copies ran while one was open for 9% of the time, Pallas kernels for 0%

profile of v5, /device:TPU:0, one launch (start us, length us, event | category | flops | bytes accessed | tf_op | source)
XLA Modules:
  0.0 50.6 jit_solution(6683742405982035790)
XLA Ops:
  0.0 0.0 copy-start
  0.0 1.5 %pad_maximum_fusion = bf16[2,2,4,16384]{3,2,1,0:T(4,128)(2,1)S(1)} fusion(bf16[1,2,4,16384]{3,2,1,0:T(4,128)(2,1)} %param.5, bf16[1,2,4,16384]{3,2,1,0:T(4,128)(2,1)} %param.4), kind=kLoop, calls=%fused_computation.9 | loop fusion | flops 262144 | bytes 1048576 | tf_op jit(solution)/shard_map/stack | solution.py:74
  1.5 0.2 copy.28
  1.7 0.9 %reshape.229 = bf16[8,16,2048]{2,1,0:T(8,128)(2,1)} reshape(bf16[8,2,2,4,2048]{4,3,2,1,0:T(4,128)(2,1)S(1)} %bitcast.68) | data formatting | bytes 1048576 | tf_op jit(solution)/shard_map/reshape | solution.py:77
  2.6 5.2 %all-to-all-start = ((bf16[8,16,2048]{2,1,0:T(8,128)(2,1)}), bf16[8,16,2048]{2,1,0:T(8,128)(2,1)S(1)}, u32[]{:S(2)}, u32[]{:S(2)}) async-start(bf16[8,16,2048]{2,1,0:T(8,128)(2,1)} %reshape.229), calls=%async_computation | async-start | bytes 1048576 | tf_op jit(solution)/shard_map/all_to_all | solution.py:78
  7.8 0.2 fusion.26
  8.0 0.1 copy.8
  8.1 0.2 copy.9
  8.3 0.3 reshape.227
  8.6 0.2 fusion.29
  8.8 0.1 maximum_maximum_fusion
  8.9 8.6 %all-to-all-done = bf16[8,16,2048]{2,1,0:T(8,128)(2,1)S(1)} async-done(((bf16[8,16,2048]{2,1,0:T(8,128)(2,1)}), bf16[8,16,2048]{2,1,0:T(8,128)(2,1)S(1)}, u32[]{:S(2)}, u32[]{:S(2)}) %all-to-all-start) | async-done | bytes 524320 | tf_op jit(solution)/shard_map/all_to_all | solution.py:78
  17.5 0.7 %fusion.4 = f32[512,2048]{1,0:T(8,128)S(1)} fusion(bf16[128,2048]{1,0:T(8,128)(2,1)S(1)} %bitcast.67, bf16[256,128]{0,1:T(8,128)(2,1)S(1)} %get-tuple-element.14, bf16[256,128]{0,1:T(8,128)(2,1)S(1)} %get-tuple-element.13), kind=kOutput, calls=%fused_computation.17 | convolution fusion | flops 268697600 | bytes 4849664 | tf_op jit(solution)/shard_map/dot_general | solution.py:47
  18.3 0.3 slice_add_fusion
  18.6 0.1 multiply_add_fusion
  18.8 0.7 %fusion = f32[8,8,2048]{2,1,0:T(8,128)S(1)} fusion(f32[8,8,128]{2,1,0:T(8,128)S(1)} %bitcast.71, f32[64,2048]{1,0:T(8,128)S(1)} %get-tuple-element.12, f32[64,2048]{1,0:T(8,128)S(1)} %get-tuple-element.11), kind=kOutput, calls=%fused_computation.5 | convolution fusion | flops 201588736 | bytes 1605632 | tf_op jit(solution)/shard_map/dot_general | solution.py:55
  19.4 12.2 %all_to_all.10 = f32[8,8,2048]{2,1,0:T(8,128)S(1)} all-to-all(f32[8,8,2048]{2,1,0:T(8,128)S(1)} %fusion), channel_id=1, replica_groups=mesh['energy'=8,'space'=4] {'energy'}, dimensions={0} | all-to-all | bytes 1048576 | tf_op jit(solution)/shard_map/all_to_all | solution.py:82
  31.6 0.3 copy.25
  31.9 0.0 copy-start.1
  31.9 0.1 reshape_reshape.3
  32.0 0.2 copy.16
  32.2 1.3 %collective-permute-start.1 = (f32[2,4,128,128]{2,3,1,0:T(8,128)S(1)}, f32[2,4,128,128]{2,3,1,0:T(8,128)S(1)}, u32[]{:S(2)}, u32[]{:S(2)}) collective-permute-start(f32[2,4,128,128]{2,3,1,0:T(8,128)S(1)} %copy.16), channel_id=1, source_target_pairs={{1,0},{2,1},{3,2},{5,4},{6,5},{7,6},{9,8},{10,9},{11,10},{13,12},{... | collective-permute-start | bytes 1572872 | tf_op jit(solution)/shard_map/ppermute | solution.py:15
  33.5 0.0 copy-done
  33.5 0.6 %convolution_bitcast_fusion.1 = f32[2,4,128,128]{2,3,1,0:T(8,128)S(1)} fusion(f32[2,4,128,128]{3,2,1,0:T(8,128)S(1)} %reshape_reshape.3, f32[1,128,128]{2,1,0:T(8,128)S(1)} %copy-done), kind=kOutput, calls=%fused_computation.2 | convolution fusion | flops 100663296 | bytes 1114112 | tf_op jit(solution)/shard_map/dot_general | solution.py:59
  34.1 0.6 %fusion.14 = f32[2,4,128,128]{3,2,1,0:T(8,128)S(1)} fusion(f32[2,4,128,128]{2,3,1,0:T(8,128)S(1)} %convolution_bitcast_fusion.1, f32[1,128,128]{2,1,0:T(8,128)S(1)} %copy-done), kind=kOutput, calls=%fused_computation.30 | convolution fusion | flops 100663296 | bytes 1114112 | tf_op jit(solution)/shard_map/dot_general | solution.py:60
  34.7 4.6 %collective-permute-start = (f32[2,4,128,128]{3,2,1,0:T(8,128)S(1)}, f32[2,4,128,128]{3,2,1,0:T(8,128)S(1)}, u32[]{:S(2)}, u32[]{:S(2)}) collective-permute-start(f32[2,4,128,128]{3,2,1,0:T(8,128)S(1)} %fusion.14), channel_id=1, source_target_pairs={{0,1},{1,2},{2,3},{4,5},{5,6},{6,7},{8,9},{9,10},{10,11},{12,13},{... | collective-permute-start | bytes 1572872 | tf_op jit(solution)/shard_map/ppermute | solution.py:15
  39.3 0.0 copy-done.1
  39.3 0.6 %convolution_bitcast_fusion.2 = f32[2,4,128,128]{2,3,1,0:T(8,128)S(1)} fusion(f32[2,4,128,128]{3,2,1,0:T(8,128)S(1)} %reshape_reshape.3, f32[1,128,128]{2,1,0:T(8,128)S(1)} %copy-done.1), kind=kOutput, calls=%fused_computation.3 | convolution fusion | flops 100663296 | bytes 1114112 | tf_op jit(solution)/shard_map/dot_general | solution.py:59
  39.9 0.6 %fusion.8 = f32[2,4,128,128]{3,2,1,0:T(8,128)S(1)} fusion(f32[2,4,128,128]{2,3,1,0:T(8,128)S(1)} %convolution_bitcast_fusion.2, f32[1,128,128]{2,1,0:T(8,128)S(1)} %copy-done.1), kind=kOutput, calls=%fused_computation.24 | convolution fusion | flops 100663296 | bytes 1114112 | tf_op jit(solution)/shard_map/dot_general | solution.py:60
  40.5 6.6 %collective-permute-done.1 = f32[2,4,128,128]{2,3,1,0:T(8,128)S(1)} collective-permute-done((f32[2,4,128,128]{2,3,1,0:T(8,128)S(1)}, f32[2,4,128,128]{2,3,1,0:T(8,128)S(1)}, u32[]{:S(2)}, u32[]{:S(2)}) %collective-permute-start.1) | collective-permute-done | bytes 524320 | tf_op jit(solution)/shard_map/ppermute | solution.py:15
  47.1 0.4 convolution_bitcast_fusion
  47.5 0.6 %fusion.11 = f32[2,4,128,128]{3,2,1,0:T(8,128)S(1)} fusion(f32[2,4,128,128]{2,3,1,0:T(8,128)S(1)} %convolution_bitcast_fusion, f32[1,128,128]{2,1,0:T(8,128)S(1)} %copy-done), kind=kOutput, calls=%fused_computation.27 | convolution fusion | flops 100663296 | bytes 1114112 | tf_op jit(solution)/shard_map/dot_general | solution.py:60
  48.1 1.4 %collective-permute-done = f32[2,4,128,128]{3,2,1,0:T(8,128)S(1)} collective-permute-done((f32[2,4,128,128]{3,2,1,0:T(8,128)S(1)}, f32[2,4,128,128]{3,2,1,0:T(8,128)S(1)}, u32[]{:S(2)}, u32[]{:S(2)}) %collective-permute-start) | collective-permute-done | bytes 524320 | tf_op jit(solution)/shard_map/ppermute | solution.py:15
  49.5 0.1 add_add_fusion
  49.6 1.0 %add.106 = f32[1,2,4,16384]{3,2,1,0:T(4,128)} reshape(f32[2,4,128,128]{3,2,1,0:T(8,128)S(1)} %add_add_fusion) | data formatting | bytes 1048576 | tf_op jit(solution)/shard_map/add | solution.py:95
  (5 shorter events, 0.1 us)
Async XLA Ops:
  0.0 33.5 %copy-start = (f32[1,128,128]{2,1,0:T(8,128)S(1)}, f32[1,128,128]{2,1,0:T(8,128)}, u32[]{:S(2)}) copy-start(f32[1,128,128]{2,1,0:T(8,128)} %param.7) | copy-start | bytes 196612
  2.6 14.9 %all-to-all-start = ((bf16[8,16,2048]{2,1,0:T(8,128)(2,1)}), bf16[8,16,2048]{2,1,0:T(8,128)(2,1)S(1)}, u32[]{:S(2)}, u32[]{:S(2)}) async-start(bf16[8,16,2048]{2,1,0:T(8,128)(2,1)} %reshape.229), calls=%async_computation | async-start | bytes 1048576 | tf_op jit(solution)/shard_map/all_to_all | solution.py:78
  31.9 7.4 %copy-start.1 = (f32[1,128,128]{2,1,0:T(8,128)S(1)}, f32[1,128,128]{2,1,0:T(8,128)}, u32[]{:S(2)}) copy-start(f32[1,128,128]{2,1,0:T(8,128)} %param.6) | copy-start | bytes 196612
  32.2 14.9 %collective-permute-start.1 = (f32[2,4,128,128]{2,3,1,0:T(8,128)S(1)}, f32[2,4,128,128]{2,3,1,0:T(8,128)S(1)}, u32[]{:S(2)}, u32[]{:S(2)}) collective-permute-start(f32[2,4,128,128]{2,3,1,0:T(8,128)S(1)} %copy.16), channel_id=1, source_target_pairs={{1,0},{2,1},{3,2},{5,4},{6,5},{7,6},{9,8},{10,9},{11,10},{13,12},{... | collective-permute-start | bytes 1572872 | tf_op jit(solution)/shard_map/ppermute | solution.py:15
  34.7 14.8 %collective-permute-start = (f32[2,4,128,128]{3,2,1,0:T(8,128)S(1)}, f32[2,4,128,128]{3,2,1,0:T(8,128)S(1)}, u32[]{:S(2)}, u32[]{:S(2)}) collective-permute-start(f32[2,4,128,128]{3,2,1,0:T(8,128)S(1)} %fusion.14), channel_id=1, source_target_pairs={{0,1},{1,2},{2,3},{4,5},{5,6},{6,7},{8,9},{9,10},{10,11},{12,13},{... | collective-permute-start | bytes 1572872 | tf_op jit(solution)/shard_map/ppermute | solution.py:15

commit v6 on v5

--- a/solution.py
+++ b/solution.py
@@ -43,16 +43,14 @@
 def correlate(got, forward, inverse):
     high = lax.reduce_precision(forward, exponent_bits=8, mantissa_bits=7)
     low = forward - high
-    split = jnp.concatenate([high, low]).astype(jnp.bfloat16)
-    both = jnp.dot(split, got, preferred_element_type=jnp.float32)
-    rows = forward.shape[0]
-    spectrum = both[:rows] + both[rows:]
-    length = rows // 4
+    spectrum = jnp.dot(high.astype(jnp.bfloat16), got, preferred_element_type=jnp.float32)
+    spectrum = spectrum + jnp.dot(low.astype(jnp.bfloat16), got, preferred_element_type=jnp.float32)
+    length = forward.shape[0] // 4
     l_re, l_im, g_re, g_im = (spectrum[i * length:(i + 1) * length] for i in range(4))
     z_re = l_re * g_re + l_im * g_im
     z_im = l_im * g_re - l_re * g_im
     z = jnp.concatenate([z_re, z_im])
-    return jnp.dot(inverse, z, precision=lax.Precision.HIGHEST, preferred_element_type=jnp.float32)
+    return jnp.dot(inverse, z, precision=lax.Precision.HIGH, preferred_element_type=jnp.float32)
 
 
 def sandwich(left, field, right):

time: 50.9 us -> 50.5 us (level)
    convert_element_type x0 -> x4, local copies, waits for them, and re-layouts: none -> 0.57 us  [the longest x2 0.28 us: correlate(): high.astype(jnp.bfloat16)]
    dot_general x2 -> x3, matrix products: 1.4 us -> 1.3 us  [the longest x1 0.46 us: correlate(): jnp.dot(low.astype(jnp.bfloat16), got, preferred_element_type=jnp.float32)]
where the time goes in v6:
time: 50.5 us; the launch traced here: 50.2 us
  waiting for transfers between devices  16.5 us (33%)
  blocking collectives  12.2 us (24%)
  starting transfers between devices  11 us (22%)
  matrix products  4.63 us (9%)
  local copies, waits for them, and re-layouts  3.45 us (7%)
  other arithmetic  2.2 us (4%)
    all_to_all x1, blocking collectives, per_device(): back = lax.all_to_all(send, 'energy', 0, 0, tiled=True)  12.2 us
    all_to_all x1, waiting for transfers between devices, per_device(): got = lax.all_to_all(both, 'energy', 0, 0, tiled=True)  8.5 us
    ppermute x2, waiting for transfers between devices, shifted(): return lax.ppermute(x, axis, pairs)  8.01 us
    ppermute x2, starting transfers between devices, shifted(): return lax.ppermute(x, axis, pairs)  5.87 us
    all_to_all x1, starting transfers between devices, per_device(): got = lax.all_to_all(both, 'energy', 0, 0, tiled=True)  5.17 us
    dot_general x3, matrix products, sandwich(): return jnp.matmul(inner, right, precision=lax.Precision.HIGH)  1.77 us
    dot_general x3, matrix products, sandwich(): inner = jnp.matmul(left, field, precision=lax.Precision.HIGH)  1.55 us
    another operation x1, other arithmetic, per_device(): both = jnp.stack([g_lesser[0], g_greater[0]])  1.45 us
  transfers between devices with their start and end apart: 3, of which 3 were waited for; matrix products, arithmetic and copies ran while one was open for 9% of the time, Pallas kernels for 0%

profile of v6, /device:TPU:0, one launch (start us, length us, event | category | flops | bytes accessed | tf_op | source)
XLA Modules:
  0.0 50.2 jit_solution(2612742561584490090)
XLA Ops:
  0.0 0.0 copy-start
  0.0 1.5 %pad_maximum_fusion = bf16[2,2,4,16384]{3,2,1,0:T(4,128)(2,1)S(1)} fusion(bf16[1,2,4,16384]{3,2,1,0:T(4,128)(2,1)} %param.5, bf16[1,2,4,16384]{3,2,1,0:T(4,128)(2,1)} %param.4), kind=kLoop, calls=%fused_computation.9 | loop fusion | flops 262144 | bytes 1048576 | tf_op jit(solution)/shard_map/stack | solution.py:72
  1.5 0.2 copy.29
  1.7 0.9 %reshape.240 = bf16[8,16,2048]{2,1,0:T(8,128)(2,1)} reshape(bf16[8,2,2,4,2048]{4,3,2,1,0:T(4,128)(2,1)S(1)} %bitcast.74) | data formatting | bytes 1048576 | tf_op jit(solution)/shard_map/reshape | solution.py:75
  2.6 5.2 %all-to-all-start = ((bf16[8,16,2048]{2,1,0:T(8,128)(2,1)}), bf16[8,16,2048]{2,1,0:T(8,128)(2,1)S(1)}, u32[]{:S(2)}, u32[]{:S(2)}) async-start(bf16[8,16,2048]{2,1,0:T(8,128)(2,1)} %reshape.240), calls=%async_computation | async-start | bytes 1048576 | tf_op jit(solution)/shard_map/all_to_all | solution.py:76
  7.8 0.2 fusion.22
  8.0 0.1 copy.8
  8.1 0.1 copy.9
  8.3 0.1 convert_element_type.77
  8.4 0.1 copy.11
  8.6 0.1 convert_element_type.79
  8.7 0.2 fusion.25
  8.9 0.1 maximum_maximum_fusion
  9.0 8.5 %all-to-all-done = bf16[8,16,2048]{2,1,0:T(8,128)(2,1)S(1)} async-done(((bf16[8,16,2048]{2,1,0:T(8,128)(2,1)}), bf16[8,16,2048]{2,1,0:T(8,128)(2,1)S(1)}, u32[]{:S(2)}, u32[]{:S(2)}) %all-to-all-start) | async-done | bytes 524320 | tf_op jit(solution)/shard_map/all_to_all | solution.py:76
  17.5 0.4 fusion.27
  18.0 0.5 convolution_add_fusion
  18.5 0.1 multiply_add_fusion
  18.6 0.4 fusion
  19.0 12.2 %all_to_all.10 = f32[8,8,2048]{2,1,0:T(8,128)S(1)} all-to-all(f32[8,8,2048]{2,1,0:T(8,128)S(1)} %fusion), channel_id=1, replica_groups=mesh['energy'=8,'space'=4] {'energy'}, dimensions={0} | all-to-all | bytes 1048576 | tf_op jit(solution)/shard_map/all_to_all | solution.py:80
  31.2 0.3 copy.26
  31.5 0.0 copy-start.1
  31.5 0.1 reshape_reshape.3
  31.6 0.2 copy.17
  31.8 1.3 %collective-permute-start.1 = (f32[2,4,128,128]{2,3,1,0:T(8,128)S(1)}, f32[2,4,128,128]{2,3,1,0:T(8,128)S(1)}, u32[]{:S(2)}, u32[]{:S(2)}) collective-permute-start(f32[2,4,128,128]{2,3,1,0:T(8,128)S(1)} %copy.17), channel_id=1, source_target_pairs={{1,0},{2,1},{3,2},{5,4},{6,5},{7,6},{9,8},{10,9},{11,10},{13,12},{... | collective-permute-start | bytes 1572872 | tf_op jit(solution)/shard_map/ppermute | solution.py:15
  33.1 0.0 copy-done
  33.1 0.6 %convolution_bitcast_fusion.1 = f32[2,4,128,128]{2,3,1,0:T(8,128)S(1)} fusion(f32[2,4,128,128]{3,2,1,0:T(8,128)S(1)} %reshape_reshape.3, f32[1,128,128]{2,1,0:T(8,128)S(1)} %copy-done), kind=kOutput, calls=%fused_computation.2 | convolution fusion | flops 100663296 | bytes 1114112 | tf_op jit(solution)/shard_map/dot_general | solution.py:57
  33.7 0.6 %fusion.10 = f32[2,4,128,128]{3,2,1,0:T(8,128)S(1)} fusion(f32[2,4,128,128]{2,3,1,0:T(8,128)S(1)} %convolution_bitcast_fusion.1, f32[1,128,128]{2,1,0:T(8,128)S(1)} %copy-done), kind=kOutput, calls=%fused_computation.26 | convolution fusion | flops 100663296 | bytes 1114112 | tf_op jit(solution)/shard_map/dot_general | solution.py:58
  34.3 4.6 %collective-permute-start = (f32[2,4,128,128]{3,2,1,0:T(8,128)S(1)}, f32[2,4,128,128]{3,2,1,0:T(8,128)S(1)}, u32[]{:S(2)}, u32[]{:S(2)}) collective-permute-start(f32[2,4,128,128]{3,2,1,0:T(8,128)S(1)} %fusion.10), channel_id=1, source_target_pairs={{0,1},{1,2},{2,3},{4,5},{5,6},{6,7},{8,9},{9,10},{10,11},{12,13},{... | collective-permute-start | bytes 1572872 | tf_op jit(solution)/shard_map/ppermute | solution.py:15
  38.9 0.0 copy-done.1
  38.9 0.6 %convolution_bitcast_fusion.2 = f32[2,4,128,128]{2,3,1,0:T(8,128)S(1)} fusion(f32[2,4,128,128]{3,2,1,0:T(8,128)S(1)} %reshape_reshape.3, f32[1,128,128]{2,1,0:T(8,128)S(1)} %copy-done.1), kind=kOutput, calls=%fused_computation.3 | convolution fusion | flops 100663296 | bytes 1114112 | tf_op jit(solution)/shard_map/dot_general | solution.py:57
  39.5 0.6 %fusion.4 = f32[2,4,128,128]{3,2,1,0:T(8,128)S(1)} fusion(f32[2,4,128,128]{2,3,1,0:T(8,128)S(1)} %convolution_bitcast_fusion.2, f32[1,128,128]{2,1,0:T(8,128)S(1)} %copy-done.1), kind=kOutput, calls=%fused_computation.20 | convolution fusion | flops 100663296 | bytes 1114112 | tf_op jit(solution)/shard_map/dot_general | solution.py:58
  40.1 6.6 %collective-permute-done.1 = f32[2,4,128,128]{2,3,1,0:T(8,128)S(1)} collective-permute-done((f32[2,4,128,128]{2,3,1,0:T(8,128)S(1)}, f32[2,4,128,128]{2,3,1,0:T(8,128)S(1)}, u32[]{:S(2)}, u32[]{:S(2)}) %collective-permute-start.1) | collective-permute-done | bytes 524320 | tf_op jit(solution)/shard_map/ppermute | solution.py:15
  46.7 0.4 convolution_bitcast_fusion
  47.1 0.6 %fusion.7 = f32[2,4,128,128]{3,2,1,0:T(8,128)S(1)} fusion(f32[2,4,128,128]{2,3,1,0:T(8,128)S(1)} %convolution_bitcast_fusion, f32[1,128,128]{2,1,0:T(8,128)S(1)} %copy-done), kind=kOutput, calls=%fused_computation.23 | convolution fusion | flops 100663296 | bytes 1114112 | tf_op jit(solution)/shard_map/dot_general | solution.py:58
  47.7 1.4 %collective-permute-done = f32[2,4,128,128]{3,2,1,0:T(8,128)S(1)} collective-permute-done((f32[2,4,128,128]{3,2,1,0:T(8,128)S(1)}, f32[2,4,128,128]{3,2,1,0:T(8,128)S(1)}, u32[]{:S(2)}, u32[]{:S(2)}) %collective-permute-start) | collective-permute-done | bytes 524320 | tf_op jit(solution)/shard_map/ppermute | solution.py:15
  49.1 0.1 add_add_fusion
  49.2 1.0 %add.106 = f32[1,2,4,16384]{3,2,1,0:T(4,128)} reshape(f32[2,4,128,128]{3,2,1,0:T(8,128)S(1)} %add_add_fusion) | data formatting | bytes 1048576 | tf_op jit(solution)/shard_map/add | solution.py:93
  (4 shorter events, 0.1 us)
Async XLA Ops:
  0.0 33.1 %copy-start = (f32[1,128,128]{2,1,0:T(8,128)S(1)}, f32[1,128,128]{2,1,0:T(8,128)}, u32[]{:S(2)}) copy-start(f32[1,128,128]{2,1,0:T(8,128)} %param.7) | copy-start | bytes 196612
  2.6 14.9 %all-to-all-start = ((bf16[8,16,2048]{2,1,0:T(8,128)(2,1)}), bf16[8,16,2048]{2,1,0:T(8,128)(2,1)S(1)}, u32[]{:S(2)}, u32[]{:S(2)}) async-start(bf16[8,16,2048]{2,1,0:T(8,128)(2,1)} %reshape.240), calls=%async_computation | async-start | bytes 1048576 | tf_op jit(solution)/shard_map/all_to_all | solution.py:76
  31.5 7.4 %copy-start.1 = (f32[1,128,128]{2,1,0:T(8,128)S(1)}, f32[1,128,128]{2,1,0:T(8,128)}, u32[]{:S(2)}) copy-start(f32[1,128,128]{2,1,0:T(8,128)} %param.6) | copy-start | bytes 196612
  31.8 14.9 %collective-permute-start.1 = (f32[2,4,128,128]{2,3,1,0:T(8,128)S(1)}, f32[2,4,128,128]{2,3,1,0:T(8,128)S(1)}, u32[]{:S(2)}, u32[]{:S(2)}) collective-permute-start(f32[2,4,128,128]{2,3,1,0:T(8,128)S(1)} %copy.17), channel_id=1, source_target_pairs={{1,0},{2,1},{3,2},{5,4},{6,5},{7,6},{9,8},{10,9},{11,10},{13,12},{... | collective-permute-start | bytes 1572872 | tf_op jit(solution)/shard_map/ppermute | solution.py:15
  34.3 14.8 %collective-permute-start = (f32[2,4,128,128]{3,2,1,0:T(8,128)S(1)}, f32[2,4,128,128]{3,2,1,0:T(8,128)S(1)}, u32[]{:S(2)}, u32[]{:S(2)}) collective-permute-start(f32[2,4,128,128]{3,2,1,0:T(8,128)S(1)} %fusion.10), channel_id=1, source_target_pairs={{0,1},{1,2},{2,3},{4,5},{5,6},{6,7},{8,9},{9,10},{10,11},{12,13},{... | collective-permute-start | bytes 1572872 | tf_op jit(solution)/shard_map/ppermute | solution.py:15

commit v7 on v6

--- a/solution.py
+++ b/solution.py
@@ -3,6 +3,8 @@
 import jax
 import jax.numpy as jnp
 from jax import lax
+from jax.experimental import pallas as pl
+from jax.experimental.pallas import tpu as pltpu
 from jax.sharding import PartitionSpec as P
 
 BS = 128
@@ -58,6 +60,24 @@
     return jnp.matmul(inner, right, precision=lax.Precision.HIGH)
 
 
+def by_destination(g_lesser, g_greater, groups, tile_width):
+    e_local = g_lesser.shape[2]
+
+    def kernel(lesser_ref, greater_ref, out_ref):
+        for dest in range(groups):
+            for which, ref in enumerate((lesser_ref, greater_ref)):
+                for part in range(2):
+                    row = (which * 2 + part) * e_local
+                    out_ref[dest, row:row + e_local, :] = ref[0, part, :, dest * tile_width:(dest + 1) * tile_width]
+
+    return pl.pallas_call(
+        kernel,
+        out_shape=jax.ShapeDtypeStruct((groups, 4 * e_local, tile_width), g_lesser.dtype),
+        in_specs=[pl.BlockSpec(memory_space=pltpu.VMEM)] * 2,
+        out_specs=pl.BlockSpec(memory_space=pltpu.VMEM),
+    )(g_lesser, g_greater)
+
+
 def per_device(g_lesser, g_greater, v_diag, v_couple):
     groups = lax.axis_size("energy")
     e_local = g_lesser.shape[2]
@@ -69,10 +89,13 @@
     couple_own = v_couple[0]
     forward, inverse = tables(count, e_local, groups)
 
-    both = jnp.stack([g_lesser[0], g_greater[0]])
-    both = jnp.pad(both, ((0, 0), (0, 0), (0, 0), (0, padding)))
-    both = both.reshape(2, 2, e_local, groups, tile_width)
-    both = both.transpose(3, 0, 1, 2, 4).reshape(groups, 4 * e_local, tile_width)
+    if padding == 0:
+        both = by_destination(g_lesser, g_greater, groups, tile_width)
+    else:
+        both = jnp.stack([g_lesser[0], g_greater[0]])
+        both = jnp.pad(both, ((0, 0), (0, 0), (0, 0), (0, padding)))
+        both = both.reshape(2, 2, e_local, groups, tile_width)
+        both = both.transpose(3, 0, 1, 2, 4).reshape(groups, 4 * e_local, tile_width)
     got = lax.all_to_all(both, "energy", 0, 0, tiled=True)
     polar_tile = correlate(got.reshape(groups * 4 * e_local, tile_width), forward, inverse)
 

time: 50.5 us -> 49.9 us (0.988)
  Pallas kernels: 0 us -> 1.99 us
  other arithmetic: 2.2 us -> 0.75 us
  local copies, waits for them, and re-layouts: 3.45 us -> 2.29 us
    pallas_call x0 -> x1, Pallas kernels: none -> 1.99 us  [by_destination(): pl.pallas_call(kernel, out_shape=jax.ShapeDtypeStruct((groups, 4 * e_loca...]
    another operation x1 -> x0, other arithmetic: 1.45 us -> none  [per_device(): both = jnp.stack([g_lesser[0], g_greater[0]])]
    reshape x2 -> x0, local copies, waits for them, and re-layouts: 1.16 us -> none  [the longest x1 0.92 us: per_device(): both.transpose(3, 0, 1, 2, 4).reshape(groups, 4 * e_local, tile_width)]
where the time goes in v7:
time: 49.9 us; the launch traced here: 49.6 us
  waiting for transfers between devices  16.5 us (33%)
  blocking collectives  12.2 us (24%)
  starting transfers between devices  11 us (22%)
  matrix products  4.63 us (9%)
  local copies, waits for them, and re-layouts  2.29 us (5%)
  Pallas kernels  1.99 us (4%)
  other arithmetic  0.75 us (2%)
    all_to_all x1, blocking collectives, per_device(): back = lax.all_to_all(send, 'energy', 0, 0, tiled=True)  12.2 us
    all_to_all x1, waiting for transfers between devices, per_device(): got = lax.all_to_all(both, 'energy', 0, 0, tiled=True)  8.5 us
    ppermute x2, waiting for transfers between devices, shifted(): return lax.ppermute(x, axis, pairs)  8.01 us
    ppermute x2, starting transfers between devices, shifted(): return lax.ppermute(x, axis, pairs)  5.87 us
    all_to_all x1, starting transfers between devices, per_device(): got = lax.all_to_all(both, 'energy', 0, 0, tiled=True)  5.17 us
    pallas_call x1, Pallas kernels, by_destination(): pl.pallas_call(kernel, out_shape=jax.ShapeDtypeStruct((groups, 4 * e_loca...  1.99 us
    dot_general x3, matrix products, sandwich(): return jnp.matmul(inner, right, precision=lax.Precision.HIGH)  1.77 us
    dot_general x3, matrix products, sandwich(): inner = jnp.matmul(left, field, precision=lax.Precision.HIGH)  1.55 us
  transfers between devices with their start and end apart: 3, of which 3 were waited for; matrix products, arithmetic and copies ran while one was open for 9% of the time, Pallas kernels for 0%

profile of v7, /device:TPU:0, one launch (start us, length us, event | category | flops | bytes accessed | tf_op | source)
XLA Modules:
  0.0 49.6 jit_solution(3472854685760373037)
XLA Ops:
  0.0 0.0 copy-start
  0.0 2.0 %shard_map.46 = bf16[8,16,2048]{2,1,0:T(8,128)(2,1)} custom-call(bf16[1,2,4,16384]{3,2,1,0:T(4,128)(2,1)} %lesser_ref.1, bf16[1,2,4,16384]{3,2,1,0:T(4,128)(2,1)} %greater_ref.1), custom_call_target="tpu_custom_call" | custom-call | tf_op jit(solution)/shard_map/pallas_call | solution.py:73
  2.0 5.2 %all-to-all-start = ((bf16[8,16,2048]{2,1,0:T(8,128)(2,1)}), bf16[8,16,2048]{2,1,0:T(8,128)(2,1)S(1)}, u32[]{:S(2)}, u32[]{:S(2)}) async-start(bf16[8,16,2048]{2,1,0:T(8,128)(2,1)} %shard_map.46), calls=%async_computation | async-start | bytes 1048576 | tf_op jit(solution)/shard_map/all_to_all | solution.py:99
  7.2 0.2 fusion.22
  7.4 0.1 copy.7
  7.5 0.1 copy.8
  7.6 0.1 convert_element_type.77
  7.8 0.1 copy.9
  7.9 0.1 convert_element_type.79
  8.1 0.2 fusion.25
  8.3 0.1 maximum_maximum_fusion
  8.4 8.5 %all-to-all-done = bf16[8,16,2048]{2,1,0:T(8,128)(2,1)S(1)} async-done(((bf16[8,16,2048]{2,1,0:T(8,128)(2,1)}), bf16[8,16,2048]{2,1,0:T(8,128)(2,1)S(1)}, u32[]{:S(2)}, u32[]{:S(2)}) %all-to-all-start) | async-done | bytes 524320 | tf_op jit(solution)/shard_map/all_to_all | solution.py:99
  16.9 0.5 fusion.27
  17.4 0.5 convolution_add_fusion
  17.8 0.1 multiply_add_fusion
  18.0 0.4 fusion
  18.4 12.2 %all_to_all.10 = f32[8,8,2048]{2,1,0:T(8,128)S(1)} all-to-all(f32[8,8,2048]{2,1,0:T(8,128)S(1)} %fusion), channel_id=1, replica_groups=mesh['energy'=8,'space'=4] {'energy'}, dimensions={0} | all-to-all | bytes 1048576 | tf_op jit(solution)/shard_map/all_to_all | solution.py:103
  30.5 0.3 copy.24
  30.8 0.0 copy-start.1
  30.9 0.1 reshape_reshape.3
  31.0 0.2 copy.15
  31.2 1.3 %collective-permute-start.1 = (f32[2,4,128,128]{2,3,1,0:T(8,128)S(1)}, f32[2,4,128,128]{2,3,1,0:T(8,128)S(1)}, u32[]{:S(2)}, u32[]{:S(2)}) collective-permute-start(f32[2,4,128,128]{2,3,1,0:T(8,128)S(1)} %copy.15), channel_id=1, source_target_pairs={{1,0},{2,1},{3,2},{5,4},{6,5},{7,6},{9,8},{10,9},{11,10},{13,12},{... | collective-permute-start | bytes 1572872 | tf_op jit(solution)/shard_map/ppermute | solution.py:17
  32.5 0.0 copy-done
  32.5 0.6 %convolution_bitcast_fusion.1 = f32[2,4,128,128]{2,3,1,0:T(8,128)S(1)} fusion(f32[2,4,128,128]{3,2,1,0:T(8,128)S(1)} %reshape_reshape.3, f32[1,128,128]{2,1,0:T(8,128)S(1)} %copy-done), kind=kOutput, calls=%fused_computation.2 | convolution fusion | flops 100663296 | bytes 1114112 | tf_op jit(solution)/shard_map/dot_general | solution.py:59
  33.1 0.6 %fusion.10 = f32[2,4,128,128]{3,2,1,0:T(8,128)S(1)} fusion(f32[2,4,128,128]{2,3,1,0:T(8,128)S(1)} %convolution_bitcast_fusion.1, f32[1,128,128]{2,1,0:T(8,128)S(1)} %copy-done), kind=kOutput, calls=%fused_computation.24 | convolution fusion | flops 100663296 | bytes 1114112 | tf_op jit(solution)/shard_map/dot_general | solution.py:60
  33.7 4.6 %collective-permute-start = (f32[2,4,128,128]{3,2,1,0:T(8,128)S(1)}, f32[2,4,128,128]{3,2,1,0:T(8,128)S(1)}, u32[]{:S(2)}, u32[]{:S(2)}) collective-permute-start(f32[2,4,128,128]{3,2,1,0:T(8,128)S(1)} %fusion.10), channel_id=1, source_target_pairs={{0,1},{1,2},{2,3},{4,5},{5,6},{6,7},{8,9},{9,10},{10,11},{12,13},{... | collective-permute-start | bytes 1572872 | tf_op jit(solution)/shard_map/ppermute | solution.py:17
  38.2 0.0 copy-done.1
  38.3 0.6 %convolution_bitcast_fusion.2 = f32[2,4,128,128]{2,3,1,0:T(8,128)S(1)} fusion(f32[2,4,128,128]{3,2,1,0:T(8,128)S(1)} %reshape_reshape.3, f32[1,128,128]{2,1,0:T(8,128)S(1)} %copy-done.1), kind=kOutput, calls=%fused_computation.3 | convolution fusion | flops 100663296 | bytes 1114112 | tf_op jit(solution)/shard_map/dot_general | solution.py:59
  38.9 0.6 %fusion.4 = f32[2,4,128,128]{3,2,1,0:T(8,128)S(1)} fusion(f32[2,4,128,128]{2,3,1,0:T(8,128)S(1)} %convolution_bitcast_fusion.2, f32[1,128,128]{2,1,0:T(8,128)S(1)} %copy-done.1), kind=kOutput, calls=%fused_computation.18 | convolution fusion | flops 100663296 | bytes 1114112 | tf_op jit(solution)/shard_map/dot_general | solution.py:60
  39.4 6.6 %collective-permute-done.1 = f32[2,4,128,128]{2,3,1,0:T(8,128)S(1)} collective-permute-done((f32[2,4,128,128]{2,3,1,0:T(8,128)S(1)}, f32[2,4,128,128]{2,3,1,0:T(8,128)S(1)}, u32[]{:S(2)}, u32[]{:S(2)}) %collective-permute-start.1) | collective-permute-done | bytes 524320 | tf_op jit(solution)/shard_map/ppermute | solution.py:17
  46.1 0.4 convolution_bitcast_fusion
  46.4 0.6 %fusion.7 = f32[2,4,128,128]{3,2,1,0:T(8,128)S(1)} fusion(f32[2,4,128,128]{2,3,1,0:T(8,128)S(1)} %convolution_bitcast_fusion, f32[1,128,128]{2,1,0:T(8,128)S(1)} %copy-done), kind=kOutput, calls=%fused_computation.21 | convolution fusion | flops 100663296 | bytes 1114112 | tf_op jit(solution)/shard_map/dot_general | solution.py:60
  47.0 1.4 %collective-permute-done = f32[2,4,128,128]{3,2,1,0:T(8,128)S(1)} collective-permute-done((f32[2,4,128,128]{3,2,1,0:T(8,128)S(1)}, f32[2,4,128,128]{3,2,1,0:T(8,128)S(1)}, u32[]{:S(2)}, u32[]{:S(2)}) %collective-permute-start) | collective-permute-done | bytes 524320 | tf_op jit(solution)/shard_map/ppermute | solution.py:17
  48.4 0.1 add_add_fusion
  48.5 1.0 %add.106 = f32[1,2,4,16384]{3,2,1,0:T(4,128)} reshape(f32[2,4,128,128]{3,2,1,0:T(8,128)S(1)} %add_add_fusion) | data formatting | bytes 1048576 | tf_op jit(solution)/shard_map/add | solution.py:116
  (4 shorter events, 0.1 us)
Async XLA Ops:
  0.0 32.5 %copy-start = (f32[1,128,128]{2,1,0:T(8,128)S(1)}, f32[1,128,128]{2,1,0:T(8,128)}, u32[]{:S(2)}) copy-start(f32[1,128,128]{2,1,0:T(8,128)} %param.7) | copy-start | bytes 196612
  2.0 14.9 %all-to-all-start = ((bf16[8,16,2048]{2,1,0:T(8,128)(2,1)}), bf16[8,16,2048]{2,1,0:T(8,128)(2,1)S(1)}, u32[]{:S(2)}, u32[]{:S(2)}) async-start(bf16[8,16,2048]{2,1,0:T(8,128)(2,1)} %shard_map.46), calls=%async_computation | async-start | bytes 1048576 | tf_op jit(solution)/shard_map/all_to_all | solution.py:99
  30.8 7.4 %copy-start.1 = (f32[1,128,128]{2,1,0:T(8,128)S(1)}, f32[1,128,128]{2,1,0:T(8,128)}, u32[]{:S(2)}) copy-start(f32[1,128,128]{2,1,0:T(8,128)} %param.6) | copy-start | bytes 196612
  31.2 14.9 %collective-permute-start.1 = (f32[2,4,128,128]{2,3,1,0:T(8,128)S(1)}, f32[2,4,128,128]{2,3,1,0:T(8,128)S(1)}, u32[]{:S(2)}, u32[]{:S(2)}) collective-permute-start(f32[2,4,128,128]{2,3,1,0:T(8,128)S(1)} %copy.15), channel_id=1, source_target_pairs={{1,0},{2,1},{3,2},{5,4},{6,5},{7,6},{9,8},{10,9},{11,10},{13,12},{... | collective-permute-start | bytes 1572872 | tf_op jit(solution)/shard_map/ppermute | solution.py:17
  33.7 14.8 %collective-permute-start = (f32[2,4,128,128]{3,2,1,0:T(8,128)S(1)}, f32[2,4,128,128]{3,2,1,0:T(8,128)S(1)}, u32[]{:S(2)}, u32[]{:S(2)}) collective-permute-start(f32[2,4,128,128]{3,2,1,0:T(8,128)S(1)} %fusion.10), channel_id=1, source_target_pairs={{0,1},{1,2},{2,3},{4,5},{5,6},{6,7},{8,9},{9,10},{10,11},{12,13},{... | collective-permute-start | bytes 1572872 | tf_op jit(solution)/shard_map/ppermute | solution.py:17

commit v8 on v7

--- a/solution.py
+++ b/solution.py
@@ -111,9 +111,10 @@
     from_below = shifted(to_next, "space", 1)
     local = sandwich(diag_block, polar, diag_block)
     from_above = sandwich(couple_own, polar_above, couple_own.T)
-    local, from_below, from_above = lax.optimization_barrier((local, from_below, from_above))
     shape = (1, 2, e_local, elements)
-    return local.reshape(shape) + from_below.reshape(shape) + from_above.reshape(shape)
+    partial = (local + from_above).reshape(shape)
+    partial, from_below = lax.optimization_barrier((partial, from_below))
+    return partial + from_below.reshape(shape)
 
 
 def solution(mesh):

time: 49.9 us -> 49.9 us (level)
  other arithmetic: 0.75 us -> 1.6 us
  local copies, waits for them, and re-layouts: 2.29 us -> 1.7 us
    add x1 -> x0, local copies, waits for them, and re-layouts: 1.02 us -> none  [per_device(): local.reshape(shape) + from_below.reshape(shape) + from_above.reshape(shape)]
    add x1, other arithmetic: 0.08 us -> 0.93 us  [per_device(): return partial + from_below.reshape(shape)]
  transfers between devices with their start and end apart: 3 -> 3, of which waited for: 3 -> 3; matrix products, arithmetic and copies ran while one was open for 9% -> 10% of each run, Pallas kernels for 0% -> 0%
where the time goes in v8:
time: 49.9 us; the launch traced here: 49.6 us
  waiting for transfers between devices  16.3 us (33%)
  blocking collectives  12.2 us (24%)
  starting transfers between devices  11 us (22%)
  matrix products  4.63 us (9%)
  Pallas kernels  1.99 us (4%)
  local copies, waits for them, and re-layouts  1.7 us (3%)
  other arithmetic  1.6 us (3%)
    all_to_all x1, blocking collectives, per_device(): back = lax.all_to_all(send, 'energy', 0, 0, tiled=True)  12.2 us
    all_to_all x1, waiting for transfers between devices, per_device(): got = lax.all_to_all(both, 'energy', 0, 0, tiled=True)  8.5 us
    ppermute x2, waiting for transfers between devices, shifted(): return lax.ppermute(x, axis, pairs)  7.79 us
    ppermute x2, starting transfers between devices, shifted(): return lax.ppermute(x, axis, pairs)  5.87 us
    all_to_all x1, starting transfers between devices, per_device(): got = lax.all_to_all(both, 'energy', 0, 0, tiled=True)  5.17 us
    pallas_call x1, Pallas kernels, by_destination(): pl.pallas_call(kernel, out_shape=jax.ShapeDtypeStruct((groups, 4 * e_loca...  1.99 us
    dot_general x3, matrix products, sandwich(): return jnp.matmul(inner, right, precision=lax.Precision.HIGH)  1.77 us
    dot_general x3, matrix products, sandwich(): inner = jnp.matmul(left, field, precision=lax.Precision.HIGH)  1.55 us
  transfers between devices with their start and end apart: 3, of which 3 were waited for; matrix products, arithmetic and copies ran while one was open for 10% of the time, Pallas kernels for 0%

profile of v8, /device:TPU:0, one launch (start us, length us, event | category | flops | bytes accessed | tf_op | source)
XLA Modules:
  0.0 49.6 jit_solution(10396914046242773421)
XLA Ops:
  0.0 0.0 copy-start
  0.0 2.0 %shard_map.46 = bf16[8,16,2048]{2,1,0:T(8,128)(2,1)} custom-call(bf16[1,2,4,16384]{3,2,1,0:T(4,128)(2,1)} %lesser_ref.1, bf16[1,2,4,16384]{3,2,1,0:T(4,128)(2,1)} %greater_ref.1), custom_call_target="tpu_custom_call" | custom-call | tf_op jit(solution)/shard_map/pallas_call | solution.py:73
  2.0 5.2 %all-to-all-start = ((bf16[8,16,2048]{2,1,0:T(8,128)(2,1)}), bf16[8,16,2048]{2,1,0:T(8,128)(2,1)S(1)}, u32[]{:S(2)}, u32[]{:S(2)}) async-start(bf16[8,16,2048]{2,1,0:T(8,128)(2,1)} %shard_map.46), calls=%async_computation | async-start | bytes 1048576 | tf_op jit(solution)/shard_map/all_to_all | solution.py:99
  7.2 0.2 fusion.21
  7.4 0.1 copy.7
  7.5 0.1 copy.8
  7.6 0.1 convert_element_type.77
  7.8 0.1 copy.9
  7.9 0.1 convert_element_type.79
  8.1 0.2 fusion.24
  8.3 0.1 maximum_maximum_fusion
  8.4 8.5 %all-to-all-done = bf16[8,16,2048]{2,1,0:T(8,128)(2,1)S(1)} async-done(((bf16[8,16,2048]{2,1,0:T(8,128)(2,1)}), bf16[8,16,2048]{2,1,0:T(8,128)(2,1)S(1)}, u32[]{:S(2)}, u32[]{:S(2)}) %all-to-all-start) | async-done | bytes 524320 | tf_op jit(solution)/shard_map/all_to_all | solution.py:99
  16.9 0.5 fusion.26
  17.4 0.5 convolution_add_fusion
  17.8 0.1 multiply_add_fusion
  18.0 0.4 fusion
  18.4 12.2 %all_to_all.10 = f32[8,8,2048]{2,1,0:T(8,128)S(1)} all-to-all(f32[8,8,2048]{2,1,0:T(8,128)S(1)} %fusion), channel_id=1, replica_groups=mesh['energy'=8,'space'=4] {'energy'}, dimensions={0} | all-to-all | bytes 1048576 | tf_op jit(solution)/shard_map/all_to_all | solution.py:103
  30.5 0.3 copy.24
  30.8 0.0 copy-start.1
  30.9 0.1 reshape_reshape.3
  31.0 0.2 copy.13
  31.2 1.3 %collective-permute-start = (f32[2,4,128,128]{2,3,1,0:T(8,128)S(1)}, f32[2,4,128,128]{2,3,1,0:T(8,128)S(1)}, u32[]{:S(2)}, u32[]{:S(2)}) collective-permute-start(f32[2,4,128,128]{2,3,1,0:T(8,128)S(1)} %copy.13), channel_id=1, source_target_pairs={{1,0},{2,1},{3,2},{5,4},{6,5},{7,6},{9,8},{10,9},{11,10},{13,12},{... | collective-permute-start | bytes 1572872 | tf_op jit(solution)/shard_map/ppermute | solution.py:17
  32.5 0.0 copy-done
  32.5 0.6 %convolution_bitcast_fusion = f32[2,4,128,128]{2,3,1,0:T(8,128)S(1)} fusion(f32[2,4,128,128]{3,2,1,0:T(8,128)S(1)} %reshape_reshape.3, f32[1,128,128]{2,1,0:T(8,128)S(1)} %copy-done), kind=kOutput, calls=%fused_computation.1 | convolution fusion | flops 100663296 | bytes 1114112 | tf_op jit(solution)/shard_map/dot_general | solution.py:59
  33.1 0.6 %fusion.7 = f32[2,4,128,128]{3,2,1,0:T(8,128)S(1)} fusion(f32[2,4,128,128]{2,3,1,0:T(8,128)S(1)} %convolution_bitcast_fusion, f32[1,128,128]{2,1,0:T(8,128)S(1)} %copy-done), kind=kOutput, calls=%fused_computation.21 | convolution fusion | flops 100663296 | bytes 1114112 | tf_op jit(solution)/shard_map/dot_general | solution.py:60
  33.7 4.6 %collective-permute-start.1 = (f32[2,4,128,128]{3,2,1,0:T(8,128)S(1)}, f32[2,4,128,128]{3,2,1,0:T(8,128)S(1)}, u32[]{:S(2)}, u32[]{:S(2)}) collective-permute-start(f32[2,4,128,128]{3,2,1,0:T(8,128)S(1)} %fusion.7), channel_id=1, source_target_pairs={{0,1},{1,2},{2,3},{4,5},{5,6},{6,7},{8,9},{9,10},{10,11},{12,13},{... | collective-permute-start | bytes 1572872 | tf_op jit(solution)/shard_map/ppermute | solution.py:17
  38.2 0.0 copy-done.1
  38.3 0.6 %convolution_bitcast_fusion.2 = f32[2,4,128,128]{2,3,1,0:T(8,128)S(1)} fusion(f32[2,4,128,128]{3,2,1,0:T(8,128)S(1)} %reshape_reshape.3, f32[1,128,128]{2,1,0:T(8,128)S(1)} %copy-done.1), kind=kOutput, calls=%fused_computation.3 | convolution fusion | flops 100663296 | bytes 1114112 | tf_op jit(solution)/shard_map/dot_general | solution.py:59
  38.9 0.6 %fusion.4 = f32[2,4,128,128]{3,2,1,0:T(8,128)S(1)} fusion(f32[2,4,128,128]{2,3,1,0:T(8,128)S(1)} %convolution_bitcast_fusion.2, f32[1,128,128]{2,1,0:T(8,128)S(1)} %copy-done.1), kind=kOutput, calls=%fused_computation.18 | convolution fusion | flops 100663296 | bytes 1114112 | tf_op jit(solution)/shard_map/dot_general | solution.py:60
  39.4 6.6 %collective-permute-done = f32[2,4,128,128]{2,3,1,0:T(8,128)S(1)} collective-permute-done((f32[2,4,128,128]{2,3,1,0:T(8,128)S(1)}, f32[2,4,128,128]{2,3,1,0:T(8,128)S(1)}, u32[]{:S(2)}, u32[]{:S(2)}) %collective-permute-start) | collective-permute-done | bytes 524320 | tf_op jit(solution)/shard_map/ppermute | solution.py:17
  46.1 0.4 convolution_bitcast_fusion.1
  46.4 0.6 %convolution_add_fusion.1 = f32[2,4,128,128]{3,2,1,0:T(8,128)S(1)} fusion(f32[2,4,128,128]{3,2,1,0:T(8,128)S(1)} %fusion.4, f32[2,4,128,128]{2,3,1,0:T(8,128)S(1)} %convolution_bitcast_fusion.1, f32[1,128,128]{2,1,0:T(8,128)S(1)} %copy-done), kind=kOutput, calls=%fused_computation.4 | convolution fusion | flops 100794368 | bytes 1638400 | tf_op jit(solution)/shard_map/dot_general | solution.py:60
  47.0 0.2 reshape.204
  47.3 1.2 %collective-permute-done.1 = f32[2,4,128,128]{3,2,1,0:T(8,128)S(1)} collective-permute-done((f32[2,4,128,128]{3,2,1,0:T(8,128)S(1)}, f32[2,4,128,128]{3,2,1,0:T(8,128)S(1)}, u32[]{:S(2)}, u32[]{:S(2)}) %collective-permute-start.1) | collective-permute-done | bytes 524320 | tf_op jit(solution)/shard_map/ppermute | solution.py:17
  48.4 0.2 reshape.205
  48.7 0.9 %add.85 = f32[1,2,4,16384]{3,2,1,0:T(4,128)} add(f32[1,2,4,16384]{3,2,1,0:T(4,128)S(1)} %reshape.204, f32[1,2,4,16384]{3,2,1,0:T(4,128)S(1)} %reshape.205) | non-fusion elementwise | flops 131072 | bytes 1572864 | tf_op jit(solution)/shard_map/add | solution.py:117
  (4 shorter events, 0.1 us)
Async XLA Ops:
  0.0 32.5 %copy-start = (f32[1,128,128]{2,1,0:T(8,128)S(1)}, f32[1,128,128]{2,1,0:T(8,128)}, u32[]{:S(2)}) copy-start(f32[1,128,128]{2,1,0:T(8,128)} %param.7) | copy-start | bytes 196612
  2.0 14.9 %all-to-all-start = ((bf16[8,16,2048]{2,1,0:T(8,128)(2,1)}), bf16[8,16,2048]{2,1,0:T(8,128)(2,1)S(1)}, u32[]{:S(2)}, u32[]{:S(2)}) async-start(bf16[8,16,2048]{2,1,0:T(8,128)(2,1)} %shard_map.46), calls=%async_computation | async-start | bytes 1048576 | tf_op jit(solution)/shard_map/all_to_all | solution.py:99
  30.8 7.4 %copy-start.1 = (f32[1,128,128]{2,1,0:T(8,128)S(1)}, f32[1,128,128]{2,1,0:T(8,128)}, u32[]{:S(2)}) copy-start(f32[1,128,128]{2,1,0:T(8,128)} %param.6) | copy-start | bytes 196612
  31.2 14.9 %collective-permute-start = (f32[2,4,128,128]{2,3,1,0:T(8,128)S(1)}, f32[2,4,128,128]{2,3,1,0:T(8,128)S(1)}, u32[]{:S(2)}, u32[]{:S(2)}) collective-permute-start(f32[2,4,128,128]{2,3,1,0:T(8,128)S(1)} %copy.13), channel_id=1, source_target_pairs={{1,0},{2,1},{3,2},{5,4},{6,5},{7,6},{9,8},{10,9},{11,10},{13,12},{... | collective-permute-start | bytes 1572872 | tf_op jit(solution)/shard_map/ppermute | solution.py:17
  33.7 14.8 %collective-permute-start.1 = (f32[2,4,128,128]{3,2,1,0:T(8,128)S(1)}, f32[2,4,128,128]{3,2,1,0:T(8,128)S(1)}, u32[]{:S(2)}, u32[]{:S(2)}) collective-permute-start(f32[2,4,128,128]{3,2,1,0:T(8,128)S(1)} %fusion.7), channel_id=1, source_target_pairs={{0,1},{1,2},{2,3},{4,5},{5,6},{6,7},{8,9},{9,10},{10,11},{12,13},{... | collective-permute-start | bytes 1572872 | tf_op jit(solution)/shard_map/ppermute | solution.py:17

commit v9 on v8

--- a/solution.py
+++ b/solution.py
@@ -63,18 +63,26 @@
 def by_destination(g_lesser, g_greater, groups, tile_width):
     e_local = g_lesser.shape[2]
 
-    def kernel(lesser_ref, greater_ref, out_ref):
+    def kernel(lesser_hbm, greater_hbm, out_ref, sems):
+        copies = []
         for dest in range(groups):
-            for which, ref in enumerate((lesser_ref, greater_ref)):
-                for part in range(2):
-                    row = (which * 2 + part) * e_local
-                    out_ref[dest, row:row + e_local, :] = ref[0, part, :, dest * tile_width:(dest + 1) * tile_width]
+            for which, ref in enumerate((lesser_hbm, greater_hbm)):
+                copy = pltpu.make_async_copy(
+                    ref.at[0, :, :, pl.ds(dest * tile_width, tile_width)],
+                    out_ref.at[dest, pl.ds(2 * which, 2)],
+                    sems.at[dest * 2 + which],
+                )
+                copy.start()
+                copies.append(copy)
+        for copy in copies:
+            copy.wait()
 
     return pl.pallas_call(
         kernel,
-        out_shape=jax.ShapeDtypeStruct((groups, 4 * e_local, tile_width), g_lesser.dtype),
-        in_specs=[pl.BlockSpec(memory_space=pltpu.VMEM)] * 2,
+        out_shape=jax.ShapeDtypeStruct((groups, 4, e_local, tile_width), g_lesser.dtype),
+        in_specs=[pl.BlockSpec(memory_space=pl.ANY)] * 2,
         out_specs=pl.BlockSpec(memory_space=pltpu.VMEM),
+        scratch_shapes=[pltpu.SemaphoreType.DMA((2 * groups,))],
     )(g_lesser, g_greater)
 
 

time: 49.9 us -> 50.1 us (level)
  no operation moved by 1% of the time
where the time goes in v9:
time: 50.1 us; the launch traced here: 49.7 us
  waiting for transfers between devices  16.3 us (33%)
  blocking collectives  12.2 us (24%)
  starting transfers between devices  11.1 us (22%)
  matrix products  4.63 us (9%)
  Pallas kernels  1.96 us (4%)
  local copies, waits for them, and re-layouts  1.82 us (4%)
  other arithmetic  1.6 us (3%)
    all_to_all x1, blocking collectives, per_device(): back = lax.all_to_all(send, 'energy', 0, 0, tiled=True)  12.2 us
    all_to_all x1, waiting for transfers between devices, per_device(): got = lax.all_to_all(both, 'energy', 0, 0, tiled=True)  8.5 us
    ppermute x2, waiting for transfers between devices, shifted(): return lax.ppermute(x, axis, pairs)  7.79 us
    ppermute x2, starting transfers between devices, shifted(): return lax.ppermute(x, axis, pairs)  5.87 us
    all_to_all x1, starting transfers between devices, per_device(): got = lax.all_to_all(both, 'energy', 0, 0, tiled=True)  5.18 us
    pallas_call x1, Pallas kernels, by_destination(): pl.pallas_call(kernel, out_shape=jax.ShapeDtypeStruct((groups, 4, e_local...  1.96 us
    dot_general x3, matrix products, sandwich(): return jnp.matmul(inner, right, precision=lax.Precision.HIGH)  1.77 us
    dot_general x3, matrix products, sandwich(): inner = jnp.matmul(left, field, precision=lax.Precision.HIGH)  1.55 us
  transfers between devices with their start and end apart: 3, of which 3 were waited for; matrix products, arithmetic and copies ran while one was open for 10% of the time, Pallas kernels for 0%

profile of v9, /device:TPU:0, one launch (start us, length us, event | category | flops | bytes accessed | tf_op | source)
XLA Modules:
  0.0 49.7 jit_solution(9274686815471860030)
XLA Ops:
  0.0 0.0 copy-start
  0.0 2.0 %shard_map.46 = bf16[8,4,4,2048]{3,2,1,0:T(4,128)(2,1)} custom-call(bf16[1,2,4,16384]{3,2,1,0:T(4,128)(2,1)} %lesser_hbm.1, bf16[1,2,4,16384]{3,2,1,0:T(4,128)(2,1)} %greater_hbm.1), custom_call_target="tpu_custom_call" | custom-call | tf_op jit(solution)/shard_map/pallas_call | solution.py:80
  2.0 5.2 %all-to-all-start = ((bf16[8,4,4,2048]{3,2,1,0:T(4,128)(2,1)}), bf16[8,4,4,2048]{3,2,1,0:T(4,128)(2,1)S(1)}, u32[]{:S(2)}, u32[]{:S(2)}) async-start(bf16[8,4,4,2048]{3,2,1,0:T(4,128)(2,1)} %shard_map.46), calls=%async_computation | async-start | bytes 1048576 | tf_op jit(solution)/shard_map/all_to_all | solution.py:107
  7.2 0.2 fusion.21
  7.4 0.1 copy.7
  7.5 0.1 copy.8
  7.6 0.1 convert_element_type.77
  7.8 0.1 copy.9
  7.9 0.1 convert_element_type.79
  8.1 0.2 fusion.24
  8.3 0.1 maximum_maximum_fusion
  8.4 8.5 %all-to-all-done = bf16[8,4,4,2048]{3,2,1,0:T(4,128)(2,1)S(1)} async-done(((bf16[8,4,4,2048]{3,2,1,0:T(4,128)(2,1)}), bf16[8,4,4,2048]{3,2,1,0:T(4,128)(2,1)S(1)}, u32[]{:S(2)}, u32[]{:S(2)}) %all-to-all-start) | async-done | bytes 524320 | tf_op jit(solution)/shard_map/all_to_all | solution.py:107
  16.9 0.1 reshape.202
  17.0 0.5 fusion.26
  17.5 0.5 convolution_add_fusion
  17.9 0.1 multiply_add_fusion
  18.1 0.4 fusion
  18.5 12.2 %all_to_all.10 = f32[8,8,2048]{2,1,0:T(8,128)S(1)} all-to-all(f32[8,8,2048]{2,1,0:T(8,128)S(1)} %fusion), channel_id=1, replica_groups=mesh['energy'=8,'space'=4] {'energy'}, dimensions={0} | all-to-all | bytes 1048576 | tf_op jit(solution)/shard_map/all_to_all | solution.py:111
  30.7 0.3 copy.24
  31.0 0.0 copy-start.1
  31.0 0.1 reshape_reshape.3
  31.1 0.2 copy.13
  31.3 1.3 %collective-permute-start = (f32[2,4,128,128]{2,3,1,0:T(8,128)S(1)}, f32[2,4,128,128]{2,3,1,0:T(8,128)S(1)}, u32[]{:S(2)}, u32[]{:S(2)}) collective-permute-start(f32[2,4,128,128]{2,3,1,0:T(8,128)S(1)} %copy.13), channel_id=1, source_target_pairs={{1,0},{2,1},{3,2},{5,4},{6,5},{7,6},{9,8},{10,9},{11,10},{13,12},{... | collective-permute-start | bytes 1572872 | tf_op jit(solution)/shard_map/ppermute | solution.py:17
  32.6 0.0 copy-done
  32.6 0.6 %convolution_bitcast_fusion = f32[2,4,128,128]{2,3,1,0:T(8,128)S(1)} fusion(f32[2,4,128,128]{3,2,1,0:T(8,128)S(1)} %reshape_reshape.3, f32[1,128,128]{2,1,0:T(8,128)S(1)} %copy-done), kind=kOutput, calls=%fused_computation.1 | convolution fusion | flops 100663296 | bytes 1114112 | tf_op jit(solution)/shard_map/dot_general | solution.py:59
  33.2 0.6 %fusion.7 = f32[2,4,128,128]{3,2,1,0:T(8,128)S(1)} fusion(f32[2,4,128,128]{2,3,1,0:T(8,128)S(1)} %convolution_bitcast_fusion, f32[1,128,128]{2,1,0:T(8,128)S(1)} %copy-done), kind=kOutput, calls=%fused_computation.21 | convolution fusion | flops 100663296 | bytes 1114112 | tf_op jit(solution)/shard_map/dot_general | solution.py:60
  33.8 4.6 %collective-permute-start.1 = (f32[2,4,128,128]{3,2,1,0:T(8,128)S(1)}, f32[2,4,128,128]{3,2,1,0:T(8,128)S(1)}, u32[]{:S(2)}, u32[]{:S(2)}) collective-permute-start(f32[2,4,128,128]{3,2,1,0:T(8,128)S(1)} %fusion.7), channel_id=1, source_target_pairs={{0,1},{1,2},{2,3},{4,5},{5,6},{6,7},{8,9},{9,10},{10,11},{12,13},{... | collective-permute-start | bytes 1572872 | tf_op jit(solution)/shard_map/ppermute | solution.py:17
  38.4 0.0 copy-done.1
  38.4 0.6 %convolution_bitcast_fusion.2 = f32[2,4,128,128]{2,3,1,0:T(8,128)S(1)} fusion(f32[2,4,128,128]{3,2,1,0:T(8,128)S(1)} %reshape_reshape.3, f32[1,128,128]{2,1,0:T(8,128)S(1)} %copy-done.1), kind=kOutput, calls=%fused_computation.3 | convolution fusion | flops 100663296 | bytes 1114112 | tf_op jit(solution)/shard_map/dot_general | solution.py:59
  39.0 0.6 %fusion.4 = f32[2,4,128,128]{3,2,1,0:T(8,128)S(1)} fusion(f32[2,4,128,128]{2,3,1,0:T(8,128)S(1)} %convolution_bitcast_fusion.2, f32[1,128,128]{2,1,0:T(8,128)S(1)} %copy-done.1), kind=kOutput, calls=%fused_computation.18 | convolution fusion | flops 100663296 | bytes 1114112 | tf_op jit(solution)/shard_map/dot_general | solution.py:60
  39.6 6.6 %collective-permute-done = f32[2,4,128,128]{2,3,1,0:T(8,128)S(1)} collective-permute-done((f32[2,4,128,128]{2,3,1,0:T(8,128)S(1)}, f32[2,4,128,128]{2,3,1,0:T(8,128)S(1)}, u32[]{:S(2)}, u32[]{:S(2)}) %collective-permute-start) | collective-permute-done | bytes 524320 | tf_op jit(solution)/shard_map/ppermute | solution.py:17
  46.2 0.4 convolution_bitcast_fusion.1
  46.6 0.6 %convolution_add_fusion.1 = f32[2,4,128,128]{3,2,1,0:T(8,128)S(1)} fusion(f32[2,4,128,128]{3,2,1,0:T(8,128)S(1)} %fusion.4, f32[2,4,128,128]{2,3,1,0:T(8,128)S(1)} %convolution_bitcast_fusion.1, f32[1,128,128]{2,1,0:T(8,128)S(1)} %copy-done), kind=kOutput, calls=%fused_computation.4 | convolution fusion | flops 100794368 | bytes 1638400 | tf_op jit(solution)/shard_map/dot_general | solution.py:60
  47.2 0.2 reshape.204
  47.4 1.2 %collective-permute-done.1 = f32[2,4,128,128]{3,2,1,0:T(8,128)S(1)} collective-permute-done((f32[2,4,128,128]{3,2,1,0:T(8,128)S(1)}, f32[2,4,128,128]{3,2,1,0:T(8,128)S(1)}, u32[]{:S(2)}, u32[]{:S(2)}) %collective-permute-start.1) | collective-permute-done | bytes 524320 | tf_op jit(solution)/shard_map/ppermute | solution.py:17
  48.6 0.2 reshape.205
  48.8 0.9 %add.85 = f32[1,2,4,16384]{3,2,1,0:T(4,128)} add(f32[1,2,4,16384]{3,2,1,0:T(4,128)S(1)} %reshape.204, f32[1,2,4,16384]{3,2,1,0:T(4,128)S(1)} %reshape.205) | non-fusion elementwise | flops 131072 | bytes 1572864 | tf_op jit(solution)/shard_map/add | solution.py:125
  (4 shorter events, 0.1 us)
Async XLA Ops:
  0.0 32.6 %copy-start = (f32[1,128,128]{2,1,0:T(8,128)S(1)}, f32[1,128,128]{2,1,0:T(8,128)}, u32[]{:S(2)}) copy-start(f32[1,128,128]{2,1,0:T(8,128)} %param.7) | copy-start | bytes 196612
  2.0 14.9 %all-to-all-start = ((bf16[8,4,4,2048]{3,2,1,0:T(4,128)(2,1)}), bf16[8,4,4,2048]{3,2,1,0:T(4,128)(2,1)S(1)}, u32[]{:S(2)}, u32[]{:S(2)}) async-start(bf16[8,4,4,2048]{3,2,1,0:T(4,128)(2,1)} %shard_map.46), calls=%async_computation | async-start | bytes 1048576 | tf_op jit(solution)/shard_map/all_to_all | solution.py:107
  31.0 7.4 %copy-start.1 = (f32[1,128,128]{2,1,0:T(8,128)S(1)}, f32[1,128,128]{2,1,0:T(8,128)}, u32[]{:S(2)}) copy-start(f32[1,128,128]{2,1,0:T(8,128)} %param.6) | copy-start | bytes 196612
  31.3 14.9 %collective-permute-start = (f32[2,4,128,128]{2,3,1,0:T(8,128)S(1)}, f32[2,4,128,128]{2,3,1,0:T(8,128)S(1)}, u32[]{:S(2)}, u32[]{:S(2)}) collective-permute-start(f32[2,4,128,128]{2,3,1,0:T(8,128)S(1)} %copy.13), channel_id=1, source_target_pairs={{1,0},{2,1},{3,2},{5,4},{6,5},{7,6},{9,8},{10,9},{11,10},{13,12},{... | collective-permute-start | bytes 1572872 | tf_op jit(solution)/shard_map/ppermute | solution.py:17
  33.8 14.8 %collective-permute-start.1 = (f32[2,4,128,128]{3,2,1,0:T(8,128)S(1)}, f32[2,4,128,128]{3,2,1,0:T(8,128)S(1)}, u32[]{:S(2)}, u32[]{:S(2)}) collective-permute-start(f32[2,4,128,128]{3,2,1,0:T(8,128)S(1)} %fusion.7), channel_id=1, source_target_pairs={{0,1},{1,2},{2,3},{4,5},{5,6},{6,7},{8,9},{9,10},{10,11},{12,13},{... | collective-permute-start | bytes 1572872 | tf_op jit(solution)/shard_map/ppermute | solution.py:17

commit v10 on v9

--- a/solution.py
+++ b/solution.py
@@ -109,12 +109,16 @@
 
     send = polar_tile.reshape(groups, 2 * e_local, tile_width)
     back = lax.all_to_all(send, "energy", 0, 0, tiled=True)
-    back = back.reshape(groups, 2, e_local, tile_width).transpose(1, 2, 0, 3)
-    back = back.reshape(2, e_local, groups * tile_width)[:, :, :elements]
-    polar = back.reshape(2, e_local, BS, BS)
+    back_above = shifted(back, "space", -1)
 
+    def as_blocks(received):
+        received = received.reshape(groups, 2, e_local, tile_width).transpose(1, 2, 0, 3)
+        received = received.reshape(2, e_local, groups * tile_width)[:, :, :elements]
+        return received.reshape(2, e_local, BS, BS)
+
+    polar = as_blocks(back)
+    polar_above = as_blocks(back_above)
     diag_block = v_diag[0]
-    polar_above = shifted(polar, "space", -1)
     to_next = sandwich(couple_own.T, polar, couple_own)
     from_below = shifted(to_next, "space", 1)
     local = sandwich(diag_block, polar, diag_block)

time: 50.1 us -> 49.9 us (level)
  waiting for transfers between devices: 16.3 us -> 15.7 us
    ppermute x2, waiting for transfers between devices: 7.79 us -> 7.22 us  [shifted(): return lax.ppermute(x, axis, pairs)]
  transfers between devices with their start and end apart: 3 -> 3, of which waited for: 3 -> 2; matrix products, arithmetic and copies ran while one was open for 10% -> 10% of each run, Pallas kernels for 0% -> 0%
where the time goes in v10:
time: 49.9 us; the launch traced here: 49.6 us
  waiting for transfers between devices  15.7 us (31%)
  blocking collectives  12.2 us (24%)
  starting transfers between devices  11.1 us (22%)
  matrix products  4.84 us (10%)
  local copies, waits for them, and re-layouts  2.01 us (4%)
  Pallas kernels  1.96 us (4%)
  other arithmetic  1.6 us (3%)
    all_to_all x1, blocking collectives, per_device(): back = lax.all_to_all(send, 'energy', 0, 0, tiled=True)  12.2 us
    all_to_all x1, waiting for transfers between devices, per_device(): got = lax.all_to_all(both, 'energy', 0, 0, tiled=True)  8.5 us
    ppermute x2, waiting for transfers between devices, shifted(): return lax.ppermute(x, axis, pairs)  7.22 us
    ppermute x2, starting transfers between devices, shifted(): return lax.ppermute(x, axis, pairs)  5.87 us
    all_to_all x1, starting transfers between devices, per_device(): got = lax.all_to_all(both, 'energy', 0, 0, tiled=True)  5.18 us
    pallas_call x1, Pallas kernels, by_destination(): pl.pallas_call(kernel, out_shape=jax.ShapeDtypeStruct((groups, 4, e_local...  1.96 us
    dot_general x3, matrix products, sandwich(): return jnp.matmul(inner, right, precision=lax.Precision.HIGH)  1.77 us
    dot_general x3, matrix products, sandwich(): inner = jnp.matmul(left, field, precision=lax.Precision.HIGH)  1.76 us
  transfers between devices with their start and end apart: 3, of which 2 were waited for; matrix products, arithmetic and copies ran while one was open for 10% of the time, Pallas kernels for 0%

profile of v10, /device:TPU:0, one launch (start us, length us, event | category | flops | bytes accessed | tf_op | source)
XLA Modules:
  0.0 49.6 jit_solution(8851634761832779525)
XLA Ops:
  0.0 0.0 copy-start
  0.0 2.0 %shard_map.46 = bf16[8,4,4,2048]{3,2,1,0:T(4,128)(2,1)} custom-call(bf16[1,2,4,16384]{3,2,1,0:T(4,128)(2,1)} %lesser_hbm.1, bf16[1,2,4,16384]{3,2,1,0:T(4,128)(2,1)} %greater_hbm.1), custom_call_target="tpu_custom_call" | custom-call | tf_op jit(solution)/shard_map/pallas_call | solution.py:80
  2.0 5.2 %all-to-all-start = ((bf16[8,4,4,2048]{3,2,1,0:T(4,128)(2,1)}), bf16[8,4,4,2048]{3,2,1,0:T(4,128)(2,1)S(1)}, u32[]{:S(2)}, u32[]{:S(2)}) async-start(bf16[8,4,4,2048]{3,2,1,0:T(4,128)(2,1)} %shard_map.46), calls=%async_computation | async-start | bytes 1048576 | tf_op jit(solution)/shard_map/all_to_all | solution.py:107
  7.2 0.2 fusion.21
  7.4 0.1 copy.8
  7.5 0.1 copy.9
  7.6 0.1 convert_element_type.77
  7.8 0.1 copy.10
  7.9 0.1 convert_element_type.79
  8.1 0.2 fusion.24
  8.3 0.1 maximum_maximum_fusion
  8.4 8.5 %all-to-all-done = bf16[8,4,4,2048]{3,2,1,0:T(4,128)(2,1)S(1)} async-done(((bf16[8,4,4,2048]{3,2,1,0:T(4,128)(2,1)}), bf16[8,4,4,2048]{3,2,1,0:T(4,128)(2,1)S(1)}, u32[]{:S(2)}, u32[]{:S(2)}) %all-to-all-start) | async-done | bytes 524320 | tf_op jit(solution)/shard_map/all_to_all | solution.py:107
  16.9 0.1 reshape.205
  17.0 0.5 fusion.26
  17.5 0.5 convolution_add_fusion
  17.9 0.1 multiply_add_fusion
  18.1 0.4 fusion
  18.5 12.2 %all_to_all.10 = f32[8,8,2048]{2,1,0:T(8,128)S(1)} all-to-all(f32[8,8,2048]{2,1,0:T(8,128)S(1)} %fusion), channel_id=1, replica_groups=mesh['energy'=8,'space'=4] {'energy'}, dimensions={0} | all-to-all | bytes 1048576 | tf_op jit(solution)/shard_map/all_to_all | solution.py:111
  30.7 0.0 copy-start.1
  30.7 0.3 copy.27
  31.0 0.1 reshape_reshape.6
  31.1 0.0 copy-done
  31.1 0.6 %convolution_bitcast_fusion = f32[2,4,128,128]{2,3,1,0:T(8,128)S(1)} fusion(f32[2,4,128,128]{3,2,1,0:T(8,128)S(1)} %reshape_reshape.6, f32[1,128,128]{2,1,0:T(8,128)S(1)} %copy-done), kind=kOutput, calls=%fused_computation.1 | convolution fusion | flops 100663296 | bytes 1114112 | tf_op jit(solution)/shard_map/dot_general | solution.py:59
  31.7 1.3 %collective-permute-start = (f32[8,8,2048]{2,1,0:T(8,128)S(1)}, f32[8,8,2048]{2,1,0:T(8,128)S(1)}, u32[]{:S(2)}, u32[]{:S(2)}) collective-permute-start(f32[8,8,2048]{2,1,0:T(8,128)S(1)} %all_to_all.10), channel_id=1, source_target_pairs={{1,0},{2,1},{3,2},{5,4},{6,5},{7,6},{9,8},{10,9},{11,10},{13,12},{... | collective-permute-start | bytes 1572872 | tf_op jit(solution)/shard_map/ppermute | solution.py:17
  33.0 0.6 %fusion.7 = f32[2,4,128,128]{3,2,1,0:T(8,128)S(1)} fusion(f32[2,4,128,128]{2,3,1,0:T(8,128)S(1)} %convolution_bitcast_fusion, f32[1,128,128]{2,1,0:T(8,128)S(1)} %copy-done), kind=kOutput, calls=%fused_computation.21 | convolution fusion | flops 100663296 | bytes 1114112 | tf_op jit(solution)/shard_map/dot_general | solution.py:60
  33.6 4.6 %collective-permute-start.1 = (f32[2,4,128,128]{3,2,1,0:T(8,128)S(1)}, f32[2,4,128,128]{3,2,1,0:T(8,128)S(1)}, u32[]{:S(2)}, u32[]{:S(2)}) collective-permute-start(f32[2,4,128,128]{3,2,1,0:T(8,128)S(1)} %fusion.7), channel_id=1, source_target_pairs={{0,1},{1,2},{2,3},{4,5},{5,6},{6,7},{8,9},{9,10},{10,11},{12,13},{... | collective-permute-start | bytes 1572872 | tf_op jit(solution)/shard_map/ppermute | solution.py:17
  38.1 0.0 copy-done.1
  38.2 0.6 %convolution_bitcast_fusion.2 = f32[2,4,128,128]{2,3,1,0:T(8,128)S(1)} fusion(f32[2,4,128,128]{3,2,1,0:T(8,128)S(1)} %reshape_reshape.6, f32[1,128,128]{2,1,0:T(8,128)S(1)} %copy-done.1), kind=kOutput, calls=%fused_computation.3 | convolution fusion | flops 100663296 | bytes 1114112 | tf_op jit(solution)/shard_map/dot_general | solution.py:59
  38.8 0.6 %fusion.4 = f32[2,4,128,128]{3,2,1,0:T(8,128)S(1)} fusion(f32[2,4,128,128]{2,3,1,0:T(8,128)S(1)} %convolution_bitcast_fusion.2, f32[1,128,128]{2,1,0:T(8,128)S(1)} %copy-done.1), kind=kOutput, calls=%fused_computation.18 | convolution fusion | flops 100663296 | bytes 1114112 | tf_op jit(solution)/shard_map/dot_general | solution.py:60
  39.4 7.2 %collective-permute-done = f32[8,8,2048]{2,1,0:T(8,128)S(1)} collective-permute-done((f32[8,8,2048]{2,1,0:T(8,128)S(1)}, f32[8,8,2048]{2,1,0:T(8,128)S(1)}, u32[]{:S(2)}, u32[]{:S(2)}) %collective-permute-start) | collective-permute-done | bytes 524320 | tf_op jit(solution)/shard_map/ppermute | solution.py:17
  46.6 0.3 copy.28
  46.9 0.1 reshape_reshape.7
  47.0 0.6 %convolution_bitcast_fusion.1 = f32[2,4,128,128]{2,3,1,0:T(8,128)S(1)} fusion(f32[2,4,128,128]{3,2,1,0:T(8,128)S(1)} %reshape_reshape.7, f32[1,128,128]{2,1,0:T(8,128)S(1)} %copy-done), kind=kOutput, calls=%fused_computation.2 | convolution fusion | flops 100663296 | bytes 1114112 | tf_op jit(solution)/shard_map/dot_general | solution.py:59
  47.6 0.6 %convolution_add_fusion.1 = f32[2,4,128,128]{3,2,1,0:T(8,128)S(1)} fusion(f32[2,4,128,128]{3,2,1,0:T(8,128)S(1)} %fusion.4, f32[2,4,128,128]{2,3,1,0:T(8,128)S(1)} %convolution_bitcast_fusion.1, f32[1,128,128]{2,1,0:T(8,128)S(1)} %copy-done), kind=kOutput, calls=%fused_computation.4 | convolution fusion | flops 100794368 | bytes 1638400 | tf_op jit(solution)/shard_map/dot_general | solution.py:60
  48.2 0.2 reshape.208
  48.4 0.0 collective-permute-done.1
  48.4 0.2 reshape.209
  48.6 0.9 %add.85 = f32[1,2,4,16384]{3,2,1,0:T(4,128)} add(f32[1,2,4,16384]{3,2,1,0:T(4,128)S(1)} %reshape.208, f32[1,2,4,16384]{3,2,1,0:T(4,128)S(1)} %reshape.209) | non-fusion elementwise | flops 131072 | bytes 1572864 | tf_op jit(solution)/shard_map/add | solution.py:129
  (4 shorter events, 0.1 us)
Async XLA Ops:
  0.0 31.1 %copy-start = (f32[1,128,128]{2,1,0:T(8,128)S(1)}, f32[1,128,128]{2,1,0:T(8,128)}, u32[]{:S(2)}) copy-start(f32[1,128,128]{2,1,0:T(8,128)} %param.7) | copy-start | bytes 196612
  2.0 14.9 %all-to-all-start = ((bf16[8,4,4,2048]{3,2,1,0:T(4,128)(2,1)}), bf16[8,4,4,2048]{3,2,1,0:T(4,128)(2,1)S(1)}, u32[]{:S(2)}, u32[]{:S(2)}) async-start(bf16[8,4,4,2048]{3,2,1,0:T(4,128)(2,1)} %shard_map.46), calls=%async_computation | async-start | bytes 1048576 | tf_op jit(solution)/shard_map/all_to_all | solution.py:107
  30.7 7.5 %copy-start.1 = (f32[1,128,128]{2,1,0:T(8,128)S(1)}, f32[1,128,128]{2,1,0:T(8,128)}, u32[]{:S(2)}) copy-start(f32[1,128,128]{2,1,0:T(8,128)} %param.6) | copy-start | bytes 196612
  31.7 14.9 %collective-permute-start = (f32[8,8,2048]{2,1,0:T(8,128)S(1)}, f32[8,8,2048]{2,1,0:T(8,128)S(1)}, u32[]{:S(2)}, u32[]{:S(2)}) collective-permute-start(f32[8,8,2048]{2,1,0:T(8,128)S(1)} %all_to_all.10), channel_id=1, source_target_pairs={{1,0},{2,1},{3,2},{5,4},{6,5},{7,6},{9,8},{10,9},{11,10},{13,12},{... | collective-permute-start | bytes 1572872 | tf_op jit(solution)/shard_map/ppermute | solution.py:17
  33.6 14.8 %collective-permute-start.1 = (f32[2,4,128,128]{3,2,1,0:T(8,128)S(1)}, f32[2,4,128,128]{3,2,1,0:T(8,128)S(1)}, u32[]{:S(2)}, u32[]{:S(2)}) collective-permute-start(f32[2,4,128,128]{3,2,1,0:T(8,128)S(1)} %fusion.7), channel_id=1, source_target_pairs={{0,1},{1,2},{2,3},{4,5},{5,6},{6,7},{8,9},{9,10},{10,11},{12,13},{... | collective-permute-start | bytes 1572872 | tf_op jit(solution)/shard_map/ppermute | solution.py:17

commit v11 on v10

--- a/solution.py
+++ b/solution.py
@@ -63,13 +63,13 @@
 def by_destination(g_lesser, g_greater, groups, tile_width):
     e_local = g_lesser.shape[2]
 
-    def kernel(lesser_hbm, greater_hbm, out_ref, sems):
+    def kernel(lesser_hbm, greater_hbm, out_hbm, sems):
         copies = []
         for dest in range(groups):
             for which, ref in enumerate((lesser_hbm, greater_hbm)):
                 copy = pltpu.make_async_copy(
                     ref.at[0, :, :, pl.ds(dest * tile_width, tile_width)],
-                    out_ref.at[dest, pl.ds(2 * which, 2)],
+                    out_hbm.at[dest, pl.ds(2 * which, 2)],
                     sems.at[dest * 2 + which],
                 )
                 copy.start()
@@ -81,7 +81,7 @@
         kernel,
         out_shape=jax.ShapeDtypeStruct((groups, 4, e_local, tile_width), g_lesser.dtype),
         in_specs=[pl.BlockSpec(memory_space=pl.ANY)] * 2,
-        out_specs=pl.BlockSpec(memory_space=pltpu.VMEM),
+        out_specs=pl.BlockSpec(memory_space=pl.ANY),
         scratch_shapes=[pltpu.SemaphoreType.DMA((2 * groups,))],
     )(g_lesser, g_greater)
 

time: 49.9 us -> 65 us (1.30)
  Pallas kernels: 1.96 us -> 17.1 us
    pallas_call x1, Pallas kernels: 1.96 us -> 17.1 us  [by_destination(): pl.pallas_call(kernel, out_shape=jax.ShapeDtypeStruct((groups, 4, e_local...]
  transfers between devices with their start and end apart: 3 -> 3, of which waited for: 2 -> 2; matrix products, arithmetic and copies ran while one was open for 10% -> 7% of each run, Pallas kernels for 0% -> 0%
where the time goes in v11:
time: 65 us; the launch traced here: 64.7 us
  Pallas kernels  17.1 us (26%)
  waiting for transfers between devices  15.7 us (24%)
  blocking collectives  12.2 us (19%)
  starting transfers between devices  11.1 us (17%)
  matrix products  4.84 us (7%)
  local copies, waits for them, and re-layouts  2.01 us (3%)
  other arithmetic  1.6 us (2%)
    pallas_call x1, Pallas kernels, by_destination(): pl.pallas_call(kernel, out_shape=jax.ShapeDtypeStruct((groups, 4, e_local...  17.1 us
    all_to_all x1, blocking collectives, per_device(): back = lax.all_to_all(send, 'energy', 0, 0, tiled=True)  12.2 us
    all_to_all x1, waiting for transfers between devices, per_device(): got = lax.all_to_all(both, 'energy', 0, 0, tiled=True)  8.5 us
    ppermute x2, waiting for transfers between devices, shifted(): return lax.ppermute(x, axis, pairs)  7.22 us
    ppermute x2, starting transfers between devices, shifted(): return lax.ppermute(x, axis, pairs)  5.87 us
    all_to_all x1, starting transfers between devices, per_device(): got = lax.all_to_all(both, 'energy', 0, 0, tiled=True)  5.18 us
    dot_general x3, matrix products, sandwich(): return jnp.matmul(inner, right, precision=lax.Precision.HIGH)  1.77 us
    dot_general x3, matrix products, sandwich(): inner = jnp.matmul(left, field, precision=lax.Precision.HIGH)  1.76 us
  transfers between devices with their start and end apart: 3, of which 2 were waited for; matrix products, arithmetic and copies ran while one was open for 7% of the time, Pallas kernels for 0%

profile of v11, /device:TPU:0, one launch (start us, length us, event | category | flops | bytes accessed | tf_op | source)
XLA Modules:
  0.0 64.7 jit_solution(6428107670018554883)
XLA Ops:
  0.0 0.0 copy-start
  0.0 17.1 %shard_map.46 = bf16[8,4,4,2048]{3,2,1,0:T(4,128)(2,1)} custom-call(bf16[1,2,4,16384]{3,2,1,0:T(4,128)(2,1)} %lesser_hbm.1, bf16[1,2,4,16384]{3,2,1,0:T(4,128)(2,1)} %greater_hbm.1), custom_call_target="tpu_custom_call" | custom-call | tf_op jit(solution)/shard_map/pallas_call | solution.py:80
  17.1 5.2 %all-to-all-start = ((bf16[8,4,4,2048]{3,2,1,0:T(4,128)(2,1)}), bf16[8,4,4,2048]{3,2,1,0:T(4,128)(2,1)S(1)}, u32[]{:S(2)}, u32[]{:S(2)}) async-start(bf16[8,4,4,2048]{3,2,1,0:T(4,128)(2,1)} %shard_map.46), calls=%async_computation | async-start | bytes 1048576 | tf_op jit(solution)/shard_map/all_to_all | solution.py:107
  22.3 0.2 fusion.21
  22.5 0.1 copy.8
  22.7 0.1 copy.9
  22.8 0.1 convert_element_type.77
  23.0 0.1 copy.10
  23.1 0.1 convert_element_type.79
  23.2 0.2 fusion.24
  23.5 0.1 maximum_maximum_fusion
  23.6 8.5 %all-to-all-done = bf16[8,4,4,2048]{3,2,1,0:T(4,128)(2,1)S(1)} async-done(((bf16[8,4,4,2048]{3,2,1,0:T(4,128)(2,1)}), bf16[8,4,4,2048]{3,2,1,0:T(4,128)(2,1)S(1)}, u32[]{:S(2)}, u32[]{:S(2)}) %all-to-all-start) | async-done | bytes 524320 | tf_op jit(solution)/shard_map/all_to_all | solution.py:107
  32.1 0.1 reshape.205
  32.2 0.5 fusion.26
  32.6 0.5 convolution_add_fusion
  33.1 0.1 multiply_add_fusion
  33.3 0.4 fusion
  33.7 12.2 %all_to_all.10 = f32[8,8,2048]{2,1,0:T(8,128)S(1)} all-to-all(f32[8,8,2048]{2,1,0:T(8,128)S(1)} %fusion), channel_id=1, replica_groups=mesh['energy'=8,'space'=4] {'energy'}, dimensions={0} | all-to-all | bytes 1048576 | tf_op jit(solution)/shard_map/all_to_all | solution.py:111
  45.8 0.0 copy-start.1
  45.8 0.3 copy.27
  46.1 0.1 reshape_reshape.6
  46.2 0.0 copy-done
  46.2 0.6 convolution_bitcast_fusion
  46.8 1.3 %collective-permute-start = (f32[8,8,2048]{2,1,0:T(8,128)S(1)}, f32[8,8,2048]{2,1,0:T(8,128)S(1)}, u32[]{:S(2)}, u32[]{:S(2)}) collective-permute-start(f32[8,8,2048]{2,1,0:T(8,128)S(1)} %all_to_all.10), channel_id=1, source_target_pairs={{1,0},{2,1},{3,2},{5,4},{6,5},{7,6},{9,8},{10,9},{11,10},{13,12},{... | collective-permute-start | bytes 1572872 | tf_op jit(solution)/shard_map/ppermute | solution.py:17
  48.1 0.6 fusion.7
  48.7 4.6 %collective-permute-start.1 = (f32[2,4,128,128]{3,2,1,0:T(8,128)S(1)}, f32[2,4,128,128]{3,2,1,0:T(8,128)S(1)}, u32[]{:S(2)}, u32[]{:S(2)}) collective-permute-start(f32[2,4,128,128]{3,2,1,0:T(8,128)S(1)} %fusion.7), channel_id=1, source_target_pairs={{0,1},{1,2},{2,3},{4,5},{5,6},{6,7},{8,9},{9,10},{10,11},{12,13},{... | collective-permute-start | bytes 1572872 | tf_op jit(solution)/shard_map/ppermute | solution.py:17
  53.3 0.0 copy-done.1
  53.3 0.6 convolution_bitcast_fusion.2
  53.9 0.6 fusion.4
  54.5 7.2 %collective-permute-done = f32[8,8,2048]{2,1,0:T(8,128)S(1)} collective-permute-done((f32[8,8,2048]{2,1,0:T(8,128)S(1)}, f32[8,8,2048]{2,1,0:T(8,128)S(1)}, u32[]{:S(2)}, u32[]{:S(2)}) %collective-permute-start) | collective-permute-done | bytes 524320 | tf_op jit(solution)/shard_map/ppermute | solution.py:17
  61.7 0.3 copy.28
  62.0 0.1 reshape_reshape.7
  62.1 0.6 convolution_bitcast_fusion.1
  62.7 0.6 convolution_add_fusion.1
  63.3 0.2 reshape.208
  63.6 0.0 collective-permute-done.1
  63.6 0.2 reshape.209
  63.8 0.9 %add.85 = f32[1,2,4,16384]{3,2,1,0:T(4,128)} add(f32[1,2,4,16384]{3,2,1,0:T(4,128)S(1)} %reshape.208, f32[1,2,4,16384]{3,2,1,0:T(4,128)S(1)} %reshape.209) | non-fusion elementwise | flops 131072 | bytes 1572864 | tf_op jit(solution)/shard_map/add | solution.py:129
  (4 shorter events, 0.1 us)
Async XLA Ops:
  0.0 46.2 %copy-start = (f32[1,128,128]{2,1,0:T(8,128)S(1)}, f32[1,128,128]{2,1,0:T(8,128)}, u32[]{:S(2)}) copy-start(f32[1,128,128]{2,1,0:T(8,128)} %param.7) | copy-start | bytes 196612
  17.1 14.9 %all-to-all-start = ((bf16[8,4,4,2048]{3,2,1,0:T(4,128)(2,1)}), bf16[8,4,4,2048]{3,2,1,0:T(4,128)(2,1)S(1)}, u32[]{:S(2)}, u32[]{:S(2)}) async-start(bf16[8,4,4,2048]{3,2,1,0:T(4,128)(2,1)} %shard_map.46), calls=%async_computation | async-start | bytes 1048576 | tf_op jit(solution)/shard_map/all_to_all | solution.py:107
  45.8 7.5 %copy-start.1 = (f32[1,128,128]{2,1,0:T(8,128)S(1)}, f32[1,128,128]{2,1,0:T(8,128)}, u32[]{:S(2)}) copy-start(f32[1,128,128]{2,1,0:T(8,128)} %param.6) | copy-start | bytes 196612
  46.8 14.9 %collective-permute-start = (f32[8,8,2048]{2,1,0:T(8,128)S(1)}, f32[8,8,2048]{2,1,0:T(8,128)S(1)}, u32[]{:S(2)}, u32[]{:S(2)}) collective-permute-start(f32[8,8,2048]{2,1,0:T(8,128)S(1)} %all_to_all.10), channel_id=1, source_target_pairs={{1,0},{2,1},{3,2},{5,4},{6,5},{7,6},{9,8},{10,9},{11,10},{13,12},{... | collective-permute-start | bytes 1572872 | tf_op jit(solution)/shard_map/ppermute | solution.py:17
  48.7 14.8 %collective-permute-start.1 = (f32[2,4,128,128]{3,2,1,0:T(8,128)S(1)}, f32[2,4,128,128]{3,2,1,0:T(8,128)S(1)}, u32[]{:S(2)}, u32[]{:S(2)}) collective-permute-start(f32[2,4,128,128]{3,2,1,0:T(8,128)S(1)} %fusion.7), channel_id=1, source_target_pairs={{0,1},{1,2},{2,3},{4,5},{5,6},{6,7},{8,9},{9,10},{10,11},{12,13},{... | collective-permute-start | bytes 1572872 | tf_op jit(solution)/shard_map/ppermute | solution.py:17

commit v12 on v10

--- a/solution.py
+++ b/solution.py
@@ -42,17 +42,41 @@
     return forward, inverse
 
 
+def split_bf16(table):
+    high = lax.reduce_precision(table, exponent_bits=8, mantissa_bits=7)
+    return high.astype(jnp.bfloat16), (table - high).astype(jnp.bfloat16)
+
+
 def correlate(got, forward, inverse):
-    high = lax.reduce_precision(forward, exponent_bits=8, mantissa_bits=7)
-    low = forward - high
-    spectrum = jnp.dot(high.astype(jnp.bfloat16), got, preferred_element_type=jnp.float32)
-    spectrum = spectrum + jnp.dot(low.astype(jnp.bfloat16), got, preferred_element_type=jnp.float32)
     length = forward.shape[0] // 4
-    l_re, l_im, g_re, g_im = (spectrum[i * length:(i + 1) * length] for i in range(4))
-    z_re = l_re * g_re + l_im * g_im
-    z_im = l_im * g_re - l_re * g_im
-    z = jnp.concatenate([z_re, z_im])
-    return jnp.dot(inverse, z, precision=lax.Precision.HIGH, preferred_element_type=jnp.float32)
+    f_hi, f_lo = split_bf16(forward)
+    re_hi, re_lo = split_bf16(inverse[:, :length])
+    im_hi, im_lo = split_bf16(inverse[:, length:])
+
+    def kernel(y_ref, f_hi_ref, f_lo_ref, re_hi_ref, re_lo_ref, im_hi_ref, im_lo_ref, o_ref):
+        y = y_ref[...]
+        spectrum = jnp.dot(f_hi_ref[...], y, preferred_element_type=jnp.float32)
+        spectrum = spectrum + jnp.dot(f_lo_ref[...], y, preferred_element_type=jnp.float32)
+        l_re, l_im, g_re, g_im = (spectrum[i * length:(i + 1) * length] for i in range(4))
+        z_re = l_re * g_re + l_im * g_im
+        z_im = l_im * g_re - l_re * g_im
+        total = None
+        for z, hi_ref, lo_ref in ((z_re, re_hi_ref, re_lo_ref), (z_im, im_hi_ref, im_lo_ref)):
+            z_hi = z.astype(jnp.bfloat16)
+            z_lo = (z - z_hi.astype(jnp.float32)).astype(jnp.bfloat16)
+            hi = hi_ref[...]
+            part = jnp.dot(hi, z_hi, preferred_element_type=jnp.float32)
+            part = part + jnp.dot(hi, z_lo, preferred_element_type=jnp.float32)
+            part = part + jnp.dot(lo_ref[...], z_hi, preferred_element_type=jnp.float32)
+            total = part if total is None else total + part
+        o_ref[...] = total
+
+    return pl.pallas_call(
+        kernel,
+        out_shape=jax.ShapeDtypeStruct((inverse.shape[0], got.shape[1]), jnp.float32),
+        in_specs=[pl.BlockSpec(memory_space=pltpu.VMEM)] * 7,
+        out_specs=pl.BlockSpec(memory_space=pltpu.VMEM),
+    )(got, f_hi, f_lo, re_hi, re_lo, im_hi, im_lo)
 
 
 def sandwich(left, field, right):

time: 49.9 us -> 53.5 us (1.072)
  Pallas kernels: 1.96 us -> 5.08 us
  matrix products: 4.84 us -> 3.53 us
  waiting for transfers between devices: 15.7 us -> 14.4 us
  other arithmetic: 1.6 us -> 2.79 us
  blocking collectives: 12.2 us -> 13.1 us
  local copies, waits for them, and re-layouts: 2.01 us -> 2.79 us
    pallas_call x0 -> x1, Pallas kernels: none -> 3.12 us  [correlate(): pl.pallas_call(kernel, out_shape=jax.ShapeDtypeStruct((inverse.shape[0],...]
    convert_element_type x1 -> x2, other arithmetic: 0.05 us -> 1.37 us  [split_bf16(): return (high.astype(jnp.bfloat16), (table - high).astype(jnp.bfloat16))]
    all_to_all x1, waiting for transfers between devices: 8.5 us -> 7.19 us  [per_device(): got = lax.all_to_all(both, 'energy', 0, 0, tiled=True)]
    dot_general x3 -> x0, matrix products: 1.31 us -> none  [the longest x1 0.46 us: correlate(): jnp.dot(low.astype(jnp.bfloat16), got, preferred_element_type=jnp.float32)]
    all_to_all x1, blocking collectives: 12.2 us -> 13.1 us  [per_device(): back = lax.all_to_all(send, 'energy', 0, 0, tiled=True)]
    reshape x1, local copies, waits for them, and re-layouts: 0.12 us -> 0.91 us  [per_device(): got.reshape(groups * 4 * e_local, tile_width)]
    convert_element_type x4 -> x0, local copies, waits for them, and re-layouts: 0.57 us -> none  [the longest x2 0.28 us: correlate(): high.astype(jnp.bfloat16)]
  transfers between devices with their start and end apart: 3 -> 3, of which waited for: 2 -> 2; matrix products, arithmetic and copies ran while one was open for 10% -> 11% of each run, Pallas kernels for 0% -> 0%
where the time goes in v12:
time: 53.5 us; the launch traced here: 53.1 us
  waiting for transfers between devices  14.4 us (27%)
  blocking collectives  13.1 us (24%)
  starting transfers between devices  11.2 us (21%)
  Pallas kernels  5.08 us (9%)
  matrix products  3.53 us (7%)
  local copies, waits for them, and re-layouts  2.79 us (5%)
  other arithmetic  2.79 us (5%)
    all_to_all x1, blocking collectives, per_device(): back = lax.all_to_all(send, 'energy', 0, 0, tiled=True)  13.1 us
    ppermute x2, waiting for transfers between devices, shifted(): return lax.ppermute(x, axis, pairs)  7.22 us
    all_to_all x1, waiting for transfers between devices, per_device(): got = lax.all_to_all(both, 'energy', 0, 0, tiled=True)  7.19 us
    ppermute x2, starting transfers between devices, shifted(): return lax.ppermute(x, axis, pairs)  6 us
    all_to_all x1, starting transfers between devices, per_device(): got = lax.all_to_all(both, 'energy', 0, 0, tiled=True)  5.18 us
    pallas_call x1, Pallas kernels, correlate(): pl.pallas_call(kernel, out_shape=jax.ShapeDtypeStruct((inverse.shape[0],...  3.12 us
    pallas_call x1, Pallas kernels, by_destination(): pl.pallas_call(kernel, out_shape=jax.ShapeDtypeStruct((groups, 4, e_local...  1.96 us
    dot_general x3, matrix products, sandwich(): return jnp.matmul(inner, right, precision=lax.Precision.HIGH)  1.77 us
  transfers between devices with their start and end apart: 3, of which 2 were waited for; matrix products, arithmetic and copies ran while one was open for 11% of the time, Pallas kernels for 0%

profile of v12, /device:TPU:0, one launch (start us, length us, event | category | flops | bytes accessed | tf_op | source)
XLA Modules:
  0.0 53.1 jit_solution(12628811579610903276)
XLA Ops:
  0.0 0.0 copy-start
  0.0 2.0 %shard_map.46 = bf16[8,4,4,2048]{3,2,1,0:T(4,128)(2,1)} custom-call(bf16[1,2,4,16384]{3,2,1,0:T(4,128)(2,1)} %lesser_hbm.1, bf16[1,2,4,16384]{3,2,1,0:T(4,128)(2,1)} %greater_hbm.1), custom_call_target="tpu_custom_call" | custom-call | tf_op jit(solution)/shard_map/pallas_call | solution.py:104
  2.0 5.2 %all-to-all-start = ((bf16[8,4,4,2048]{3,2,1,0:T(4,128)(2,1)}), bf16[8,4,4,2048]{3,2,1,0:T(4,128)(2,1)S(1)}, u32[]{:S(2)}, u32[]{:S(2)}) async-start(bf16[8,4,4,2048]{3,2,1,0:T(4,128)(2,1)} %shard_map.46), calls=%async_computation | async-start | bytes 1048576 | tf_op jit(solution)/shard_map/all_to_all | solution.py:131
  7.2 0.2 fusion.20
  7.3 0.1 copy.13
  7.4 0.2 fusion.23
  7.7 0.1 maximum_maximum_fusion
  7.8 0.2 copy.10
  8.0 0.3 reshape.196
  8.2 0.1 copy.11
  8.3 0.7 %fusion.10 = (bf16[64,64]{1,0:T(8,128)(2,1)}, bf16[64,64]{1,0:T(8,128)(2,1)}, bf16[64,64]{1,0:T(8,128)(2,1)}, bf16[64,64]{1,0:T(8,128)(2,1)}) fusion(f32[64,128]{1,0:T(8,128)S(1)} %bitcast.65), kind=kLoop, calls=%fused_computation.24 | loop fusion | flops 32768 | bytes 65536 | tf_op jit(solution)/shard_map/convert_element_type | solution.py:47
  9.0 0.7 %fusion = (bf16[256,128]{1,0:T(8,128)(2,1)}, bf16[256,128]{1,0:T(8,128)(2,1)}) fusion(f32[256,128]{1,0:T(8,128)S(1)} %copy.11), kind=kLoop, calls=%fused_computation.7 | loop fusion | flops 131072 | bytes 262144 | tf_op jit(solution)/shard_map/convert_element_type | solution.py:47
  9.7 7.2 %all-to-all-done = bf16[8,4,4,2048]{3,2,1,0:T(4,128)(2,1)S(1)} async-done(((bf16[8,4,4,2048]{3,2,1,0:T(4,128)(2,1)}), bf16[8,4,4,2048]{3,2,1,0:T(4,128)(2,1)S(1)}, u32[]{:S(2)}, u32[]{:S(2)}) %all-to-all-start) | async-done | bytes 524320 | tf_op jit(solution)/shard_map/all_to_all | solution.py:131
  16.9 0.9 %reshape.195.y_ref = bf16[128,2048]{1,0:T(8,128)(2,1)} reshape(bf16[8,4,4,2048]{3,2,1,0:T(4,128)(2,1)S(1)} %all-to-all-done) | data formatting | bytes 1048576 | tf_op jit(solution)/shard_map/reshape | solution.py:132
  17.8 3.1 %shard_map.47 = f32[64,2048]{1,0:T(8,128)} custom-call(bf16[128,2048]{1,0:T(8,128)(2,1)} %reshape.195.y_ref, bf16[256,128]{1,0:T(8,128)(2,1)} %get-tuple-element.10.f_hi_ref, bf16[256,128]{1,0:T(8,128)(2,1)} %get-tuple-element.9.f_lo_ref, bf16[64,64]{1,0:T(8,128)(2,1)} %get-tuple-element.16.re_hi_ref, bf16[64,64]{1,0:T(8,128)(2,1)} %get-tuple-element.14.re_lo_ref, ...), custom_call_target="tpu_custom_call" | custom-call | tf_op jit(solution)/shard_map/pallas_call | solution.py:74
  20.9 13.1 %all_to_all.10 = f32[8,8,2048]{2,1,0:T(8,128)S(1)} all-to-all(f32[8,8,2048]{2,1,0:T(8,128)} %bitcast.62), channel_id=1, replica_groups=mesh['energy'=8,'space'=4] {'energy'}, dimensions={0} | all-to-all | bytes 1048576 | tf_op jit(solution)/shard_map/all_to_all | solution.py:135
  34.1 0.3 copy.14
  34.4 0.1 reshape_reshape.6
  34.5 0.0 copy-done
  34.5 0.6 %convolution_bitcast_fusion = f32[2,4,128,128]{2,3,1,0:T(8,128)S(1)} fusion(f32[2,4,128,128]{3,2,1,0:T(8,128)S(1)} %reshape_reshape.6, f32[1,128,128]{2,1,0:T(8,128)S(1)} %copy-done), kind=kOutput, calls=%fused_computation | convolution fusion | flops 100663296 | bytes 1114112 | tf_op jit(solution)/shard_map/dot_general | solution.py:83
  35.1 0.0 copy-start.1
  35.1 1.4 %collective-permute-start = (f32[8,8,2048]{2,1,0:T(8,128)S(1)}, f32[8,8,2048]{2,1,0:T(8,128)S(1)}, u32[]{:S(2)}, u32[]{:S(2)}) collective-permute-start(f32[8,8,2048]{2,1,0:T(8,128)S(1)} %all_to_all.10), channel_id=1, source_target_pairs={{1,0},{2,1},{3,2},{5,4},{6,5},{7,6},{9,8},{10,9},{11,10},{13,12},{... | collective-permute-start | bytes 1572872 | tf_op jit(solution)/shard_map/ppermute | solution.py:17
  36.5 0.6 %fusion.4 = f32[2,4,128,128]{3,2,1,0:T(8,128)S(1)} fusion(f32[2,4,128,128]{2,3,1,0:T(8,128)S(1)} %convolution_bitcast_fusion, f32[1,128,128]{2,1,0:T(8,128)S(1)} %copy-done), kind=kOutput, calls=%fused_computation.14 | convolution fusion | flops 100663296 | bytes 1114112 | tf_op jit(solution)/shard_map/dot_general | solution.py:84
  37.1 4.6 %collective-permute-start.1 = (f32[2,4,128,128]{3,2,1,0:T(8,128)S(1)}, f32[2,4,128,128]{3,2,1,0:T(8,128)S(1)}, u32[]{:S(2)}, u32[]{:S(2)}) collective-permute-start(f32[2,4,128,128]{3,2,1,0:T(8,128)S(1)} %fusion.4), channel_id=1, source_target_pairs={{0,1},{1,2},{2,3},{4,5},{5,6},{6,7},{8,9},{9,10},{10,11},{12,13},{... | collective-permute-start | bytes 1572872 | tf_op jit(solution)/shard_map/ppermute | solution.py:17
  41.7 0.0 copy-done.1
  41.7 0.6 %convolution_bitcast_fusion.2 = f32[2,4,128,128]{2,3,1,0:T(8,128)S(1)} fusion(f32[2,4,128,128]{3,2,1,0:T(8,128)S(1)} %reshape_reshape.6, f32[1,128,128]{2,1,0:T(8,128)S(1)} %copy-done.1), kind=kOutput, calls=%fused_computation.2 | convolution fusion | flops 100663296 | bytes 1114112 | tf_op jit(solution)/shard_map/dot_general | solution.py:83
  42.3 0.6 %fusion.1 = f32[2,4,128,128]{3,2,1,0:T(8,128)S(1)} fusion(f32[2,4,128,128]{2,3,1,0:T(8,128)S(1)} %convolution_bitcast_fusion.2, f32[1,128,128]{2,1,0:T(8,128)S(1)} %copy-done.1), kind=kOutput, calls=%fused_computation.11 | convolution fusion | flops 100663296 | bytes 1114112 | tf_op jit(solution)/shard_map/dot_general | solution.py:84
  42.9 7.2 %collective-permute-done = f32[8,8,2048]{2,1,0:T(8,128)S(1)} collective-permute-done((f32[8,8,2048]{2,1,0:T(8,128)S(1)}, f32[8,8,2048]{2,1,0:T(8,128)S(1)}, u32[]{:S(2)}, u32[]{:S(2)}) %collective-permute-start) | collective-permute-done | bytes 524320 | tf_op jit(solution)/shard_map/ppermute | solution.py:17
  50.1 0.3 copy.17
  50.4 0.1 reshape_reshape.7
  50.5 0.6 %convolution_bitcast_fusion.1 = f32[2,4,128,128]{2,3,1,0:T(8,128)S(1)} fusion(f32[2,4,128,128]{3,2,1,0:T(8,128)S(1)} %reshape_reshape.7, f32[1,128,128]{2,1,0:T(8,128)S(1)} %copy-done), kind=kOutput, calls=%fused_computation.1 | convolution fusion | flops 100663296 | bytes 1114112 | tf_op jit(solution)/shard_map/dot_general | solution.py:83
  51.1 0.6 %convolution_add_fusion = f32[2,4,128,128]{3,2,1,0:T(8,128)S(1)} fusion(f32[2,4,128,128]{3,2,1,0:T(8,128)S(1)} %fusion.1, f32[2,4,128,128]{2,3,1,0:T(8,128)S(1)} %convolution_bitcast_fusion.1, f32[1,128,128]{2,1,0:T(8,128)S(1)} %copy-done), kind=kOutput, calls=%fused_computation.3 | convolution fusion | flops 100794368 | bytes 1638400 | tf_op jit(solution)/shard_map/dot_general | solution.py:84
  51.7 0.2 reshape.201
  52.0 0.0 collective-permute-done.1
  52.0 0.2 reshape.202
  52.2 0.9 %add.77 = f32[1,2,4,16384]{3,2,1,0:T(4,128)} add(f32[1,2,4,16384]{3,2,1,0:T(4,128)S(1)} %reshape.201, f32[1,2,4,16384]{3,2,1,0:T(4,128)S(1)} %reshape.202) | non-fusion elementwise | flops 131072 | bytes 1572864 | tf_op jit(solution)/shard_map/add | solution.py:153
  (4 shorter events, 0.1 us)
Async XLA Ops:
  0.0 34.5 %copy-start = (f32[1,128,128]{2,1,0:T(8,128)S(1)}, f32[1,128,128]{2,1,0:T(8,128)}, u32[]{:S(2)}) copy-start(f32[1,128,128]{2,1,0:T(8,128)} %param.7) | copy-start | bytes 196612
  2.0 14.9 %all-to-all-start = ((bf16[8,4,4,2048]{3,2,1,0:T(4,128)(2,1)}), bf16[8,4,4,2048]{3,2,1,0:T(4,128)(2,1)S(1)}, u32[]{:S(2)}, u32[]{:S(2)}) async-start(bf16[8,4,4,2048]{3,2,1,0:T(4,128)(2,1)} %shard_map.46), calls=%async_computation | async-start | bytes 1048576 | tf_op jit(solution)/shard_map/all_to_all | solution.py:131
  35.1 6.6 %copy-start.1 = (f32[1,128,128]{2,1,0:T(8,128)S(1)}, f32[1,128,128]{2,1,0:T(8,128)}, u32[]{:S(2)}) copy-start(f32[1,128,128]{2,1,0:T(8,128)} %param.6) | copy-start | bytes 196612
  35.1 15.0 %collective-permute-start = (f32[8,8,2048]{2,1,0:T(8,128)S(1)}, f32[8,8,2048]{2,1,0:T(8,128)S(1)}, u32[]{:S(2)}, u32[]{:S(2)}) collective-permute-start(f32[8,8,2048]{2,1,0:T(8,128)S(1)} %all_to_all.10), channel_id=1, source_target_pairs={{1,0},{2,1},{3,2},{5,4},{6,5},{7,6},{9,8},{10,9},{11,10},{13,12},{... | collective-permute-start | bytes 1572872 | tf_op jit(solution)/shard_map/ppermute | solution.py:17
  37.1 14.8 %collective-permute-start.1 = (f32[2,4,128,128]{3,2,1,0:T(8,128)S(1)}, f32[2,4,128,128]{3,2,1,0:T(8,128)S(1)}, u32[]{:S(2)}, u32[]{:S(2)}) collective-permute-start(f32[2,4,128,128]{3,2,1,0:T(8,128)S(1)} %fusion.4), channel_id=1, source_target_pairs={{0,1},{1,2},{2,3},{4,5},{5,6},{6,7},{8,9},{9,10},{10,11},{12,13},{... | collective-permute-start | bytes 1572872 | tf_op jit(solution)/shard_map/ppermute | solution.py:17

commit v13 on v10

--- a/solution.py
+++ b/solution.py
@@ -119,9 +119,11 @@
     polar = as_blocks(back)
     polar_above = as_blocks(back_above)
     diag_block = v_diag[0]
-    to_next = sandwich(couple_own.T, polar, couple_own)
+    lefts = jnp.stack([couple_own.T, diag_block])
+    inner = jnp.einsum("sij,abjk->sabik", lefts, polar, precision=lax.Precision.HIGH)
+    to_next = jnp.matmul(inner[0], couple_own, precision=lax.Precision.HIGH)
     from_below = shifted(to_next, "space", 1)
-    local = sandwich(diag_block, polar, diag_block)
+    local = jnp.matmul(inner[1], diag_block, precision=lax.Precision.HIGH)
     from_above = sandwich(couple_own, polar_above, couple_own.T)
     shape = (1, 2, e_local, elements)
     partial = (local + from_above).reshape(shape)

time: 49.9 us -> 51.2 us (1.026)
  the two profiles are of different devices: /device:TPU:0 before, /device:TPU:26 now
where the time goes in v13:
time: 51.2 us; the launch traced here: 50.8 us
  waiting for transfers between devices  27 us (53%)
  starting transfers between devices  12.8 us (25%)
  matrix products  5.09 us (10%)
  local copies, waits for them, and re-layouts  2.1 us (4%)
  Pallas kernels  1.93 us (4%)
  other arithmetic  1.6 us (3%)
    ppermute x2, waiting for transfers between devices, shifted(): return lax.ppermute(x, axis, pairs)  11.8 us
    all_to_all x1, waiting for transfers between devices, per_device(): back = lax.all_to_all(send, 'energy', 0, 0, tiled=True)  8.2 us
    all_to_all x1, waiting for transfers between devices, per_device(): got = lax.all_to_all(both, 'energy', 0, 0, tiled=True)  7.04 us
    all_to_all x1, starting transfers between devices, per_device(): back = lax.all_to_all(send, 'energy', 0, 0, tiled=True)  4.87 us
    all_to_all x1, starting transfers between devices, per_device(): got = lax.all_to_all(both, 'energy', 0, 0, tiled=True)  4.27 us
    ppermute x2, starting transfers between devices, shifted(): return lax.ppermute(x, axis, pairs)  3.68 us
    pallas_call x1, Pallas kernels, by_destination(): pl.pallas_call(kernel, out_shape=jax.ShapeDtypeStruct((groups, 4, e_local...  1.93 us
    dot_general x1, matrix products, correlate(): jnp.dot(inverse, z, precision=lax.Precision.HIGH, preferred_element_type=...  1.2 us
  transfers between devices with their start and end apart: 4, of which 4 were waited for; matrix products, arithmetic and copies ran while one was open for 10% of the time, Pallas kernels for 0%

profile of v13, /device:TPU:26, one launch (start us, length us, event | category | flops | bytes accessed | tf_op | source)
XLA Modules:
  0.0 50.8 jit_solution(14290933914303986006)
XLA Ops:
  0.0 1.9 %shard_map.46 = bf16[8,4,4,2048]{3,2,1,0:T(4,128)(2,1)} custom-call(bf16[1,2,4,16384]{3,2,1,0:T(4,128)(2,1)} %lesser_hbm.1, bf16[1,2,4,16384]{3,2,1,0:T(4,128)(2,1)} %greater_hbm.1), custom_call_target="tpu_custom_call" | custom-call | tf_op jit(solution)/shard_map/pallas_call | solution.py:80
  1.9 4.3 %all-to-all-start = ((bf16[8,4,4,2048]{3,2,1,0:T(4,128)(2,1)}), bf16[8,4,4,2048]{3,2,1,0:T(4,128)(2,1)S(1)}, u32[]{:S(2)}, u32[]{:S(2)}) async-start(bf16[8,4,4,2048]{3,2,1,0:T(4,128)(2,1)} %shard_map.46), calls=%async_computation | async-start | bytes 1048576 | tf_op jit(solution)/shard_map/all_to_all | solution.py:107
  6.2 0.2 fusion.22
  6.4 0.1 copy.19
  6.5 0.1 copy.20
  6.7 0.1 convert_element_type.77
  6.8 0.1 copy.21
  7.0 0.1 convert_element_type.79
  7.1 0.2 fusion.25
  7.4 0.1 maximum_maximum_fusion
  7.4 7.0 %all-to-all-done = bf16[8,4,4,2048]{3,2,1,0:T(4,128)(2,1)S(1)} async-done(((bf16[8,4,4,2048]{3,2,1,0:T(4,128)(2,1)}), bf16[8,4,4,2048]{3,2,1,0:T(4,128)(2,1)S(1)}, u32[]{:S(2)}, u32[]{:S(2)}) %all-to-all-start) | async-done | bytes 524320 | tf_op jit(solution)/shard_map/all_to_all | solution.py:107
  14.5 0.1 reshape.205
  14.6 0.5 fusion.28
  15.1 0.5 convolution_add_fusion
  15.5 0.1 multiply_add_fusion
  15.7 0.0 copy-start
  15.7 0.0 copy-start.1
  15.7 1.2 %fusion = f32[8,8,2048]{2,1,0:T(8,128)} fusion(f32[8,8,128]{2,1,0:T(8,128)S(1)} %bitcast.87, f32[64,2048]{1,0:T(8,128)S(1)} %get-tuple-element.10, f32[64,2048]{1,0:T(8,128)S(1)} %get-tuple-element.9), kind=kOutput, calls=%fused_computation.5 | convolution fusion | flops 100925440 | bytes 1605632 | tf_op jit(solution)/shard_map/dot_general | solution.py:55
  16.9 4.9 %all-to-all-start.1 = ((f32[8,8,2048]{2,1,0:T(8,128)}), f32[8,8,2048]{2,1,0:T(8,128)S(1)}, u32[]{:S(2)}, u32[]{:S(2)}) async-start(f32[8,8,2048]{2,1,0:T(8,128)} %fusion), calls=%async_computation.1 | async-start | bytes 1048576 | tf_op jit(solution)/shard_map/all_to_all | solution.py:111
  21.8 0.0 copy-done
  21.8 0.1 copy.23
  21.9 8.2 %all-to-all-done.1 = f32[8,8,2048]{2,1,0:T(8,128)S(1)} async-done(((f32[8,8,2048]{2,1,0:T(8,128)}), f32[8,8,2048]{2,1,0:T(8,128)S(1)}, u32[]{:S(2)}, u32[]{:S(2)}) %all-to-all-start.1) | async-done | bytes 524320 | tf_op jit(solution)/shard_map/all_to_all | solution.py:111
  30.1 0.3 copy.43
  30.4 0.1 reshape_reshape.6
  30.5 2.4 %collective-permute-start = (f32[8,8,2048]{2,1,0:T(8,128)S(1)}, f32[8,8,2048]{2,1,0:T(8,128)S(1)}, u32[]{:S(2)}, u32[]{:S(2)}) collective-permute-start(f32[8,8,2048]{2,1,0:T(8,128)S(1)} %all-to-all-done.1), channel_id=1, source_target_pairs={{1,0},{2,1},{3,2},{5,4},{6,5},{7,6},{9,8},{10,9},{11,10},{13,12},{... | collective-permute-start | bytes 1572872 | tf_op jit(solution)/shard_map/ppermute | solution.py:17
  32.9 0.0 copy-done.1
  32.9 0.6 %convolution_bitcast_fusion = f32[2,2,4,128,128]{3,4,0,2,1:T(8,128)S(1)} fusion(f32[2,4,128,128]{3,2,1,0:T(8,128)S(1)} %reshape_reshape.6, f32[1,128,128]{2,1,0:T(8,128)S(1)} %copy-done.1, f32[1,128,128]{2,1,0:T(8,128)S(1)} %bitcast.86), kind=kOutput, calls=%fused_computation.1 | convolution fusion | flops 201359360 | bytes 1703936 | tf_op jit(solution)/shard_map/sij,abjk->sabik/dot_general | solution.py:123
  33.5 0.6 %fusion.3 = f32[2,4,128,128]{3,2,1,0:T(8,128)S(1)} fusion(f32[2,2,4,128,128]{3,4,0,2,1:T(8,128)S(1)} %convolution_bitcast_fusion, f32[1,128,128]{2,1,0:T(8,128)S(1)} %copy-done), kind=kOutput, calls=%fused_computation.9 | convolution fusion | flops 100663296 | bytes 1114112 | tf_op jit(solution)/shard_map/dot_general | solution.py:124
  34.1 1.3 %collective-permute-start.1 = (f32[2,4,128,128]{3,2,1,0:T(8,128)S(1)}, f32[2,4,128,128]{3,2,1,0:T(8,128)S(1)}, u32[]{:S(2)}, u32[]{:S(2)}) collective-permute-start(f32[2,4,128,128]{3,2,1,0:T(8,128)S(1)} %fusion.3), channel_id=1, source_target_pairs={{0,1},{1,2},{2,3},{4,5},{5,6},{6,7},{8,9},{9,10},{10,11},{12,13},{... | collective-permute-start | bytes 1572872 | tf_op jit(solution)/shard_map/ppermute | solution.py:17
  35.4 0.6 %fusion.4 = f32[2,4,128,128]{3,2,1,0:T(8,128)S(1)} fusion(f32[2,2,4,128,128]{3,4,0,2,1:T(8,128)S(1)} %convolution_bitcast_fusion, f32[1,128,128]{2,1,0:T(8,128)S(1)} %copy-done.1), kind=kOutput, calls=%fused_computation.11 | convolution fusion | flops 100663296 | bytes 1114112 | tf_op jit(solution)/shard_map/dot_general | solution.py:126
  36.0 8.2 %collective-permute-done = f32[8,8,2048]{2,1,0:T(8,128)S(1)} collective-permute-done((f32[8,8,2048]{2,1,0:T(8,128)S(1)}, f32[8,8,2048]{2,1,0:T(8,128)S(1)}, u32[]{:S(2)}, u32[]{:S(2)}) %collective-permute-start) | collective-permute-done | bytes 524320 | tf_op jit(solution)/shard_map/ppermute | solution.py:17
  44.2 0.3 copy.46
  44.5 0.1 reshape_reshape.7
  44.6 0.6 %convolution_bitcast_fusion.1 = f32[2,4,128,128]{2,3,1,0:T(8,128)S(1)} fusion(f32[2,4,128,128]{3,2,1,0:T(8,128)S(1)} %reshape_reshape.7, f32[1,128,128]{2,1,0:T(8,128)S(1)} %copy-done), kind=kOutput, calls=%fused_computation.2 | convolution fusion | flops 100663296 | bytes 1114112 | tf_op jit(solution)/shard_map/dot_general | solution.py:59
  45.2 0.6 %convolution_add_fusion.1 = f32[2,4,128,128]{3,2,1,0:T(8,128)S(1)} fusion(f32[2,4,128,128]{3,2,1,0:T(8,128)S(1)} %fusion.4, f32[2,4,128,128]{2,3,1,0:T(8,128)S(1)} %convolution_bitcast_fusion.1, f32[1,128,128]{2,1,0:T(8,128)S(1)} %copy-done), kind=kOutput, calls=%fused_computation.3 | convolution fusion | flops 100794368 | bytes 1638400 | tf_op jit(solution)/shard_map/dot_general | solution.py:60
  45.8 0.2 reshape.208
  46.1 3.6 %collective-permute-done.1 = f32[2,4,128,128]{3,2,1,0:T(8,128)S(1)} collective-permute-done((f32[2,4,128,128]{3,2,1,0:T(8,128)S(1)}, f32[2,4,128,128]{3,2,1,0:T(8,128)S(1)}, u32[]{:S(2)}, u32[]{:S(2)}) %collective-permute-start.1) | collective-permute-done | bytes 524320 | tf_op jit(solution)/shard_map/ppermute | solution.py:17
  49.6 0.2 reshape.209
  49.8 0.9 %add.85 = f32[1,2,4,16384]{3,2,1,0:T(4,128)} add(f32[1,2,4,16384]{3,2,1,0:T(4,128)S(1)} %reshape.208, f32[1,2,4,16384]{3,2,1,0:T(4,128)S(1)} %reshape.209) | non-fusion elementwise | flops 131072 | bytes 1572864 | tf_op jit(solution)/shard_map/add | solution.py:131
  (4 shorter events, 0.1 us)
Async XLA Ops:
  1.9 12.6 %all-to-all-start = ((bf16[8,4,4,2048]{3,2,1,0:T(4,128)(2,1)}), bf16[8,4,4,2048]{3,2,1,0:T(4,128)(2,1)S(1)}, u32[]{:S(2)}, u32[]{:S(2)}) async-start(bf16[8,4,4,2048]{3,2,1,0:T(4,128)(2,1)} %shard_map.46), calls=%async_computation | async-start | bytes 1048576 | tf_op jit(solution)/shard_map/all_to_all | solution.py:107
  15.7 6.1 %copy-start = (f32[1,128,128]{2,1,0:T(8,128)S(1)}, f32[1,128,128]{2,1,0:T(8,128)}, u32[]{:S(2)}) copy-start(f32[1,128,128]{2,1,0:T(8,128)} %param.7) | copy-start | bytes 196612
  15.7 17.2 %copy-start.1 = (f32[1,128,128]{2,1,0:T(8,128)S(1)}, f32[1,128,128]{2,1,0:T(8,128)}, u32[]{:S(2)}) copy-start(f32[1,128,128]{2,1,0:T(8,128)} %param.6) | copy-start | bytes 196612
  16.9 13.2 %all-to-all-start.1 = ((f32[8,8,2048]{2,1,0:T(8,128)}), f32[8,8,2048]{2,1,0:T(8,128)S(1)}, u32[]{:S(2)}, u32[]{:S(2)}) async-start(f32[8,8,2048]{2,1,0:T(8,128)} %fusion), calls=%async_computation.1 | async-start | bytes 1048576 | tf_op jit(solution)/shard_map/all_to_all | solution.py:111
  30.5 13.8 %collective-permute-start = (f32[8,8,2048]{2,1,0:T(8,128)S(1)}, f32[8,8,2048]{2,1,0:T(8,128)S(1)}, u32[]{:S(2)}, u32[]{:S(2)}) collective-permute-start(f32[8,8,2048]{2,1,0:T(8,128)S(1)} %all-to-all-done.1), channel_id=1, source_target_pairs={{1,0},{2,1},{3,2},{5,4},{6,5},{7,6},{9,8},{10,9},{11,10},{13,12},{... | collective-permute-start | bytes 1572872 | tf_op jit(solution)/shard_map/ppermute | solution.py:17
  34.1 15.5 %collective-permute-start.1 = (f32[2,4,128,128]{3,2,1,0:T(8,128)S(1)}, f32[2,4,128,128]{3,2,1,0:T(8,128)S(1)}, u32[]{:S(2)}, u32[]{:S(2)}) collective-permute-start(f32[2,4,128,128]{3,2,1,0:T(8,128)S(1)} %fusion.3), channel_id=1, source_target_pairs={{0,1},{1,2},{2,3},{4,5},{5,6},{6,7},{8,9},{9,10},{10,11},{12,13},{... | collective-permute-start | bytes 1572872 | tf_op jit(solution)/shard_map/ppermute | solution.py:17

commit v14 on v13

--- a/solution.py
+++ b/solution.py
@@ -104,6 +104,8 @@
         both = jnp.pad(both, ((0, 0), (0, 0), (0, 0), (0, padding)))
         both = both.reshape(2, 2, e_local, groups, tile_width)
         both = both.transpose(3, 0, 1, 2, 4).reshape(groups, 4 * e_local, tile_width)
+    lefts = jnp.stack([couple_own.T, v_diag[0]])
+    both, lefts, couple_own = lax.optimization_barrier((both, lefts, couple_own))
     got = lax.all_to_all(both, "energy", 0, 0, tiled=True)
     polar_tile = correlate(got.reshape(groups * 4 * e_local, tile_width), forward, inverse)
 
@@ -119,7 +121,6 @@
     polar = as_blocks(back)
     polar_above = as_blocks(back_above)
     diag_block = v_diag[0]
-    lefts = jnp.stack([couple_own.T, diag_block])
     inner = jnp.einsum("sij,abjk->sabik", lefts, polar, precision=lax.Precision.HIGH)
     to_next = jnp.matmul(inner[0], couple_own, precision=lax.Precision.HIGH)
     from_below = shifted(to_next, "space", 1)

time: 51.2 us -> 51.8 us (1.012)
  the two profiles are of different devices: /device:TPU:26 before, /device:TPU:0 now
where the time goes in v14:
time: 51.8 us; the launch traced here: 51.3 us
  waiting for transfers between devices  16.7 us (32%)
  blocking collectives  12.2 us (24%)
  starting transfers between devices  11 us (21%)
  matrix products  3.87 us (7%)
  local copies, waits for them, and re-layouts  2.94 us (6%)
  other arithmetic  2.45 us (5%)
  Pallas kernels  1.94 us (4%)
    all_to_all x1, blocking collectives, per_device(): back = lax.all_to_all(send, 'energy', 0, 0, tiled=True)  12.2 us
    all_to_all x1, waiting for transfers between devices, per_device(): got = lax.all_to_all(both, 'energy', 0, 0, tiled=True)  8.5 us
    ppermute x2, waiting for transfers between devices, shifted(): return lax.ppermute(x, axis, pairs)  8.18 us
    ppermute x2, starting transfers between devices, shifted(): return lax.ppermute(x, axis, pairs)  5.87 us
    all_to_all x1, starting transfers between devices, per_device(): got = lax.all_to_all(both, 'energy', 0, 0, tiled=True)  5.18 us
    pallas_call x1, Pallas kernels, by_destination(): pl.pallas_call(kernel, out_shape=jax.ShapeDtypeStruct((groups, 4, e_local...  1.94 us
  transfers between devices with their start and end apart: 3, of which 3 were waited for; matrix products, arithmetic and copies ran while one was open for 8% of the time, Pallas kernels for 0%

profile of v14, /device:TPU:0, one launch (start us, length us, event | category | flops | bytes accessed | tf_op | source)
XLA Modules:
  0.0 51.3 jit_solution(5822940856609876155)
XLA Ops:
  0.0 0.9 %copy.19 = f32[1,128,128]{1,2,0:T(8,128)S(1)} copy(f32[1,128,128]{2,1,0:T(8,128)} %param.6) | data formatting | bytes 131072 | tf_op args[2]
  0.9 1.9 %shard_map.46 = bf16[8,4,4,2048]{3,2,1,0:T(4,128)(2,1)} custom-call(bf16[1,2,4,16384]{3,2,1,0:T(4,128)(2,1)} %lesser_hbm.1, bf16[1,2,4,16384]{3,2,1,0:T(4,128)(2,1)} %greater_hbm.1), custom_call_target="tpu_custom_call" | custom-call | tf_op jit(solution)/shard_map/pallas_call | solution.py:80
  2.9 0.9 %pad_maximum_fusion.1 = f32[2,128,128]{1,2,0:T(8,128)S(1)} fusion(f32[1,128,128]{1,2,0:T(8,128)S(1)} %copy.19, f32[1,128,128]{1,2,0:T(8,128)} %bitcast.80), kind=kLoop, calls=%fused_computation.19 | loop fusion | flops 32768 | bytes 262144 | tf_op jit(solution)/shard_map/stack | solution.py:107
  3.7 5.2 %all-to-all-start = ((bf16[8,4,4,2048]{3,2,1,0:T(4,128)(2,1)}), bf16[8,4,4,2048]{3,2,1,0:T(4,128)(2,1)S(1)}, u32[]{:S(2)}, u32[]{:S(2)}) async-start(bf16[8,4,4,2048]{3,2,1,0:T(4,128)(2,1)} %shard_map.46), calls=%async_computation | async-start | bytes 1048576 | tf_op jit(solution)/shard_map/all_to_all | solution.py:109
  8.9 0.2 fusion.21
  9.1 0.1 copy.17
  9.3 0.1 copy.18
  9.4 0.1 convert_element_type.77
  9.6 0.1 copy.20
  9.7 0.1 convert_element_type.79
  9.8 0.2 fusion.24
  10.1 0.1 maximum_maximum_fusion
  10.2 8.5 %all-to-all-done = bf16[8,4,4,2048]{3,2,1,0:T(4,128)(2,1)S(1)} async-done(((bf16[8,4,4,2048]{3,2,1,0:T(4,128)(2,1)}), bf16[8,4,4,2048]{3,2,1,0:T(4,128)(2,1)S(1)}, u32[]{:S(2)}, u32[]{:S(2)}) %all-to-all-start) | async-done | bytes 524320 | tf_op jit(solution)/shard_map/all_to_all | solution.py:109
  18.7 0.1 reshape.205
  18.8 0.5 fusion.26
  19.2 0.5 convolution_add_fusion
  19.7 0.1 multiply_add_fusion
  19.9 0.4 fusion
  20.3 12.2 %all_to_all.10 = f32[8,8,2048]{2,1,0:T(8,128)S(1)} all-to-all(f32[8,8,2048]{2,1,0:T(8,128)S(1)} %fusion), channel_id=1, replica_groups=mesh['energy'=8,'space'=4] {'energy'}, dimensions={0} | all-to-all | bytes 1048576 | tf_op jit(solution)/shard_map/all_to_all | solution.py:113
  32.4 0.0 copy-start
  32.4 0.3 copy.33
  32.7 0.0 copy-start.1
  32.7 0.1 reshape_reshape.6
  32.8 1.3 %collective-permute-start = (f32[8,8,2048]{2,1,0:T(8,128)S(1)}, f32[8,8,2048]{2,1,0:T(8,128)S(1)}, u32[]{:S(2)}, u32[]{:S(2)}) collective-permute-start(f32[8,8,2048]{2,1,0:T(8,128)S(1)} %all_to_all.10), channel_id=1, source_target_pairs={{1,0},{2,1},{3,2},{5,4},{6,5},{7,6},{9,8},{10,9},{11,10},{13,12},{... | collective-permute-start | bytes 1572872 | tf_op jit(solution)/shard_map/ppermute | solution.py:17
  34.1 0.6 %convolution_bitcast_fusion = f32[2,2,4,128,128]{3,4,0,2,1:T(8,128)S(1)} fusion(f32[2,4,128,128]{3,2,1,0:T(8,128)S(1)} %reshape_reshape.6, f32[2,128,128]{1,2,0:T(8,128)S(1)} %pad_maximum_fusion.1), kind=kOutput, calls=%fused_computation.1 | convolution fusion | flops 201326592 | bytes 1703936 | tf_op jit(solution)/shard_map/sij,abjk->sabik/dot_general | solution.py:124
  34.8 0.0 copy-done
  34.8 0.6 %fusion.3 = f32[2,4,128,128]{3,2,1,0:T(8,128)S(1)} fusion(f32[2,2,4,128,128]{3,4,0,2,1:T(8,128)S(1)} %convolution_bitcast_fusion, f32[128,128]{1,0:T(8,128)S(1)} %bitcast.81), kind=kOutput, calls=%fused_computation.9 | convolution fusion | flops 100663296 | bytes 1114112 | tf_op jit(solution)/shard_map/dot_general | solution.py:125
  35.4 4.6 %collective-permute-start.1 = (f32[2,4,128,128]{3,2,1,0:T(8,128)S(1)}, f32[2,4,128,128]{3,2,1,0:T(8,128)S(1)}, u32[]{:S(2)}, u32[]{:S(2)}) collective-permute-start(f32[2,4,128,128]{3,2,1,0:T(8,128)S(1)} %fusion.3), channel_id=1, source_target_pairs={{0,1},{1,2},{2,3},{4,5},{5,6},{6,7},{8,9},{9,10},{10,11},{12,13},{... | collective-permute-start | bytes 1572872 | tf_op jit(solution)/shard_map/ppermute | solution.py:17
  39.9 0.0 copy-done.1
  40.0 0.6 %fusion.4 = f32[2,4,128,128]{3,2,1,0:T(8,128)S(1)} fusion(f32[2,2,4,128,128]{3,4,0,2,1:T(8,128)S(1)} %convolution_bitcast_fusion, f32[1,128,128]{2,1,0:T(8,128)S(1)} %copy-done.1), kind=kOutput, calls=%fused_computation.11 | convolution fusion | flops 100663296 | bytes 1114112 | tf_op jit(solution)/shard_map/dot_general | solution.py:127
  40.6 7.2 %collective-permute-done = f32[8,8,2048]{2,1,0:T(8,128)S(1)} collective-permute-done((f32[8,8,2048]{2,1,0:T(8,128)S(1)}, f32[8,8,2048]{2,1,0:T(8,128)S(1)}, u32[]{:S(2)}, u32[]{:S(2)}) %collective-permute-start) | collective-permute-done | bytes 524320 | tf_op jit(solution)/shard_map/ppermute | solution.py:17
  47.7 0.3 copy.37
  48.0 0.1 reshape_reshape.7
  48.1 0.4 convolution_bitcast_fusion.1
  48.5 0.4 convolution_add_fusion.1
  48.9 0.2 reshape.208
  49.1 1.0 %collective-permute-done.1 = f32[2,4,128,128]{3,2,1,0:T(8,128)S(1)} collective-permute-done((f32[2,4,128,128]{3,2,1,0:T(8,128)S(1)}, f32[2,4,128,128]{3,2,1,0:T(8,128)S(1)}, u32[]{:S(2)}, u32[]{:S(2)}) %collective-permute-start.1) | collective-permute-done | bytes 524320 | tf_op jit(solution)/shard_map/ppermute | solution.py:17
  50.1 0.2 reshape.209
  50.4 0.9 %add.85 = f32[1,2,4,16384]{3,2,1,0:T(4,128)} add(f32[1,2,4,16384]{3,2,1,0:T(4,128)S(1)} %reshape.208, f32[1,2,4,16384]{3,2,1,0:T(4,128)S(1)} %reshape.209) | non-fusion elementwise | flops 131072 | bytes 1572864 | tf_op jit(solution)/shard_map/add | solution.py:132
  (4 shorter events, 0.1 us)
Async XLA Ops:
  3.7 14.9 %all-to-all-start = ((bf16[8,4,4,2048]{3,2,1,0:T(4,128)(2,1)}), bf16[8,4,4,2048]{3,2,1,0:T(4,128)(2,1)S(1)}, u32[]{:S(2)}, u32[]{:S(2)}) async-start(bf16[8,4,4,2048]{3,2,1,0:T(4,128)(2,1)} %shard_map.46), calls=%async_computation | async-start | bytes 1048576 | tf_op jit(solution)/shard_map/all_to_all | solution.py:109
  32.4 2.3 %copy-start = (f32[1,128,128]{2,1,0:T(8,128)S(1)}, f32[1,128,128]{2,1,0:T(8,128)}, u32[]{:S(2)}) copy-start(f32[1,128,128]{2,1,0:T(8,128)} %param.7) | copy-start | bytes 196612
  32.7 7.2 %copy-start.1 = (f32[1,128,128]{2,1,0:T(8,128)S(1)}, f32[1,128,128]{2,1,0:T(8,128)}, u32[]{:S(2)}) copy-start(f32[1,128,128]{2,1,0:T(8,128)} %param.6) | copy-start | bytes 196612
  32.8 14.9 %collective-permute-start = (f32[8,8,2048]{2,1,0:T(8,128)S(1)}, f32[8,8,2048]{2,1,0:T(8,128)S(1)}, u32[]{:S(2)}, u32[]{:S(2)}) collective-permute-start(f32[8,8,2048]{2,1,0:T(8,128)S(1)} %all_to_all.10), channel_id=1, source_target_pairs={{1,0},{2,1},{3,2},{5,4},{6,5},{7,6},{9,8},{10,9},{11,10},{13,12},{... | collective-permute-start | bytes 1572872 | tf_op jit(solution)/shard_map/ppermute | solution.py:17
  35.4 14.8 %collective-permute-start.1 = (f32[2,4,128,128]{3,2,1,0:T(8,128)S(1)}, f32[2,4,128,128]{3,2,1,0:T(8,128)S(1)}, u32[]{:S(2)}, u32[]{:S(2)}) collective-permute-start(f32[2,4,128,128]{3,2,1,0:T(8,128)S(1)} %fusion.3), channel_id=1, source_target_pairs={{0,1},{1,2},{2,3},{4,5},{5,6},{6,7},{8,9},{9,10},{10,11},{12,13},{... | collective-permute-start | bytes 1572872 | tf_op jit(solution)/shard_map/ppermute | solution.py:17

commit v15 on v10

--- a/solution.py
+++ b/solution.py
@@ -45,8 +45,8 @@
 def correlate(got, forward, inverse):
     high = lax.reduce_precision(forward, exponent_bits=8, mantissa_bits=7)
     low = forward - high
-    spectrum = jnp.dot(high.astype(jnp.bfloat16), got, preferred_element_type=jnp.float32)
-    spectrum = spectrum + jnp.dot(low.astype(jnp.bfloat16), got, preferred_element_type=jnp.float32)
+    split = jnp.concatenate([high, low], axis=1).astype(jnp.bfloat16)
+    spectrum = jnp.dot(split, jnp.concatenate([got, got]), preferred_element_type=jnp.float32)
     length = forward.shape[0] // 4
     l_re, l_im, g_re, g_im = (spectrum[i * length:(i + 1) * length] for i in range(4))
     z_re = l_re * g_re + l_im * g_im

time: 49.9 us -> 49.4 us (0.990)
    convert_element_type x4 -> x0, local copies, waits for them, and re-layouts: 0.57 us -> none  [the longest x2 0.28 us: correlate(): high.astype(jnp.bfloat16)]
  transfers between devices with their start and end apart: 3 -> 3, of which waited for: 2 -> 2; matrix products, arithmetic and copies ran while one was open for 10% -> 9% of each run, Pallas kernels for 0% -> 0%
where the time goes in v15:
time: 49.4 us; the launch traced here: 49.1 us
  waiting for transfers between devices  15.8 us (32%)
  blocking collectives  12.2 us (25%)
  starting transfers between devices  11.1 us (22%)
  matrix products  4.38 us (9%)
  Pallas kernels  1.96 us (4%)
  local copies, waits for them, and re-layouts  1.9 us (4%)
  other arithmetic  1.59 us (3%)
    all_to_all x1, blocking collectives, per_device(): back = lax.all_to_all(send, 'energy', 0, 0, tiled=True)  12.2 us
    all_to_all x1, waiting for transfers between devices, per_device(): got = lax.all_to_all(both, 'energy', 0, 0, tiled=True)  8.63 us
    ppermute x2, waiting for transfers between devices, shifted(): return lax.ppermute(x, axis, pairs)  7.22 us
    ppermute x2, starting transfers between devices, shifted(): return lax.ppermute(x, axis, pairs)  5.87 us
    all_to_all x1, starting transfers between devices, per_device(): got = lax.all_to_all(both, 'energy', 0, 0, tiled=True)  5.18 us
    pallas_call x1, Pallas kernels, by_destination(): pl.pallas_call(kernel, out_shape=jax.ShapeDtypeStruct((groups, 4, e_local...  1.96 us
    dot_general x3, matrix products, sandwich(): return jnp.matmul(inner, right, precision=lax.Precision.HIGH)  1.77 us
    dot_general x3, matrix products, sandwich(): inner = jnp.matmul(left, field, precision=lax.Precision.HIGH)  1.76 us
  transfers between devices with their start and end apart: 3, of which 2 were waited for; matrix products, arithmetic and copies ran while one was open for 9% of the time, Pallas kernels for 0%

profile of v15, /device:TPU:0, one launch (start us, length us, event | category | flops | bytes accessed | tf_op | source)
XLA Modules:
  0.0 49.1 jit_solution(18135753563979431680)
XLA Ops:
  0.0 0.0 copy-start
  0.0 2.0 %shard_map.46 = bf16[8,4,4,2048]{3,2,1,0:T(4,128)(2,1)} custom-call(bf16[1,2,4,16384]{3,2,1,0:T(4,128)(2,1)} %lesser_hbm.1, bf16[1,2,4,16384]{3,2,1,0:T(4,128)(2,1)} %greater_hbm.1), custom_call_target="tpu_custom_call" | custom-call | tf_op jit(solution)/shard_map/pallas_call | solution.py:80
  2.0 5.2 %all-to-all-start = ((bf16[8,4,4,2048]{3,2,1,0:T(4,128)(2,1)}), bf16[8,4,4,2048]{3,2,1,0:T(4,128)(2,1)S(1)}, u32[]{:S(2)}, u32[]{:S(2)}) async-start(bf16[8,4,4,2048]{3,2,1,0:T(4,128)(2,1)} %shard_map.46), calls=%async_computation | async-start | bytes 1048576 | tf_op jit(solution)/shard_map/all_to_all | solution.py:107
  7.2 0.2 fusion.28
  7.3 0.1 copy.8
  7.5 0.2 copy.9
  7.7 0.3 reshape.193
  7.9 0.2 fusion.31
  8.2 0.1 maximum_maximum_fusion
  8.3 8.6 %all-to-all-done = bf16[8,4,4,2048]{3,2,1,0:T(4,128)(2,1)S(1)} async-done(((bf16[8,4,4,2048]{3,2,1,0:T(4,128)(2,1)}), bf16[8,4,4,2048]{3,2,1,0:T(4,128)(2,1)S(1)}, u32[]{:S(2)}, u32[]{:S(2)}) %all-to-all-start) | async-done | bytes 524320 | tf_op jit(solution)/shard_map/all_to_all | solution.py:107
  16.9 0.1 reshape.194
  17.0 0.5 fusion
  17.5 0.1 multiply_add_fusion
  17.6 0.4 fusion.4
  18.0 12.2 %all_to_all.10 = f32[8,8,2048]{2,1,0:T(8,128)S(1)} all-to-all(f32[8,8,2048]{2,1,0:T(8,128)S(1)} %fusion.4), channel_id=1, replica_groups=mesh['energy'=8,'space'=4] {'energy'}, dimensions={0} | all-to-all | bytes 1048576 | tf_op jit(solution)/shard_map/all_to_all | solution.py:111
  30.2 0.0 copy-start.1
  30.2 0.3 copy.26
  30.5 0.1 reshape_reshape.6
  30.6 0.0 copy-done
  30.6 0.6 %convolution_bitcast_fusion = f32[2,4,128,128]{2,3,1,0:T(8,128)S(1)} fusion(f32[2,4,128,128]{3,2,1,0:T(8,128)S(1)} %reshape_reshape.6, f32[1,128,128]{2,1,0:T(8,128)S(1)} %copy-done), kind=kOutput, calls=%fused_computation | convolution fusion | flops 100663296 | bytes 1114112 | tf_op jit(solution)/shard_map/dot_general | solution.py:59
  31.2 1.3 %collective-permute-start = (f32[8,8,2048]{2,1,0:T(8,128)S(1)}, f32[8,8,2048]{2,1,0:T(8,128)S(1)}, u32[]{:S(2)}, u32[]{:S(2)}) collective-permute-start(f32[8,8,2048]{2,1,0:T(8,128)S(1)} %all_to_all.10), channel_id=1, source_target_pairs={{1,0},{2,1},{3,2},{5,4},{6,5},{7,6},{9,8},{10,9},{11,10},{13,12},{... | collective-permute-start | bytes 1572872 | tf_op jit(solution)/shard_map/ppermute | solution.py:17
  32.5 0.6 %fusion.14 = f32[2,4,128,128]{3,2,1,0:T(8,128)S(1)} fusion(f32[2,4,128,128]{2,3,1,0:T(8,128)S(1)} %convolution_bitcast_fusion, f32[1,128,128]{2,1,0:T(8,128)S(1)} %copy-done), kind=kOutput, calls=%fused_computation.27 | convolution fusion | flops 100663296 | bytes 1114112 | tf_op jit(solution)/shard_map/dot_general | solution.py:60
  33.1 4.6 %collective-permute-start.1 = (f32[2,4,128,128]{3,2,1,0:T(8,128)S(1)}, f32[2,4,128,128]{3,2,1,0:T(8,128)S(1)}, u32[]{:S(2)}, u32[]{:S(2)}) collective-permute-start(f32[2,4,128,128]{3,2,1,0:T(8,128)S(1)} %fusion.14), channel_id=1, source_target_pairs={{0,1},{1,2},{2,3},{4,5},{5,6},{6,7},{8,9},{9,10},{10,11},{12,13},{... | collective-permute-start | bytes 1572872 | tf_op jit(solution)/shard_map/ppermute | solution.py:17
  37.7 0.0 copy-done.1
  37.7 0.6 %convolution_bitcast_fusion.2 = f32[2,4,128,128]{2,3,1,0:T(8,128)S(1)} fusion(f32[2,4,128,128]{3,2,1,0:T(8,128)S(1)} %reshape_reshape.6, f32[1,128,128]{2,1,0:T(8,128)S(1)} %copy-done.1), kind=kOutput, calls=%fused_computation.2 | convolution fusion | flops 100663296 | bytes 1114112 | tf_op jit(solution)/shard_map/dot_general | solution.py:59
  38.3 0.6 %fusion.11 = f32[2,4,128,128]{3,2,1,0:T(8,128)S(1)} fusion(f32[2,4,128,128]{2,3,1,0:T(8,128)S(1)} %convolution_bitcast_fusion.2, f32[1,128,128]{2,1,0:T(8,128)S(1)} %copy-done.1), kind=kOutput, calls=%fused_computation.24 | convolution fusion | flops 100663296 | bytes 1114112 | tf_op jit(solution)/shard_map/dot_general | solution.py:60
  38.9 7.2 %collective-permute-done = f32[8,8,2048]{2,1,0:T(8,128)S(1)} collective-permute-done((f32[8,8,2048]{2,1,0:T(8,128)S(1)}, f32[8,8,2048]{2,1,0:T(8,128)S(1)}, u32[]{:S(2)}, u32[]{:S(2)}) %collective-permute-start) | collective-permute-done | bytes 524320 | tf_op jit(solution)/shard_map/ppermute | solution.py:17
  46.1 0.3 copy.27
  46.4 0.1 reshape_reshape.7
  46.5 0.6 %convolution_bitcast_fusion.1 = f32[2,4,128,128]{2,3,1,0:T(8,128)S(1)} fusion(f32[2,4,128,128]{3,2,1,0:T(8,128)S(1)} %reshape_reshape.7, f32[1,128,128]{2,1,0:T(8,128)S(1)} %copy-done), kind=kOutput, calls=%fused_computation.1 | convolution fusion | flops 100663296 | bytes 1114112 | tf_op jit(solution)/shard_map/dot_general | solution.py:59
  47.1 0.6 %convolution_add_fusion = f32[2,4,128,128]{3,2,1,0:T(8,128)S(1)} fusion(f32[2,4,128,128]{3,2,1,0:T(8,128)S(1)} %fusion.11, f32[2,4,128,128]{2,3,1,0:T(8,128)S(1)} %convolution_bitcast_fusion.1, f32[1,128,128]{2,1,0:T(8,128)S(1)} %copy-done), kind=kOutput, calls=%fused_computation.3 | convolution fusion | flops 100794368 | bytes 1638400 | tf_op jit(solution)/shard_map/dot_general | solution.py:60
  47.7 0.2 reshape.197
  47.9 0.0 collective-permute-done.1
  47.9 0.2 reshape.198
  48.2 0.9 %add.81 = f32[1,2,4,16384]{3,2,1,0:T(4,128)} add(f32[1,2,4,16384]{3,2,1,0:T(4,128)S(1)} %reshape.197, f32[1,2,4,16384]{3,2,1,0:T(4,128)S(1)} %reshape.198) | non-fusion elementwise | flops 131072 | bytes 1572864 | tf_op jit(solution)/shard_map/add | solution.py:129
  (5 shorter events, 0.1 us)
Async XLA Ops:
  0.0 30.6 %copy-start = (f32[1,128,128]{2,1,0:T(8,128)S(1)}, f32[1,128,128]{2,1,0:T(8,128)}, u32[]{:S(2)}) copy-start(f32[1,128,128]{2,1,0:T(8,128)} %param.7) | copy-start | bytes 196612
  2.0 14.9 %all-to-all-start = ((bf16[8,4,4,2048]{3,2,1,0:T(4,128)(2,1)}), bf16[8,4,4,2048]{3,2,1,0:T(4,128)(2,1)S(1)}, u32[]{:S(2)}, u32[]{:S(2)}) async-start(bf16[8,4,4,2048]{3,2,1,0:T(4,128)(2,1)} %shard_map.46), calls=%async_computation | async-start | bytes 1048576 | tf_op jit(solution)/shard_map/all_to_all | solution.py:107
  30.2 7.5 %copy-start.1 = (f32[1,128,128]{2,1,0:T(8,128)S(1)}, f32[1,128,128]{2,1,0:T(8,128)}, u32[]{:S(2)}) copy-start(f32[1,128,128]{2,1,0:T(8,128)} %param.6) | copy-start | bytes 196612
  31.2 14.9 %collective-permute-start = (f32[8,8,2048]{2,1,0:T(8,128)S(1)}, f32[8,8,2048]{2,1,0:T(8,128)S(1)}, u32[]{:S(2)}, u32[]{:S(2)}) collective-permute-start(f32[8,8,2048]{2,1,0:T(8,128)S(1)} %all_to_all.10), channel_id=1, source_target_pairs={{1,0},{2,1},{3,2},{5,4},{6,5},{7,6},{9,8},{10,9},{11,10},{13,12},{... | collective-permute-start | bytes 1572872 | tf_op jit(solution)/shard_map/ppermute | solution.py:17
  33.1 14.8 %collective-permute-start.1 = (f32[2,4,128,128]{3,2,1,0:T(8,128)S(1)}, f32[2,4,128,128]{3,2,1,0:T(8,128)S(1)}, u32[]{:S(2)}, u32[]{:S(2)}) collective-permute-start(f32[2,4,128,128]{3,2,1,0:T(8,128)S(1)} %fusion.14), channel_id=1, source_target_pairs={{0,1},{1,2},{2,3},{4,5},{5,6},{6,7},{8,9},{9,10},{10,11},{12,13},{... | collective-permute-start | bytes 1572872 | tf_op jit(solution)/shard_map/ppermute | solution.py:17

commit v16 on v15

--- a/solution.py
+++ b/solution.py
@@ -1,6 +1,7 @@
 import math
 
 import jax
+import numpy as np
 import jax.numpy as jnp
 from jax import lax
 from jax.experimental import pallas as pl
@@ -15,6 +16,31 @@
     devices = lax.axis_size(axis)
     pairs = [(i, i + by) for i in range(devices) if 0 <= i + by < devices]
     return lax.ppermute(x, axis, pairs)
+
+
+def tables_np(count, e_local, groups):
+    length = 2 * count
+    k = np.arange(length, dtype=np.int32)
+    n = np.arange(count, dtype=np.int32)
+    phase = ((k[:, None] * n[None, :]) % length).astype(np.float32) * np.float32(2.0 * math.pi / length)
+    cosine = np.cos(phase)
+    sine = np.sin(phase)
+    re_rows = np.stack([cosine, sine], axis=1)
+    im_rows = np.stack([-sine, cosine], axis=1)
+    per_part = np.stack([re_rows, im_rows])
+    per_part = per_part.reshape(2, length, 2, groups, e_local).transpose(0, 1, 3, 2, 4)
+    zero = np.zeros_like(per_part)
+    lesser_rows = np.stack([per_part, zero], axis=3)
+    greater_rows = np.stack([zero, per_part], axis=3)
+    forward = np.stack([lesser_rows, greater_rows]).reshape(4 * length, 4 * count)
+    scale = np.float32(count ** (-0.5) / length)
+    inv_cos = cosine.T * scale
+    inv_sin = sine.T * scale
+    ri0 = np.concatenate([-inv_sin, -inv_cos], axis=1)
+    ri1 = np.concatenate([inv_cos, -inv_sin], axis=1)
+    inverse = np.stack([ri0, ri1]).reshape(2, groups, e_local, 2 * length)
+    inverse = inverse.transpose(1, 0, 2, 3).reshape(2 * count, 2 * length)
+    return forward, inverse
 
 
 def tables(count, e_local, groups):
@@ -95,7 +121,8 @@
     padding = tile_width * groups - elements
 
     couple_own = v_couple[0]
-    forward, inverse = tables(count, e_local, groups)
+    make_tables = tables_np if count <= 64 else tables
+    forward, inverse = make_tables(count, e_local, groups)
 
     if padding == 0:
         both = by_destination(g_lesser, g_greater, groups, tile_width)

time: 49.4 us -> 50.4 us (1.020)
  blocking collectives: 12.2 us -> 27.1 us
  waiting for transfers between devices: 15.8 us -> 8.06 us
  starting transfers between devices: 11.1 us -> 5.87 us
  other arithmetic: 1.59 us -> 0.93 us
    all_to_all x0 -> x1, blocking collectives: none -> 14.9 us  [per_device(): got = lax.all_to_all(both, 'energy', 0, 0, tiled=True)]
    all_to_all x1 -> x0, waiting for transfers between devices: 8.63 us -> none  [per_device(): got = lax.all_to_all(both, 'energy', 0, 0, tiled=True)]
    all_to_all x1 -> x0, starting transfers between devices: 5.18 us -> none  [per_device(): got = lax.all_to_all(both, 'energy', 0, 0, tiled=True)]
    reshape x3 -> x0, local copies, waits for them, and re-layouts: 0.87 us -> none  [the longest x2 0.62 us: as_blocks(): received.reshape(groups, 2, e_local, tile_width).transpose(1, 2, 0, 3)]
    ppermute x2, waiting for transfers between devices: 7.22 us -> 8.06 us  [shifted(): return lax.ppermute(x, axis, pairs)]
    dot_general x3, matrix products: 1.77 us -> 1.11 us  [sandwich(): return jnp.matmul(inner, right, precision=lax.Precision.HIGH)]
    dot_general x3, matrix products: 1.76 us -> 1.14 us  [sandwich(): inner = jnp.matmul(left, field, precision=lax.Precision.HIGH)]
    unnamed x4 -> x12, local copies, waits for them, and re-layouts: 0.01 us -> 0.63 us
  transfers between devices with their start and end apart: 3 -> 2, of which waited for: 2 -> 2; matrix products, arithmetic and copies ran while one was open for 9% -> 5% of each run, Pallas kernels for 0% -> 0%
where the time goes in v16:
time: 50.4 us; the launch traced here: 50 us
  blocking collectives  27.1 us (54%)
  waiting for transfers between devices  8.06 us (16%)
  starting transfers between devices  5.87 us (12%)
  matrix products  3.91 us (8%)
  local copies, waits for them, and re-layouts  1.96 us (4%)
  Pallas kernels  1.96 us (4%)
  other arithmetic  0.93 us (2%)
    all_to_all x1, blocking collectives, per_device(): got = lax.all_to_all(both, 'energy', 0, 0, tiled=True)  14.9 us
    all_to_all x1, blocking collectives, per_device(): back = lax.all_to_all(send, 'energy', 0, 0, tiled=True)  12.2 us
    ppermute x2, waiting for transfers between devices, shifted(): return lax.ppermute(x, axis, pairs)  8.06 us
    ppermute x2, starting transfers between devices, shifted(): return lax.ppermute(x, axis, pairs)  5.87 us
    pallas_call x1, Pallas kernels, by_destination(): pl.pallas_call(kernel, out_shape=jax.ShapeDtypeStruct((groups, 4, e_local...  1.96 us
    dot_general x3, matrix products, sandwich(): inner = jnp.matmul(left, field, precision=lax.Precision.HIGH)  1.14 us
    dot_general x3, matrix products, sandwich(): return jnp.matmul(inner, right, precision=lax.Precision.HIGH)  1.11 us
  transfers between devices with their start and end apart: 2, of which 2 were waited for; matrix products, arithmetic and copies ran while one was open for 5% of the time, Pallas kernels for 0%

profile of v16, /device:TPU:0, one launch (start us, length us, event | category | flops | bytes accessed | tf_op | source)
XLA Modules:
  0.0 50.0 jit_solution(17303157609333436489)
XLA Ops:
  0.0 0.0 copy-start
  0.0 0.0 copy-start.3
  0.0 2.0 %shard_map.64 = bf16[8,4,4,2048]{3,2,1,0:T(4,128)(2,1)} custom-call(bf16[1,2,4,16384]{3,2,1,0:T(4,128)(2,1)} %lesser_hbm.1, bf16[1,2,4,16384]{3,2,1,0:T(4,128)(2,1)} %greater_hbm.1), custom_call_target="tpu_custom_call" | custom-call | tf_op jit(solution)/shard_map/pallas_call | solution.py:106
  2.0 14.9 %all_to_all.10 = bf16[8,4,4,2048]{3,2,1,0:T(4,128)(2,1)S(1)} all-to-all(bf16[8,4,4,2048]{3,2,1,0:T(4,128)(2,1)} %shard_map.64), channel_id=1, replica_groups=mesh['energy'=8,'space'=4] {'energy'}, dimensions={0} | all-to-all | bytes 1048576 | tf_op jit(solution)/shard_map/all_to_all | solution.py:134
  16.9 0.0 copy-start.2
  16.9 0.1 reshape.18
  17.0 0.0 copy-done.3
  17.0 0.4 fusion.24
  17.5 0.3 copy-done.2
  17.7 0.0 copy-start.5
  17.7 0.0 copy-start.4
  17.7 0.4 convolution_add_fusion
  18.2 0.3 copy-done.5
  18.5 0.4 fusion.4
  18.9 0.0 copy-done.4
  18.9 0.4 fusion
  19.4 12.2 %all_to_all.11 = f32[8,8,2048]{2,1,0:T(8,128)S(1)} all-to-all(f32[8,8,2048]{2,1,0:T(8,128)S(1)} %fusion), channel_id=1, replica_groups=mesh['energy'=8,'space'=4] {'energy'}, dimensions={0} | all-to-all | bytes 1048576 | tf_op jit(solution)/shard_map/all_to_all | solution.py:138
  31.5 0.0 copy-start.1
  31.5 0.3 copy.7
  31.8 0.1 reshape_reshape.6
  31.9 0.0 copy-done
  31.9 0.4 convolution_bitcast_fusion
  32.3 1.3 %collective-permute-start = (f32[8,8,2048]{2,1,0:T(8,128)S(1)}, f32[8,8,2048]{2,1,0:T(8,128)S(1)}, u32[]{:S(2)}, u32[]{:S(2)}) collective-permute-start(f32[8,8,2048]{2,1,0:T(8,128)S(1)} %all_to_all.11), channel_id=1, source_target_pairs={{1,0},{2,1},{3,2},{5,4},{6,5},{7,6},{9,8},{10,9},{11,10},{13,12},{... | collective-permute-start | bytes 1572872 | tf_op jit(solution)/shard_map/ppermute | solution.py:18
  33.6 0.4 fusion.19
  34.0 4.6 %collective-permute-start.1 = (f32[2,4,128,128]{3,2,1,0:T(8,128)S(1)}, f32[2,4,128,128]{3,2,1,0:T(8,128)S(1)}, u32[]{:S(2)}, u32[]{:S(2)}) collective-permute-start(f32[2,4,128,128]{3,2,1,0:T(8,128)S(1)} %fusion.19), channel_id=1, source_target_pairs={{0,1},{1,2},{2,3},{4,5},{5,6},{6,7},{8,9},{9,10},{10,11},{12,13},{... | collective-permute-start | bytes 1572872 | tf_op jit(solution)/shard_map/ppermute | solution.py:18
  38.6 0.0 copy-done.1
  38.6 0.4 convolution_bitcast_fusion.2
  39.0 0.4 fusion.16
  39.3 7.9 %collective-permute-done = f32[8,8,2048]{2,1,0:T(8,128)S(1)} collective-permute-done((f32[8,8,2048]{2,1,0:T(8,128)S(1)}, f32[8,8,2048]{2,1,0:T(8,128)S(1)}, u32[]{:S(2)}, u32[]{:S(2)}) %collective-permute-start) | collective-permute-done | bytes 524320 | tf_op jit(solution)/shard_map/ppermute | solution.py:18
  47.2 0.3 copy.8
  47.6 0.1 reshape_reshape.7
  47.6 0.4 convolution_bitcast_fusion.1
  48.0 0.4 convolution_add_fusion.2
  48.4 0.2 reshape.22
  48.6 0.2 collective-permute-done.1
  48.8 0.2 reshape.23
  49.0 0.9 %add.11 = f32[1,2,4,16384]{3,2,1,0:T(4,128)} add(f32[1,2,4,16384]{3,2,1,0:T(4,128)S(1)} %reshape.22, f32[1,2,4,16384]{3,2,1,0:T(4,128)S(1)} %reshape.23) | non-fusion elementwise | flops 131072 | bytes 1572864 | tf_op jit(solution)/shard_map/add | solution.py:156
Async XLA Ops:
  0.0 31.9 %copy-start = (f32[1,128,128]{2,1,0:T(8,128)S(1)}, f32[1,128,128]{2,1,0:T(8,128)}, u32[]{:S(2)}) copy-start(f32[1,128,128]{2,1,0:T(8,128)} %param.9) | copy-start | bytes 196612
  0.0 17.0 %copy-start.3 = (bf16[256,128]{1,0:T(8,128)(2,1)S(1)}, bf16[256,128]{1,0:T(8,128)(2,1)}, u32[]{:S(2)}) copy-start(bf16[256,128]{1,0:T(8,128)(2,1)} %constant.17) | copy-start | bytes 196612
  16.9 0.8 %copy-start.2 = (bf16[256,128]{1,0:T(8,128)(2,1)S(1)}, bf16[256,128]{1,0:T(8,128)(2,1)}, u32[]{:S(2)}) copy-start(bf16[256,128]{1,0:T(8,128)(2,1)} %constant.18) | copy-start | bytes 196612
  17.7 0.8 %copy-start.5 = (f32[64,64]{1,0:T(8,128)S(1)}, f32[64,64]{1,0:T(8,128)}, u32[]{:S(2)}) copy-start(f32[64,64]{1,0:T(8,128)} %constant.15) | copy-start | bytes 49156
  17.7 1.2 %copy-start.4 = (f32[64,64]{1,0:T(8,128)S(1)}, f32[64,64]{1,0:T(8,128)}, u32[]{:S(2)}) copy-start(f32[64,64]{1,0:T(8,128)} %constant.16) | copy-start | bytes 49156
  31.5 7.1 %copy-start.1 = (f32[1,128,128]{2,1,0:T(8,128)S(1)}, f32[1,128,128]{2,1,0:T(8,128)}, u32[]{:S(2)}) copy-start(f32[1,128,128]{2,1,0:T(8,128)} %param.8) | copy-start | bytes 196612
  32.3 14.9 %collective-permute-start = (f32[8,8,2048]{2,1,0:T(8,128)S(1)}, f32[8,8,2048]{2,1,0:T(8,128)S(1)}, u32[]{:S(2)}, u32[]{:S(2)}) collective-permute-start(f32[8,8,2048]{2,1,0:T(8,128)S(1)} %all_to_all.11), channel_id=1, source_target_pairs={{1,0},{2,1},{3,2},{5,4},{6,5},{7,6},{9,8},{10,9},{11,10},{13,12},{... | collective-permute-start | bytes 1572872 | tf_op jit(solution)/shard_map/ppermute | solution.py:18
  34.0 14.8 %collective-permute-start.1 = (f32[2,4,128,128]{3,2,1,0:T(8,128)S(1)}, f32[2,4,128,128]{3,2,1,0:T(8,128)S(1)}, u32[]{:S(2)}, u32[]{:S(2)}) collective-permute-start(f32[2,4,128,128]{3,2,1,0:T(8,128)S(1)} %fusion.19), channel_id=1, source_target_pairs={{0,1},{1,2},{2,3},{4,5},{5,6},{6,7},{8,9},{9,10},{10,11},{12,13},{... | collective-permute-start | bytes 1572872 | tf_op jit(solution)/shard_map/ppermute | solution.py:18

commit v17 on v15

--- a/solution.py
+++ b/solution.py
@@ -121,12 +121,10 @@
     diag_block = v_diag[0]
     to_next = sandwich(couple_own.T, polar, couple_own)
     from_below = shifted(to_next, "space", 1)
-    local = sandwich(diag_block, polar, diag_block)
+    local = lax.optimization_barrier(sandwich(diag_block, polar, diag_block))
     from_above = sandwich(couple_own, polar_above, couple_own.T)
-    shape = (1, 2, e_local, elements)
-    partial = (local + from_above).reshape(shape)
-    partial, from_below = lax.optimization_barrier((partial, from_below))
-    return partial + from_below.reshape(shape)
+    total = from_above + (local + from_below)
+    return total.reshape(1, 2, e_local, elements)
 
 
 def solution(mesh):

time: 49.4 us -> 49.8 us (level)
  other arithmetic: 1.59 us -> 0.66 us
  waiting for transfers between devices: 15.8 us -> 16.6 us
  local copies, waits for them, and re-layouts: 1.9 us -> 2.49 us
    add x1 -> x0, other arithmetic: 0.93 us -> none  [per_device(): return partial + from_below.reshape(shape)]
    ppermute x2, waiting for transfers between devices: 7.22 us -> 8 us  [shifted(): return lax.ppermute(x, axis, pairs)]
    reshape x2 -> x1, local copies, waits for them, and re-layouts: 0.43 us -> 1.02 us  [per_device(): return total.reshape(1, 2, e_local, elements)]
  transfers between devices with their start and end apart: 3 -> 3, of which waited for: 2 -> 3; matrix products, arithmetic and copies ran while one was open for 9% -> 8% of each run, Pallas kernels for 0% -> 0%
where the time goes in v17:
time: 49.8 us; the launch traced here: 49.5 us
  waiting for transfers between devices  16.6 us (33%)
  blocking collectives  12.2 us (24%)
  starting transfers between devices  11.1 us (22%)
  matrix products  4.38 us (9%)
  local copies, waits for them, and re-layouts  2.49 us (5%)
  Pallas kernels  1.96 us (4%)
  other arithmetic  0.66 us (1%)
    all_to_all x1, blocking collectives, per_device(): back = lax.all_to_all(send, 'energy', 0, 0, tiled=True)  12.2 us
    all_to_all x1, waiting for transfers between devices, per_device(): got = lax.all_to_all(both, 'energy', 0, 0, tiled=True)  8.63 us
    ppermute x2, waiting for transfers between devices, shifted(): return lax.ppermute(x, axis, pairs)  8 us
    ppermute x2, starting transfers between devices, shifted(): return lax.ppermute(x, axis, pairs)  5.87 us
    all_to_all x1, starting transfers between devices, per_device(): got = lax.all_to_all(both, 'energy', 0, 0, tiled=True)  5.18 us
    pallas_call x1, Pallas kernels, by_destination(): pl.pallas_call(kernel, out_shape=jax.ShapeDtypeStruct((groups, 4, e_local...  1.96 us
    dot_general x3, matrix products, sandwich(): return jnp.matmul(inner, right, precision=lax.Precision.HIGH)  1.77 us
    dot_general x3, matrix products, sandwich(): inner = jnp.matmul(left, field, precision=lax.Precision.HIGH)  1.76 us
  transfers between devices with their start and end apart: 3, of which 3 were waited for; matrix products, arithmetic and copies ran while one was open for 8% of the time, Pallas kernels for 0%

profile of v17, /device:TPU:0, one launch (start us, length us, event | category | flops | bytes accessed | tf_op | source)
XLA Modules:
  0.0 49.5 jit_solution(811598209522657229)
XLA Ops:
  0.0 0.0 copy-start
  0.0 2.0 %shard_map.46 = bf16[8,4,4,2048]{3,2,1,0:T(4,128)(2,1)} custom-call(bf16[1,2,4,16384]{3,2,1,0:T(4,128)(2,1)} %lesser_hbm.1, bf16[1,2,4,16384]{3,2,1,0:T(4,128)(2,1)} %greater_hbm.1), custom_call_target="tpu_custom_call" | custom-call | tf_op jit(solution)/shard_map/pallas_call | solution.py:80
  2.0 5.2 %all-to-all-start = ((bf16[8,4,4,2048]{3,2,1,0:T(4,128)(2,1)}), bf16[8,4,4,2048]{3,2,1,0:T(4,128)(2,1)S(1)}, u32[]{:S(2)}, u32[]{:S(2)}) async-start(bf16[8,4,4,2048]{3,2,1,0:T(4,128)(2,1)} %shard_map.46), calls=%async_computation | async-start | bytes 1048576 | tf_op jit(solution)/shard_map/all_to_all | solution.py:107
  7.2 0.2 fusion.31
  7.3 0.1 copy.8
  7.5 0.2 copy.9
  7.7 0.3 reshape.190
  7.9 0.2 fusion.34
  8.2 0.1 maximum_maximum_fusion
  8.3 8.6 %all-to-all-done = bf16[8,4,4,2048]{3,2,1,0:T(4,128)(2,1)S(1)} async-done(((bf16[8,4,4,2048]{3,2,1,0:T(4,128)(2,1)}), bf16[8,4,4,2048]{3,2,1,0:T(4,128)(2,1)S(1)}, u32[]{:S(2)}, u32[]{:S(2)}) %all-to-all-start) | async-done | bytes 524320 | tf_op jit(solution)/shard_map/all_to_all | solution.py:107
  16.9 0.1 reshape.191
  17.0 0.5 fusion
  17.5 0.1 multiply_add_fusion
  17.6 0.4 fusion.4
  18.0 12.2 %all_to_all.10 = f32[8,8,2048]{2,1,0:T(8,128)S(1)} all-to-all(f32[8,8,2048]{2,1,0:T(8,128)S(1)} %fusion.4), channel_id=1, replica_groups=mesh['energy'=8,'space'=4] {'energy'}, dimensions={0} | all-to-all | bytes 1048576 | tf_op jit(solution)/shard_map/all_to_all | solution.py:111
  30.2 0.0 copy-start.1
  30.2 0.3 copy.27
  30.5 0.1 reshape_reshape.7
  30.6 0.0 copy-done
  30.6 0.6 %convolution_bitcast_fusion = f32[2,4,128,128]{2,3,1,0:T(8,128)S(1)} fusion(f32[2,4,128,128]{3,2,1,0:T(8,128)S(1)} %reshape_reshape.7, f32[1,128,128]{2,1,0:T(8,128)S(1)} %copy-done), kind=kOutput, calls=%fused_computation | convolution fusion | flops 100663296 | bytes 1114112 | tf_op jit(solution)/shard_map/dot_general | solution.py:59
  31.2 1.3 %collective-permute-start = (f32[8,8,2048]{2,1,0:T(8,128)S(1)}, f32[8,8,2048]{2,1,0:T(8,128)S(1)}, u32[]{:S(2)}, u32[]{:S(2)}) collective-permute-start(f32[8,8,2048]{2,1,0:T(8,128)S(1)} %all_to_all.10), channel_id=1, source_target_pairs={{1,0},{2,1},{3,2},{5,4},{6,5},{7,6},{9,8},{10,9},{11,10},{13,12},{... | collective-permute-start | bytes 1572872 | tf_op jit(solution)/shard_map/ppermute | solution.py:17
  32.5 0.6 %fusion.14 = f32[2,4,128,128]{3,2,1,0:T(8,128)S(1)} fusion(f32[2,4,128,128]{2,3,1,0:T(8,128)S(1)} %convolution_bitcast_fusion, f32[1,128,128]{2,1,0:T(8,128)S(1)} %copy-done), kind=kOutput, calls=%fused_computation.27 | convolution fusion | flops 100663296 | bytes 1114112 | tf_op jit(solution)/shard_map/dot_general | solution.py:60
  33.1 4.6 %collective-permute-start.1 = (f32[2,4,128,128]{3,2,1,0:T(8,128)S(1)}, f32[2,4,128,128]{3,2,1,0:T(8,128)S(1)}, u32[]{:S(2)}, u32[]{:S(2)}) collective-permute-start(f32[2,4,128,128]{3,2,1,0:T(8,128)S(1)} %fusion.14), channel_id=1, source_target_pairs={{0,1},{1,2},{2,3},{4,5},{5,6},{6,7},{8,9},{9,10},{10,11},{12,13},{... | collective-permute-start | bytes 1572872 | tf_op jit(solution)/shard_map/ppermute | solution.py:17
  37.7 0.0 copy-done.1
  37.7 0.6 %convolution_bitcast_fusion.1 = f32[2,4,128,128]{2,3,1,0:T(8,128)S(1)} fusion(f32[2,4,128,128]{3,2,1,0:T(8,128)S(1)} %reshape_reshape.7, f32[1,128,128]{2,1,0:T(8,128)S(1)} %copy-done.1), kind=kOutput, calls=%fused_computation.1 | convolution fusion | flops 100663296 | bytes 1114112 | tf_op jit(solution)/shard_map/dot_general | solution.py:59
  38.3 0.6 %fusion.11 = f32[2,4,128,128]{3,2,1,0:T(8,128)S(1)} fusion(f32[2,4,128,128]{2,3,1,0:T(8,128)S(1)} %convolution_bitcast_fusion.1, f32[1,128,128]{2,1,0:T(8,128)S(1)} %copy-done.1), kind=kOutput, calls=%fused_computation.24 | convolution fusion | flops 100663296 | bytes 1114112 | tf_op jit(solution)/shard_map/dot_general | solution.py:60
  38.9 7.2 %collective-permute-done = f32[8,8,2048]{2,1,0:T(8,128)S(1)} collective-permute-done((f32[8,8,2048]{2,1,0:T(8,128)S(1)}, f32[8,8,2048]{2,1,0:T(8,128)S(1)}, u32[]{:S(2)}, u32[]{:S(2)}) %collective-permute-start) | collective-permute-done | bytes 524320 | tf_op jit(solution)/shard_map/ppermute | solution.py:17
  46.1 0.3 copy.26
  46.4 0.1 reshape_reshape.6
  46.5 0.6 %convolution_bitcast_fusion.2 = f32[2,4,128,128]{2,3,1,0:T(8,128)S(1)} fusion(f32[2,4,128,128]{3,2,1,0:T(8,128)S(1)} %reshape_reshape.6, f32[1,128,128]{2,1,0:T(8,128)S(1)} %copy-done), kind=kOutput, calls=%fused_computation.2 | convolution fusion | flops 100663296 | bytes 1114112 | tf_op jit(solution)/shard_map/dot_general | solution.py:59
  47.1 0.8 %collective-permute-done.1 = f32[2,4,128,128]{3,2,1,0:T(8,128)S(1)} collective-permute-done((f32[2,4,128,128]{3,2,1,0:T(8,128)S(1)}, f32[2,4,128,128]{3,2,1,0:T(8,128)S(1)}, u32[]{:S(2)}, u32[]{:S(2)}) %collective-permute-start.1) | collective-permute-done | bytes 524320 | tf_op jit(solution)/shard_map/ppermute | solution.py:17
  47.9 0.6 %add_add_fusion = f32[2,4,128,128]{3,2,1,0:T(8,128)S(1)} fusion(f32[2,4,128,128]{3,2,1,0:T(8,128)S(1)} %fusion.11, f32[2,4,128,128]{3,2,1,0:T(8,128)S(1)} %collective-permute-done.1, f32[2,4,128,128]{2,3,1,0:T(8,128)S(1)} %convolution_bitcast_fusion.2, f32[1,128,128]{2,1,0:T(8,128)S(1)} %copy-done), kind=kOutput, calls=%fused_computation.11 | convolution fusion | flops 100925440 | bytes 2162688 | tf_op jit(solution)/shard_map/dot_general | solution.py:60
  48.5 1.0 %reshape.194 = f32[1,2,4,16384]{3,2,1,0:T(4,128)} reshape(f32[2,4,128,128]{3,2,1,0:T(8,128)S(1)} %add_add_fusion) | data formatting | bytes 1048576 | tf_op jit(solution)/shard_map/reshape | solution.py:127
  (5 shorter events, 0.1 us)
Async XLA Ops:
  0.0 30.6 %copy-start = (f32[1,128,128]{2,1,0:T(8,128)S(1)}, f32[1,128,128]{2,1,0:T(8,128)}, u32[]{:S(2)}) copy-start(f32[1,128,128]{2,1,0:T(8,128)} %param.7) | copy-start | bytes 196612
  2.0 14.9 %all-to-all-start = ((bf16[8,4,4,2048]{3,2,1,0:T(4,128)(2,1)}), bf16[8,4,4,2048]{3,2,1,0:T(4,128)(2,1)S(1)}, u32[]{:S(2)}, u32[]{:S(2)}) async-start(bf16[8,4,4,2048]{3,2,1,0:T(4,128)(2,1)} %shard_map.46), calls=%async_computation | async-start | bytes 1048576 | tf_op jit(solution)/shard_map/all_to_all | solution.py:107
  30.2 7.5 %copy-start.1 = (f32[1,128,128]{2,1,0:T(8,128)S(1)}, f32[1,128,128]{2,1,0:T(8,128)}, u32[]{:S(2)}) copy-start(f32[1,128,128]{2,1,0:T(8,128)} %param.6) | copy-start | bytes 196612
  31.2 14.9 %collective-permute-start = (f32[8,8,2048]{2,1,0:T(8,128)S(1)}, f32[8,8,2048]{2,1,0:T(8,128)S(1)}, u32[]{:S(2)}, u32[]{:S(2)}) collective-permute-start(f32[8,8,2048]{2,1,0:T(8,128)S(1)} %all_to_all.10), channel_id=1, source_target_pairs={{1,0},{2,1},{3,2},{5,4},{6,5},{7,6},{9,8},{10,9},{11,10},{13,12},{... | collective-permute-start | bytes 1572872 | tf_op jit(solution)/shard_map/ppermute | solution.py:17
  33.1 14.8 %collective-permute-start.1 = (f32[2,4,128,128]{3,2,1,0:T(8,128)S(1)}, f32[2,4,128,128]{3,2,1,0:T(8,128)S(1)}, u32[]{:S(2)}, u32[]{:S(2)}) collective-permute-start(f32[2,4,128,128]{3,2,1,0:T(8,128)S(1)} %fusion.14), channel_id=1, source_target_pairs={{0,1},{1,2},{2,3},{4,5},{5,6},{6,7},{8,9},{9,10},{10,11},{12,13},{... | collective-permute-start | bytes 1572872 | tf_op jit(solution)/shard_map/ppermute | solution.py:17
